TPU v7x, 256 devices: a whole 4x4x8 slice. The times are simulated.
256 devices in a mesh: dp: 32 (over x, z), mp: 8 (over y, core).
Axes of the slice: x: 4, y: 4, z: 8, core: 2. Of those that a mesh axis runs over, the one named last changes fastest.
Arguments:
- tokens: bfloat16 [8192, 2880], P('dp'), may hold values from -14 to 14
- w_query: bfloat16 [2880, 4096], P('dp', 'mp'), may hold values from -0.0559017 to 0.0559017
- w_key: bfloat16 [2880, 512], P('dp', 'mp'), may hold values from -0.0559017 to 0.0559017
- w_value: bfloat16 [2880, 512], P('dp', 'mp'), may hold values from -0.109375 to 0.109375
- w_out: bfloat16 [4096, 2880], P(('mp', 'dp')), may hold values from -0.09375 to 0.09375
- sinks: float32 [64], P('mp'), may hold values from -2 to 2
- grad_out: bfloat16 [8192, 2880], P('dp'), may hold values from -24 to 24
Outputs:
- grad_tokens: bfloat16 [8192, 2880], P('dp', 'mp')
- grad_w_query: float32 [2880, 4096], P('dp', 'mp')
- grad_w_key: float32 [2880, 512], P('dp', 'mp')
- grad_w_value: float32 [2880, 512], P('dp', 'mp')
- grad_w_out: float32 [4096, 2880], P(('mp', 'dp'))
All inputs are finite; a program needn't handle non-finite values.
Results may differ from a plain program's by a relative error of at most 0.04.
Values may be sent and summed in bfloat16 or wider, within the bound.
No kernel may reach another device: no remote copies, remote signals or barrier semaphores. Data moves between devices by JAX's collectives and lax.ppermute only.
A program may use at most 64 MiB of HBM per device.

v0:
```python
import math

import jax
import jax.numpy as jnp
from jax import lax
from jax.sharding import PartitionSpec as P

DH = 64
WINDOW = 128
LENGTH = 16384


masked_score = -1e30


def passed_along(array, axis, by):
    peers = lax.axis_size(axis)
    pairs = [(i, i + by) for i in range(peers) if 0 <= i + by < peers]
    return lax.ppermute(array, axis, pairs)


def contract_rows(left_side, right_side):
    return lax.dot_general(
        left_side, right_side, (((0,), (0,)), ((), ())), preferred_element_type=jnp.float32
    )


def contract_cols(left_side, right_side):
    return lax.dot_general(
        left_side, right_side, (((1,), (1,)), ((), ())), preferred_element_type=jnp.float32
    )


def band_mask(first_row, blocks, window):
    block_ids = jnp.arange(blocks, dtype=jnp.int32)[:, None, None] * window
    query_pos = first_row + block_ids + jnp.arange(window, dtype=jnp.int32)[None, :, None]
    key_pos = (
        first_row + block_ids + jnp.arange(2 * window, dtype=jnp.int32)[None, None, :] - window
    )
    offset = query_pos - key_pos
    same_resp = jnp.floor_divide(query_pos, LENGTH) == jnp.floor_divide(key_pos, LENGTH)
    return (offset >= 0) & (offset < window) & same_resp


def paired_blocks(extended, window):
    stacked = extended.reshape((-1, window) + extended.shape[1:])
    return jnp.concatenate([stacked[:-1], stacked[1:]], axis=1)


def fold_blocks(paired, window):
    widths = [(0, 0)] * (paired.ndim - 1)
    lower_half = jnp.pad(paired[:, :window], [(0, 1)] + widths)
    upper_half = jnp.pad(paired[:, window:], [(1, 0)] + widths)
    summed = lower_half + upper_half
    return summed.reshape((summed.shape[0] * window,) + summed.shape[2:])


def shards(tokens, w_query, w_key, w_value, w_out, sinks, grad_out):
    row_count = tokens.shape[0]
    window = WINDOW
    blocks = row_count // window
    score_scale = 1.0 / math.sqrt(DH)
    full_query, full_key, full_value, full_out = (
        lax.all_gather(w_query, "dp", axis=0, tiled=True),
        lax.all_gather(w_key, "dp", axis=0, tiled=True),
        lax.all_gather(w_value, "dp", axis=0, tiled=True),
        lax.all_gather(w_out, "dp", axis=0, tiled=True),
    )
    kv_heads = full_key.shape[1] // DH
    group_size = full_query.shape[1] // DH // kv_heads
    queries = jnp.dot(tokens, full_query, preferred_element_type=jnp.float32).astype(jnp.bfloat16)
    key_rows = jnp.dot(tokens, full_key, preferred_element_type=jnp.float32).astype(jnp.bfloat16)
    value_rows = jnp.dot(tokens, full_value, preferred_element_type=jnp.float32).astype(
        jnp.bfloat16
    )
    rim_keys, rim_values = passed_along((key_rows[-window:], value_rows[-window:]), "dp", 1)
    grad_attn = contract_cols(grad_out, full_out).astype(jnp.bfloat16)
    first_row = lax.axis_index("dp") * row_count
    ext_keys = jnp.concatenate([rim_keys, key_rows], axis=0).reshape(
        row_count + window, kv_heads, DH
    )
    ext_values = jnp.concatenate([rim_values, value_rows], axis=0).reshape(
        row_count + window, kv_heads, DH
    )
    key_blk = paired_blocks(ext_keys, window)
    value_blk = paired_blocks(ext_values, window)
    query_blk = queries.reshape(blocks, window, kv_heads, group_size, DH)
    dattn_blk = grad_attn.reshape(blocks, window, kv_heads, group_size, DH)
    scores = (
        jnp.einsum("bikgd,bjkd->bkgij", query_blk, key_blk, preferred_element_type=jnp.float32)
        * score_scale
    )
    allowed = band_mask(first_row, blocks, window)[:, None, None]
    scores = jnp.where(allowed, scores, masked_score)
    sink_row = sinks.reshape(kv_heads, group_size)[None, :, :, None]
    row_peak = jnp.maximum(jnp.max(scores, axis=-1), sink_row)
    row_total = jnp.exp(sink_row - row_peak) + jnp.sum(
        jnp.exp(scores - row_peak[..., None]), axis=-1
    )
    log_total = row_peak + jnp.log(row_total)
    prob_full = jnp.exp(scores - log_total[..., None])
    prob_round = prob_full.astype(jnp.bfloat16)
    attended = jnp.einsum(
        "bkgij,bjkd->bikgd", prob_round, value_blk, preferred_element_type=jnp.float32
    ).astype(jnp.bfloat16)
    attn_rows = attended.reshape(row_count, -1)
    grad_out_w = contract_rows(attn_rows, grad_out)
    row_delta = jnp.sum(
        dattn_blk.astype(jnp.float32) * attended.astype(jnp.float32), axis=-1
    ).transpose(0, 2, 3, 1)
    grad_prob = jnp.einsum(
        "bikgd,bjkd->bkgij", dattn_blk, value_blk, preferred_element_type=jnp.float32
    )
    grad_scores = (prob_full * (grad_prob - row_delta[..., None]) * score_scale).astype(
        jnp.bfloat16
    )
    grad_queries = (
        jnp.einsum("bkgij,bjkd->bikgd", grad_scores, key_blk, preferred_element_type=jnp.float32)
        .astype(jnp.bfloat16)
        .reshape(row_count, -1)
    )
    grad_key_blk = jnp.einsum(
        "bkgij,bikgd->bjkd", grad_scores, query_blk, preferred_element_type=jnp.float32
    )
    grad_value_blk = jnp.einsum(
        "bkgij,bikgd->bjkd", prob_round, dattn_blk, preferred_element_type=jnp.float32
    )
    grad_key_ext = fold_blocks(grad_key_blk, window).reshape(row_count + window, -1)
    grad_value_ext = fold_blocks(grad_value_blk, window).reshape(row_count + window, -1)
    back_keys, back_values = (
        passed_along(grad_key_ext[:window].astype(jnp.bfloat16), "dp", -1).astype(jnp.float32),
        passed_along(grad_value_ext[:window].astype(jnp.bfloat16), "dp", -1).astype(jnp.float32),
    )
    own_keys = grad_key_ext[window:]
    own_values = grad_value_ext[window:]
    grad_keys = jnp.concatenate(
        [own_keys[:-window], own_keys[-window:] + back_keys], axis=0
    ).astype(jnp.bfloat16)
    grad_values = jnp.concatenate(
        [own_values[:-window], own_values[-window:] + back_values], axis=0
    ).astype(jnp.bfloat16)
    token_terms = (
        contract_cols(grad_queries, full_query)
        + contract_cols(grad_keys, full_key)
        + contract_cols(grad_values, full_value)
    )
    grad_tokens = lax.psum_scatter(
        token_terms.astype(jnp.bfloat16), "mp", scatter_dimension=1, tiled=True
    )
    grad_q_term = contract_rows(tokens, grad_queries)
    grad_k_term = contract_rows(tokens, grad_keys)
    grad_v_term = contract_rows(tokens, grad_values)
    summed_q, summed_k, summed_v, summed_out = (
        lax.psum_scatter(
            grad_q_term.astype(jnp.bfloat16), "dp", scatter_dimension=0, tiled=True
        ).astype(jnp.float32),
        lax.psum_scatter(
            grad_k_term.astype(jnp.bfloat16), "dp", scatter_dimension=0, tiled=True
        ).astype(jnp.float32),
        lax.psum_scatter(
            grad_v_term.astype(jnp.bfloat16), "dp", scatter_dimension=0, tiled=True
        ).astype(jnp.float32),
        lax.psum_scatter(
            grad_out_w.astype(jnp.bfloat16), "dp", scatter_dimension=0, tiled=True
        ).astype(jnp.float32),
    )
    grad_scale = 1.0 / math.sqrt(row_count * lax.axis_size("dp"))
    return (
        grad_tokens,
        summed_q * grad_scale,
        summed_k * grad_scale,
        summed_v * grad_scale,
        summed_out * grad_scale,
    )


def solution(mesh):
    return jax.shard_map(
        shards,
        mesh=mesh,
        in_specs=(
            P("dp", None),
            P("dp", "mp"),
            P("dp", "mp"),
            P("dp", "mp"),
            P(("mp", "dp"), None),
            P("mp"),
            P("dp", None),
        ),
        out_specs=(
            P("dp", "mp"),
            P("dp", "mp"),
            P("dp", "mp"),
            P("dp", "mp"),
            P(("mp", "dp"), None),
        ),
        check_vma=False,
    )
```

profile of v0, /device:TPU:2, one launch (start us, length us, event | category | flops | bytes accessed | tf_op | source)
XLA Modules:
  0.0 598.7 jit_solution(12106645983945934477)
XLA Ops:
  7.2 0.7 all-gather.6.cloned.1.call-update
  8.0 0.7 all-gather.8.cloned.1.call-update
  8.7 52.4 %all-gather = bf16[32,90,64]{1,2,0:T(8,128)(2,1)S(1)} all-gather(bf16[1,90,64]{1,2,0:T(8,128)(2,1)} %bitcast.165), channel_id=1, replica_groups=mesh['dp'=32,'mp'=8] {'dp'}, dimensions={0}, use_global_device_ids=true | all-gather | bytes 380160 | tf_op jit(solution)/shard_map/all_gather | solution.py:65
  61.5 0.8 reshape.295
  62.6 2.1 collective-permute-start
  64.8 50.1 %all-gather.2 = bf16[32,90,64]{1,2,0:T(8,128)(2,1)S(1)} all-gather(bf16[1,90,64]{1,2,0:T(8,128)(2,1)S(1)} %bitcast.166), channel_id=1, replica_groups=mesh['dp'=32,'mp'=8] {'dp'}, dimensions={0}, use_global_device_ids=true | all-gather | bytes 380160 | tf_op jit(solution)/shard_map/all_gather | solution.py:66
  115.2 0.8 reshape.299
  116.4 2.2 collective-permute-start.1
  118.7 0.8 fusion.21
  119.6 0.6 copy.51
  120.2 0.6 copy.56
  120.9 0.6 copy.50
  121.5 2.7 collective-permute-done.1
  124.2 0.6 copy.55
  124.8 3.3 convolution_convert_fusion.4
  128.2 1.1 reshape.313
  129.5 41.3 %all-gather.8.cloned.1.call-done = bf16[32,90,512]{2,1,0:T(8,128)(2,1)} async-done(((bf16[1,90,512]{2,1,0:T(8,128)(2,1)}), bf16[32,90,512]{2,1,0:T(8,128)(2,1)}) %all-gather.8.cloned.1.call-update) | async-done | bytes 2949136 | tf_op jit(solution)/shard_map/all_gather | solution.py:64
  170.7 4.5 reshape.297
  175.2 2.8 convolution_convert_fusion.5
  178.0 1.1 reshape.312
  179.1 1.3 copy.53
  180.4 2.0 copy.58
  182.5 1.2 copy.61
  183.6 1.4 fusion.47
  186.2 1.2 multiply_reduce_fusion
  187.3 0.7 fusion.9
  188.5 4.9 collective-permute-start.3
  193.5 3.2 collective-permute-start.2
  196.7 1.4 fusion.4
  198.1 1.0 collective-permute-done.2
  199.7 1.3 fusion.3
  201.6 4.0 convolution_convert_fusion
  205.7 0.7 copy-done.6
  207.0 2.8 fusion.18
  209.8 0.6 convolution_add_fusion.1
  210.5 1.7 fusion.2
  212.2 2.6 fusion.1
  214.8 81.7 %fusion = bf16[96,512]{1,0:T(8,128)(2,1)S(1)} fusion(bf16[2880,512]{1,0:T(8,128)(2,1)} %fusion.1), kind=kCustom, calls=%all-reduce-scatter | all-reduce-scatter fusion | flops 1572865 | bytes 3048448
  296.5 1.9 collective-permute-start.4
  298.5 1.9 collective-permute-start.5
  300.4 0.6 fusion.46
  302.3 5.8 collective-permute-done.5
  308.6 0.7 convert_multiply_fusion
  309.3 38.9 %all-reduce.11.cloned.1.call-done = (bf16[2880,64]{0,1:T(8,128)(2,1)}, bf16[2880,64]{0,1:T(8,128)(2,1)}) async-done(((bf16[2880,64]{0,1:T(8,128)(2,1)}, bf16[2880,64]{0,1:T(8,128)(2,1)}), (bf16[2880,64]{0,1:T(8,128)(2,1)}, bf16[2880,64]{0,1:T(8,128)(2,1)})) %all-reduce.11.cloned.1.call-update) | async-done | bytes 737296
  348.2 1.5 convert_multiply_fusion.2
  349.7 204.7 %reduce-scatter.9.cloned.1.call-done = bf16[16,2880]{1,0:T(8,128)(2,1)} async-done(((bf16[512,2880]{1,0:T(8,128)(2,1)}), bf16[16,2880]{1,0:T(8,128)(2,1)}) %reduce-scatter.9.cloned.1.call-update) | async-done | bytes 92176 | tf_op jit(solution)/shard_map/reduce_scatter | solution.py:163
  554.4 1.6 convert_multiply_fusion.1
  556.0 36.2 %reduce-scatter.7.cloned.1.call-done = bf16[256,360]{0,1:T(8,128)(2,1)} async-done(((bf16[256,2880]{0,1:T(8,128)(2,1)}), bf16[256,360]{0,1:T(8,128)(2,1)}) %reduce-scatter.7.cloned.1.call-update) | async-done | bytes 184336 | tf_op jit(solution)/shard_map/reduce_scatter | solution.py:147
  (79 shorter events, 6.1 us)
Async XLA Ops:
  7.2 55.1 %copy-start = (bf16[256,2880]{0,1:T(8,128)(2,1)S(1)}, bf16[256,2880]{0,1:T(8,128)(2,1)}, u32[]{:S(2)}) copy-start(bf16[256,2880]{0,1:T(8,128)(2,1)} %param.7) | copy-start | bytes 4423684
  7.2 117.6 %all-gather.6.cloned.1.call-start = ((), (), s32[]{:S(2)}) async-start(), calls=%async_computation.2 | async-start | bytes 3108864 | tf_op jit(solution)/shard_map/all_gather | solution.py:67
  7.9 162.8 %all-gather.8.cloned.1.call-start = ((), (), s32[]{:S(2)}) async-start(), calls=%async_computation.5 | async-start | bytes 3244032 | tf_op jit(solution)/shard_map/all_gather | solution.py:64
  8.7 339.6 %all-reduce.11.cloned.1.call-start = ((), (), s32[]{:S(2)}) async-start(), calls=%async_computation.6 | async-start | bytes 1507328
  8.7 56.1 %copy-start.14 = (bf16[90,64]{0,1:T(8,128)(2,1)S(1)}, bf16[90,64]{0,1:T(8,128)(2,1)}, u32[]{:S(2)}) copy-start(bf16[90,64]{0,1:T(8,128)(2,1)} %param.10) | copy-start | bytes 34564
  62.6 58.2 %collective-permute-start = (bf16[128,64]{0,1:T(8,128)(2,1)S(1)}, bf16[128,64]{0,1:T(8,128)(2,1)S(1)}, u32[]{:S(2)}, u32[]{:S(2)}) collective-permute-start(bf16[128,64]{0,1:T(8,128)(2,1)S(1)} %slice.104), channel_id=1, source_target_pairs={{0,8},{8,16},{16,24},{24,32},{32,40},{40,48},{48,56},{56,64},{64,7... | collective-permute-start | bytes 49160 | tf_op jit(solution)/shard_map/ppermute | solution.py:19
  116.4 7.8 %collective-permute-start.1 = (bf16[128,64]{0,1:T(8,128)(2,1)S(1)}, bf16[128,64]{0,1:T(8,128)(2,1)S(1)}, u32[]{:S(2)}, u32[]{:S(2)}) collective-permute-start(bf16[128,64]{0,1:T(8,128)(2,1)S(1)} %slice.105), channel_id=1, source_target_pairs={{0,8},{8,16},{16,24},{24,32},{32,40},{40,48},{48,56},{56,64},{64,7... | collective-permute-start | bytes 49160 | tf_op jit(solution)/shard_map/ppermute | solution.py:19
  182.5 2.6 copy-start.15
  183.6 1.9 copy-start.1
  185.1 1.0 copy-start.2
  185.1 1.0 copy-start.4
  185.1 1.0 copy-start.5
  188.5 9.6 %copy-start.10 = (bf16[128,64]{0,1:T(8,128)(2,1)}, bf16[128,64]{0,1:T(8,128)(2,1)S(1)}, u32[]{:S(2)}) copy-start(bf16[128,64]{0,1:T(8,128)(2,1)S(1)} %get-tuple-element.11) | copy-start | bytes 49156
  188.5 8.2 %collective-permute-start.3 = (bf16[128,64]{0,1:T(8,128)(2,1)S(1)}, bf16[128,64]{0,1:T(8,128)(2,1)S(1)}, u32[]{:S(2)}, u32[]{:S(2)}) collective-permute-start(bf16[128,64]{0,1:T(8,128)(2,1)S(1)} %get-tuple-element.12), channel_id=1, source_target_pairs={{8,0},{16,8},{24,16},{32,24},{40,32},{48,40},{56,48},{64,56},{72,6... | collective-permute-start | bytes 49160 | tf_op jit(solution)/shard_map/ppermute | solution.py:19
  193.5 5.7 copy-start.12
  193.5 5.6 collective-permute-start.2
  196.7 4.6 copy-start.3
  199.1 0.6 copy-start.8
  201.1 353.4 %reduce-scatter.9.cloned.1.call-start = ((), (), s32[]{:S(2)}) async-start(), calls=%async_computation.4 | async-start | bytes 3108864 | tf_op jit(solution)/shard_map/reduce_scatter | solution.py:163
  205.6 0.8 copy-start.6
  205.6 0.8 copy-start.7
  205.6 386.5 %reduce-scatter.7.cloned.1.call-start = ((), (), s32[]{:S(2)}) async-start(), calls=%async_computation.3 | async-start | bytes 1658880 | tf_op jit(solution)/shard_map/reduce_scatter | solution.py:147
  207.0 2.8 copy-start.9
  207.0 2.8 copy-start.13
  209.8 0.7 copy-start.11
  214.8 85.6 %copy-start.16 = (u32[256]{0:T(256)S(1)}, u32[256]{0:T(256)}, u32[]{:S(2)}) copy-start(u32[256]{0:T(256)} %constant.68) | copy-start | bytes 3076
  296.5 11.6 %collective-permute-start.4 = (bf16[96,512]{1,0:T(8,128)(2,1)S(1)}, bf16[96,512]{1,0:T(8,128)(2,1)S(1)}, u32[]{:S(2)}, u32[]{:S(2)}) collective-permute-start(bf16[96,512]{1,0:T(8,128)(2,1)S(1)} %fusion), channel_id=1, source_target_pairs={{0,8},{8,16},{16,24},{24,32},{32,40},{40,48},{48,56},{56,64},{64,7... | collective-permute-start | bytes 294920
  298.5 9.6 %collective-permute-start.5 = (bf16[90,512]{1,0:T(8,128)(2,1)S(1)}, bf16[90,512]{1,0:T(8,128)(2,1)S(1)}, u32[]{:S(2)}, u32[]{:S(2)}) collective-permute-start(bf16[90,512]{1,0:T(8,128)(2,1)S(1)} %slice.118), channel_id=1, source_target_pairs={{0,16},{8,24},{16,32},{24,40},{32,48},{40,56},{48,64},{56,72},{64,... | collective-permute-start | bytes 276488
Sparse Core Ops, SparseCore 0:
  10.6 80.9 all-gather.5
  94.2 76.4 all-gather.7
  201.2 146.9 all-reduce.10
  351.9 202.4 reduce-scatter.8
  557.4 34.7 reduce-scatter.6
where the time goes:
time: 600 us; the launch traced here: 599 us
  waiting for transfers between devices  332 us (55%)
  blocking collectives  184 us (31%)
  matrix products  25.7 us (4%)
  local copies, waits for them, and re-layouts  19.5 us (3%)
  starting transfers between devices  16.6 us (3%)
  between operations  15.5 us (3%)
    reduce_scatter x1, waiting for transfers between devices, shards(): lax.psum_scatter(grad_out_w.astype(jnp.bfloat16), 'dp', scatter_dimension...  205 us
    unnamed x1, blocking collectives  81.7 us
    all_gather x1, blocking collectives, shards(): lax.all_gather(w_key, 'dp', axis=0, tiled=True)  52.4 us
    all_gather x1, blocking collectives, shards(): lax.all_gather(w_value, 'dp', axis=0, tiled=True)  50.1 us
    unnamed x8, waiting for transfers between devices  46.1 us
    all_gather x1, waiting for transfers between devices, shards(): lax.all_gather(w_query, 'dp', axis=0, tiled=True)  41.3 us
    reduce_scatter x1, waiting for transfers between devices, shards(): lax.psum_scatter(token_terms.astype(jnp.bfloat16), 'mp', scatter_dimensio...  36.2 us
    ppermute x4, starting transfers between devices, passed_along(): return lax.ppermute(array, axis, pairs)  12.4 us
  transfers between devices with their start and end apart: 11, of which 7 were waited for; matrix products, arithmetic and copies ran while one was open for 19% of the time, Pallas kernels for 0%

commit v1 on v0

--- a/solution.py
+++ b/solution.py
@@ -3,7 +3,7 @@
 import jax
 import jax.numpy as jnp
 from jax import lax
-from jax.sharding import PartitionSpec as P
+from jax.sharding import Mesh, PartitionSpec as P
 
 DH = 64
 WINDOW = 128
@@ -11,6 +11,8 @@
 
 
 masked_score = -1e30
+DP_AXES = ("dx", "dz")
+LANES = 128
 
 
 def passed_along(array, axis, by):
@@ -55,17 +57,65 @@
     return summed.reshape((summed.shape[0] * window,) + summed.shape[2:])
 
 
+def gather_weights(w_query, w_key, w_value, w_out):
+    pieces = (w_query, w_key, w_value, w_out)
+    flat = jnp.concatenate([p.reshape(-1) for p in pieces])
+    gathered = lax.all_gather(flat.reshape(1, -1, LANES), DP_AXES, axis=0, tiled=True)
+    peers = gathered.shape[0]
+    gathered = gathered.reshape(peers, -1)
+    full = []
+    at = 0
+    for p in pieces:
+        size = p.size
+        part = gathered[:, at : at + size].reshape((peers * p.shape[0],) + p.shape[1:])
+        full.append(part)
+        at += size
+    return full
+
+
+def scatter_weight_grads(partials, x_peers, z_peers):
+    rows = []
+    for p in partials:
+        blocked = p.astype(jnp.bfloat16).reshape(x_peers, z_peers, -1)
+        rows.append(jnp.swapaxes(blocked, 0, 1))
+    packed = jnp.concatenate(rows, axis=-1)
+    packed = packed.reshape(z_peers, x_peers, -1, LANES)
+    over_z = lax.psum_scatter(packed, "dz", scatter_dimension=0, tiled=True)[0]
+    over_x = lax.psum_scatter(over_z, "dx", scatter_dimension=0, tiled=True)[0]
+    over_x = over_x.reshape(-1)
+    out = []
+    at = 0
+    for p in partials:
+        size = p.size // (x_peers * z_peers)
+        shape = (p.shape[0] // (x_peers * z_peers),) + p.shape[1:]
+        out.append(over_x[at : at + size].astype(jnp.float32).reshape(shape))
+        at += size
+    return out
+
+
+def scatter_cols_mp(terms):
+    peers = lax.axis_size("mp")
+    me = lax.axis_index("mp")
+    width = terms.shape[1] // peers
+    blocks = terms.reshape(terms.shape[0], peers, width)
+    total = lax.dynamic_index_in_dim(blocks, me, axis=1, keepdims=False)
+    for shift in range(1, peers):
+        dest = (me + shift) % peers
+        piece = lax.dynamic_index_in_dim(blocks, dest, axis=1, keepdims=False)
+        pairs = [(i, (i + shift) % peers) for i in range(peers)]
+        got = lax.ppermute(piece.astype(jnp.bfloat16), "mp", pairs)
+        total = total + got.astype(jnp.float32)
+    return total.astype(jnp.bfloat16)
+
+
 def shards(tokens, w_query, w_key, w_value, w_out, sinks, grad_out):
     row_count = tokens.shape[0]
     window = WINDOW
     blocks = row_count // window
     score_scale = 1.0 / math.sqrt(DH)
-    full_query, full_key, full_value, full_out = (
-        lax.all_gather(w_query, "dp", axis=0, tiled=True),
-        lax.all_gather(w_key, "dp", axis=0, tiled=True),
-        lax.all_gather(w_value, "dp", axis=0, tiled=True),
-        lax.all_gather(w_out, "dp", axis=0, tiled=True),
-    )
+    x_peers = lax.axis_size("dx")
+    z_peers = lax.axis_size("dz")
+    full_query, full_key, full_value, full_out = gather_weights(w_query, w_key, w_value, w_out)
     kv_heads = full_key.shape[1] // DH
     group_size = full_query.shape[1] // DH // kv_heads
     queries = jnp.dot(tokens, full_query, preferred_element_type=jnp.float32).astype(jnp.bfloat16)
@@ -73,9 +123,9 @@
     value_rows = jnp.dot(tokens, full_value, preferred_element_type=jnp.float32).astype(
         jnp.bfloat16
     )
-    rim_keys, rim_values = passed_along((key_rows[-window:], value_rows[-window:]), "dp", 1)
+    rim_keys, rim_values = passed_along((key_rows[-window:], value_rows[-window:]), DP_AXES, 1)
     grad_attn = contract_cols(grad_out, full_out).astype(jnp.bfloat16)
-    first_row = lax.axis_index("dp") * row_count
+    first_row = (lax.axis_index("dx") * z_peers + lax.axis_index("dz")) * row_count
     ext_keys = jnp.concatenate([rim_keys, key_rows], axis=0).reshape(
         row_count + window, kv_heads, DH
     )
@@ -128,8 +178,8 @@
     grad_key_ext = fold_blocks(grad_key_blk, window).reshape(row_count + window, -1)
     grad_value_ext = fold_blocks(grad_value_blk, window).reshape(row_count + window, -1)
     back_keys, back_values = (
-        passed_along(grad_key_ext[:window].astype(jnp.bfloat16), "dp", -1).astype(jnp.float32),
-        passed_along(grad_value_ext[:window].astype(jnp.bfloat16), "dp", -1).astype(jnp.float32),
+        passed_along(grad_key_ext[:window].astype(jnp.bfloat16), DP_AXES, -1).astype(jnp.float32),
+        passed_along(grad_value_ext[:window].astype(jnp.bfloat16), DP_AXES, -1).astype(jnp.float32),
     )
     own_keys = grad_key_ext[window:]
     own_values = grad_value_ext[window:]
@@ -144,27 +194,14 @@
         + contract_cols(grad_keys, full_key)
         + contract_cols(grad_values, full_value)
     )
-    grad_tokens = lax.psum_scatter(
-        token_terms.astype(jnp.bfloat16), "mp", scatter_dimension=1, tiled=True
-    )
+    grad_tokens = scatter_cols_mp(token_terms)
     grad_q_term = contract_rows(tokens, grad_queries)
     grad_k_term = contract_rows(tokens, grad_keys)
     grad_v_term = contract_rows(tokens, grad_values)
-    summed_q, summed_k, summed_v, summed_out = (
-        lax.psum_scatter(
-            grad_q_term.astype(jnp.bfloat16), "dp", scatter_dimension=0, tiled=True
-        ).astype(jnp.float32),
-        lax.psum_scatter(
-            grad_k_term.astype(jnp.bfloat16), "dp", scatter_dimension=0, tiled=True
-        ).astype(jnp.float32),
-        lax.psum_scatter(
-            grad_v_term.astype(jnp.bfloat16), "dp", scatter_dimension=0, tiled=True
-        ).astype(jnp.float32),
-        lax.psum_scatter(
-            grad_out_w.astype(jnp.bfloat16), "dp", scatter_dimension=0, tiled=True
-        ).astype(jnp.float32),
-    )
-    grad_scale = 1.0 / math.sqrt(row_count * lax.axis_size("dp"))
+    summed_q, summed_k, summed_v, summed_out = scatter_weight_grads(
+        (grad_q_term, grad_k_term, grad_v_term, grad_out_w), x_peers, z_peers
+    )
+    grad_scale = 1.0 / math.sqrt(row_count * x_peers * z_peers)
     return (
         grad_tokens,
         summed_q * grad_scale,
@@ -174,25 +211,39 @@
     )
 
 
+def split_mesh(mesh):
+    dp = mesh.shape["dp"]
+    try:
+        x_peers = len({d.coords[0] for d in mesh.devices.flat})
+    except AttributeError:
+        x_peers = 4
+    if dp % x_peers:
+        x_peers = 1
+    devices = mesh.devices.reshape(x_peers, dp // x_peers, mesh.shape["mp"])
+    return Mesh(devices, ("dx", "dz", "mp"))
+
+
 def solution(mesh):
+    mesh = split_mesh(mesh)
+    dp = DP_AXES
     return jax.shard_map(
         shards,
         mesh=mesh,
         in_specs=(
-            P("dp", None),
-            P("dp", "mp"),
-            P("dp", "mp"),
-            P("dp", "mp"),
-            P(("mp", "dp"), None),
+            P(dp, None),
+            P(dp, "mp"),
+            P(dp, "mp"),
+            P(dp, "mp"),
+            P(("mp",) + dp, None),
             P("mp"),
-            P("dp", None),
+            P(dp, None),
         ),
         out_specs=(
-            P("dp", "mp"),
-            P("dp", "mp"),
-            P("dp", "mp"),
-            P("dp", "mp"),
-            P(("mp", "dp"), None),
+            P(dp, "mp"),
+            P(dp, "mp"),
+            P(dp, "mp"),
+            P(dp, "mp"),
+            P(("mp",) + dp, None),
         ),
         check_vma=False,
     )

time: 600 us -> 324 us (0.54)
  blocking collectives: 184 us -> 0 us
  waiting for transfers between devices: 332 us -> 182 us
  local copies, waits for them, and re-layouts: 19.5 us -> 70.5 us
  other arithmetic: 5.28 us -> 12.3 us
    reduce_scatter x2, waiting for transfers between devices: 241 us -> 76.3 us  [the longest x1 76.3 us: scatter_weight_grads(): over_z = lax.psum_scatter(packed, 'dz', scatter_dimension=0, tiled=True)[0]]
    all_gather x2 -> x0, blocking collectives: 102 us -> none  [the longest x1 52.4 us: shards(): lax.all_gather(w_key, 'dp', axis=0, tiled=True)]
    unnamed x1 -> x0, blocking collectives: 81.7 us -> none
    all_gather x2 -> x1, waiting for transfers between devices: 41.3 us -> 90.7 us  [gather_weights(): lax.all_gather(flat.reshape(1, -1, LANES), DP_AXES, axis=0, tiled=True)]
    unnamed x8 -> x3, waiting for transfers between devices: 46.1 us -> 0.05 us
    reshape x0 -> x13, local copies, waits for them, and re-layouts: none -> 37.8 us  [the longest x4 16.5 us: scatter_weight_grads(): blocked = p.astype(jnp.bfloat16).reshape(x_peers, z_peers, -1)]
    ppermute x0 -> x7, waiting for transfers between devices: none -> 15.2 us  [scatter_cols_mp(): got = lax.ppermute(piece.astype(jnp.bfloat16), 'mp', pairs)]
    convert_element_type x0 -> x4, local copies, waits for them, and re-layouts: none -> 9.02 us  [the longest x3 8.85 us: scatter_weight_grads(): blocked = p.astype(jnp.bfloat16).reshape(x_peers, z_peers, -1)]
  transfers between devices with their start and end apart: 11 -> 14, of which waited for: 7 -> 5; matrix products, arithmetic and copies ran while one was open for 19% -> 16% of each run, Pallas kernels for 0% -> 0%
where the time goes in v1:
time: 324 us; the launch traced here: 322 us
  waiting for transfers between devices  182 us (56%)
  local copies, waits for them, and re-layouts  70.5 us (22%)
  matrix products  22.4 us (7%)
  starting transfers between devices  20.6 us (6%)
  between operations  14.2 us (4%)
  other arithmetic  12.3 us (4%)
    all_gather x1, waiting for transfers between devices, gather_weights(): lax.all_gather(flat.reshape(1, -1, LANES), DP_AXES, axis=0, tiled=True)  90.7 us
    reduce_scatter x1, waiting for transfers between devices, scatter_weight_grads(): over_z = lax.psum_scatter(packed, 'dz', scatter_dimension=0, tiled=True)[0]  76.3 us
    reshape x4, local copies, waits for them, and re-layouts, scatter_weight_grads(): blocked = p.astype(jnp.bfloat16).reshape(x_peers, z_peers, -1)  16.5 us
    reshape x4, local copies, waits for them, and re-layouts, gather_weights(): gathered[:, at:at + size].reshape((peers * p.shape[0],) + p.shape[1:])  15.3 us
    ppermute x7, waiting for transfers between devices, scatter_cols_mp(): got = lax.ppermute(piece.astype(jnp.bfloat16), 'mp', pairs)  15.2 us
    ppermute x4, starting transfers between devices, passed_along(): return lax.ppermute(array, axis, pairs)  14 us
    unnamed x21, local copies, waits for them, and re-layouts  9.37 us
    convert_element_type x3, local copies, waits for them, and re-layouts, scatter_weight_grads(): blocked = p.astype(jnp.bfloat16).reshape(x_peers, z_peers, -1)  8.85 us
  transfers between devices with their start and end apart: 14, of which 5 were waited for; matrix products, arithmetic and copies ran while one was open for 16% of the time, Pallas kernels for 0%

profile of v1, /device:TPU:2, one launch (start us, length us, event | category | flops | bytes accessed | tf_op | source)
XLA Modules:
  0.0 322.3 jit_solution(4166617276591634845)
XLA Ops:
  7.2 0.9 copy.53
  8.2 0.8 copy.54
  9.2 1.0 reshape.364
  10.1 1.0 reshape.367
  12.2 0.8 fusion.31
  13.0 90.7 %all-gather.2.cloned.1.call-done = bf16[32,810,128]{2,1,0:T(8,128)(2,1)} async-done(((bf16[1,810,128]{2,1,0:T(8,128)(2,1)}), bf16[32,810,128]{2,1,0:T(8,128)(2,1)}) %all-gather.2.cloned.1.call-update) | async-done | bytes 6635536 | tf_op jit(solution)/shard_map/all_gather | solution.py:63
  103.7 4.6 %copy.115 = bf16[4,8,810,128]{3,1,2,0:T(8,128)(2,1)S(1)} copy(bf16[4,8,810,128]{3,2,1,0:T(8,128)(2,1)} %bitcast.206) | data formatting | bytes 13271040
  108.3 0.9 fusion.65
  109.3 3.0 fusion.66
  112.3 5.5 %reshape.376 = bf16[512,2880]{1,0:T(8,128)(2,1)} reshape(bf16[32,46080]{1,0:T(8,128)(2,1)} %get-tuple-element.17) | data formatting | bytes 5898240 | tf_op jit(solution)/shard_map/reshape | solution.py:70
  117.8 2.8 fusion.11
  120.7 1.1 reshape.388
  121.8 1.5 reshape.374
  124.3 3.1 collective-permute-start.1
  128.0 1.5 reshape.370
  130.5 2.6 collective-permute-start
  133.1 6.8 %reshape.372 = bf16[2880,512]{1,0:T(8,128)(2,1)} reshape(bf16[32,46080]{1,0:T(8,128)(2,1)} %get-tuple-element.18) | data formatting | bytes 5898240 | tf_op jit(solution)/shard_map/reshape | solution.py:70
  139.9 3.6 %fusion.10 = bf16[256,512]{0,1:T(8,128)(2,1)} fusion(bf16[2880,512]{1,0:T(8,128)(2,1)} %reshape.372, bf16[256,2880]{0,1:T(8,128)(2,1)S(1)} %copy-done), kind=kOutput, calls=%fused_computation.26 | convolution fusion | flops 755105792 | bytes 4685824 | tf_op jit(solution)/shard_map/dot_general | solution.py:121
  144.1 1.0 reshape.373
  145.7 1.4 slice.119
  147.9 1.3 pad_maximum_fusion.1
  150.0 1.3 fusion.69
  155.9 5.4 %collective-permute-start.3 = (bf16[128,64]{0,1:T(8,128)(2,1)}, bf16[128,64]{0,1:T(8,128)(2,1)S(1)}, u32[]{:S(2)}, u32[]{:S(2)}) collective-permute-start(bf16[128,64]{0,1:T(8,128)(2,1)} %get-tuple-element.35), channel_id=1, source_target_pairs={{8,0},{16,8},{24,16},{32,24},{40,32},{48,40},{56,48},{64,56},{72,6... | collective-permute-start | bytes 49160 | tf_op jit(solution)/shard_map/ppermute | solution.py:21
  161.3 2.9 collective-permute-start.2
  164.5 2.6 convolution_convert_fusion
  167.1 2.6 fusion
  169.7 4.6 %copy.74 = bf16[512,2880]{1,0:T(8,128)(2,1)} copy(bf16[512,2880]{0,1:T(8,128)(2,1)} %convolution_convert_fusion) | data formatting | bytes 5898240 | tf_op jit(solution)/shard_map/convert_element_type | solution.py:79
  174.2 5.7 %reshape.386 = bf16[4,8,46080]{2,1,0:T(8,128)(2,1)} reshape(bf16[512,2880]{1,0:T(8,128)(2,1)} %copy.74) | data formatting | bytes 5898240 | tf_op jit(solution)/shard_map/reshape | solution.py:79
  180.0 6.0 %reshape.382 = bf16[4,8,46080]{2,1,0:T(8,128)(2,1)} reshape(bf16[2880,512]{1,0:T(8,128)(2,1)} %fusion) | data formatting | bytes 5898240 | tf_op jit(solution)/shard_map/reshape | solution.py:79
  186.0 1.3 fusion.1
  187.3 2.1 copy.71
  189.5 2.4 reshape.383
  191.8 1.3 fusion.2
  193.2 2.1 copy.72
  195.3 2.4 reshape.384
  197.7 3.6 %maximum_bitcast_fusion = bf16[8,4,810,128]{3,0,2,1:T(8,128)(2,1)S(1)} fusion(bf16[8,4,46080]{2,0,1:T(8,128)(2,1)} %bitcast.202, bf16[8,4,5760]{2,0,1:T(8,128)(2,1)} %bitcast.210, bf16[8,4,5760]{2,0,1:T(8,128)(2,1)} %bitcast.209, bf16[8,4,46080]{2,0,1:T(8,128)(2,1)} %bitcast.203), kind=kLoop, calls=%fused_computation.1 | loop fusion | flops 26542080 | bytes 13271040 | tf_op jit(solution)/shard_map/reshape | solution.py:82
  201.3 3.9 %copy.75 = bf16[8,4,810,128]{3,2,1,0:T(8,128)(2,1)} copy(bf16[8,4,810,128]{3,0,2,1:T(8,128)(2,1)S(1)} %maximum_bitcast_fusion) | data formatting | bytes 13271040 | tf_op jit(solution)/shard_map/reshape | solution.py:82
  205.4 76.3 %reduce-scatter.3.cloned.1.call-done = bf16[1,4,810,128]{3,2,1,0:T(8,128)(2,1)} async-done(((bf16[8,4,810,128]{3,2,1,0:T(8,128)(2,1)}), bf16[1,4,810,128]{3,2,1,0:T(8,128)(2,1)}) %reduce-scatter.3.cloned.1.call-update) | async-done | bytes 829456 | tf_op jit(solution)/shard_map/reduce_scatter | solution.py:83
  281.7 2.8 fusion.28
  285.5 1.6 copy-done.1
  287.3 2.9 collective-permute-start.10
  290.2 1.5 collective-permute-start.9
  291.8 1.7 collective-permute-start.7
  293.5 1.7 collective-permute-done.10
  295.6 11.0 %collective-permute-done.9 = bf16[256,360]{0,1:T(8,128)(2,1)S(1)} collective-permute-done((bf16[256,360]{0,1:T(8,128)(2,1)S(1)}, bf16[256,360]{0,1:T(8,128)(2,1)S(1)}, u32[]{:S(2)}, u32[]{:S(2)}) %collective-permute-start.9) | collective-permute-done | bytes 184352 | tf_op jit(solution)/shard_map/ppermute | solution.py:106
  306.6 2.4 collective-permute-done.5
  309.0 2.0 fusion.22
  313.3 1.0 convert_multiply_fusion
  (81 shorter events, 16.9 us)
Async XLA Ops:
  7.2 116.1 %copy-start = (bf16[256,2880]{0,1:T(8,128)(2,1)S(1)}, bf16[256,2880]{0,1:T(8,128)(2,1)}, u32[]{:S(2)}) copy-start(bf16[256,2880]{0,1:T(8,128)(2,1)} %param.7) | copy-start | bytes 4423684
  7.2 96.6 %all-gather.2.cloned.1.call-start = ((), (), s32[]{:S(2)}) async-start(), calls=%async_computation.2 | async-start | bytes 6893568 | tf_op jit(solution)/shard_map/all_gather | solution.py:63
  12.0 269.7 %reduce-scatter.3.cloned.1.call-start = ((), (), s32[]{:S(2)}) async-start(), calls=%async_computation.3 | async-start | bytes 7520256 | tf_op jit(solution)/shard_map/reduce_scatter | solution.py:83
  112.3 5.5 %copy-start.3 = (bf16[256,2880]{0,1:T(8,128)(2,1)S(1)}, bf16[256,2880]{0,1:T(8,128)(2,1)}, u32[]{:S(2)}) copy-start(bf16[256,2880]{0,1:T(8,128)(2,1)} %param.13) | copy-start | bytes 4423684
  124.3 20.8 %collective-permute-start.1 = (bf16[128,64]{0,1:T(8,128)(2,1)}, bf16[128,64]{0,1:T(8,128)(2,1)S(1)}, u32[]{:S(2)}, u32[]{:S(2)}) collective-permute-start(bf16[128,64]{0,1:T(8,128)(2,1)} %slice.144), channel_id=1, source_target_pairs={{0,8},{8,16},{16,24},{24,32},{32,40},{40,48},{48,56},{56,64},{64,7... | collective-permute-start | bytes 49160 | tf_op jit(solution)/shard_map/ppermute | solution.py:21
  130.5 17.4 %collective-permute-start = (bf16[128,64]{0,1:T(8,128)(2,1)}, bf16[128,64]{0,1:T(8,128)(2,1)}, u32[]{:S(2)}, u32[]{:S(2)}) collective-permute-start(bf16[128,64]{0,1:T(8,128)(2,1)} %slice.142), channel_id=1, source_target_pairs={{0,8},{8,16},{16,24},{24,32},{32,40},{40,48},{48,56},{56,64},{64,7... | collective-permute-start | bytes 49160 | tf_op jit(solution)/shard_map/ppermute | solution.py:21
  145.7 6.8 %copy-start.7 = (f32[8]{0:T(128)S(1)}, f32[8]{0:T(128)}, u32[]{:S(2)}) copy-start(f32[8]{0:T(128)} %param.12) | copy-start | bytes 100
  151.4 1.6 copy-start.2
  151.4 1.6 copy-start.5
  153.5 1.1 copy-start.6
  154.2 10.3 %copy-start.4 = (bf16[256,2880]{0,1:T(8,128)(2,1)S(1)}, bf16[256,2880]{0,1:T(8,128)(2,1)}, u32[]{:S(2)}) copy-start(bf16[256,2880]{0,1:T(8,128)(2,1)} %param.13) | copy-start | bytes 4423684
  155.9 35.9 %collective-permute-start.3 = (bf16[128,64]{0,1:T(8,128)(2,1)}, bf16[128,64]{0,1:T(8,128)(2,1)S(1)}, u32[]{:S(2)}, u32[]{:S(2)}) collective-permute-start(bf16[128,64]{0,1:T(8,128)(2,1)} %get-tuple-element.35), channel_id=1, source_target_pairs={{8,0},{16,8},{24,16},{32,24},{40,32},{48,40},{56,48},{64,56},{72,6... | collective-permute-start | bytes 49160 | tf_op jit(solution)/shard_map/ppermute | solution.py:21
  161.3 24.7 %collective-permute-start.2 = (bf16[128,64]{0,1:T(8,128)(2,1)S(1)}, bf16[128,64]{0,1:T(8,128)(2,1)S(1)}, u32[]{:S(2)}, u32[]{:S(2)}) collective-permute-start(bf16[128,64]{0,1:T(8,128)(2,1)S(1)} %get-tuple-element.37), channel_id=1, source_target_pairs={{8,0},{16,8},{24,16},{32,24},{40,32},{48,40},{56,48},{64,56},{72,6... | collective-permute-start | bytes 49160 | tf_op jit(solution)/shard_map/ppermute | solution.py:21
  205.2 105.7 %reduce-scatter.5.cloned.1.call-start = ((), (), s32[]{:S(2)}) async-start(), calls=%async_computation.4 | async-start | bytes 1044480 | tf_op jit(solution)/shard_map/reduce_scatter | solution.py:84
  285.5 1.6 copy-start.1
  287.3 6.2 %collective-permute-start.4 = (bf16[256,360]{0,1:T(8,128)(2,1)S(1)}, bf16[256,360]{0,1:T(8,128)(2,1)S(1)}, u32[]{:S(2)}, u32[]{:S(2)}) collective-permute-start(bf16[256,360]{0,1:T(8,128)(2,1)S(1)} %get-tuple-element.19), channel_id=1, source_target_pairs={{0,1},{1,2},{2,3},{3,4},{4,5},{5,6},{6,7},{7,0},{8,9},{9,10},{10,1... | collective-permute-start | bytes 552968 | tf_op jit(solution)/shard_map/ppermute | solution.py:106
  287.3 8.0 %collective-permute-start.10 = (bf16[256,360]{0,1:T(8,128)(2,1)S(1)}, bf16[256,360]{0,1:T(8,128)(2,1)S(1)}, u32[]{:S(2)}, u32[]{:S(2)}) collective-permute-start(bf16[256,360]{0,1:T(8,128)(2,1)S(1)} %get-tuple-element.20), channel_id=1, source_target_pairs={{0,7},{1,0},{2,1},{3,2},{4,3},{5,4},{6,5},{7,6},{8,15},{9,8},{10,9... | collective-permute-start | bytes 552968 | tf_op jit(solution)/shard_map/ppermute | solution.py:106
  290.2 16.3 %collective-permute-start.9 = (bf16[256,360]{0,1:T(8,128)(2,1)S(1)}, bf16[256,360]{0,1:T(8,128)(2,1)S(1)}, u32[]{:S(2)}, u32[]{:S(2)}) collective-permute-start(bf16[256,360]{0,1:T(8,128)(2,1)S(1)} %get-tuple-element.21), channel_id=1, source_target_pairs={{0,6},{1,7},{2,0},{3,1},{4,2},{5,3},{6,4},{7,5},{8,14},{9,15},{10,... | collective-permute-start | bytes 552968 | tf_op jit(solution)/shard_map/ppermute | solution.py:106
  291.8 14.8 %collective-permute-start.8 = (bf16[256,360]{0,1:T(8,128)(2,1)S(1)}, bf16[256,360]{0,1:T(8,128)(2,1)S(1)}, u32[]{:S(2)}, u32[]{:S(2)}) collective-permute-start(bf16[256,360]{0,1:T(8,128)(2,1)S(1)} %get-tuple-element.22), channel_id=1, source_target_pairs={{0,5},{1,6},{2,7},{3,0},{4,1},{5,2},{6,3},{7,4},{8,13},{9,14},{10,... | collective-permute-start | bytes 552968 | tf_op jit(solution)/shard_map/ppermute | solution.py:106
  291.8 14.8 %collective-permute-start.7 = (bf16[256,360]{0,1:T(8,128)(2,1)S(1)}, bf16[256,360]{0,1:T(8,128)(2,1)S(1)}, u32[]{:S(2)}, u32[]{:S(2)}) collective-permute-start(bf16[256,360]{0,1:T(8,128)(2,1)S(1)} %get-tuple-element.23), channel_id=1, source_target_pairs={{0,4},{1,5},{2,6},{3,7},{4,0},{5,1},{6,2},{7,3},{8,12},{9,13},{10,... | collective-permute-start | bytes 552968 | tf_op jit(solution)/shard_map/ppermute | solution.py:106
  293.5 13.1 %collective-permute-start.6 = (bf16[256,360]{0,1:T(8,128)(2,1)S(1)}, bf16[256,360]{0,1:T(8,128)(2,1)S(1)}, u32[]{:S(2)}, u32[]{:S(2)}) collective-permute-start(bf16[256,360]{0,1:T(8,128)(2,1)S(1)} %get-tuple-element.24), channel_id=1, source_target_pairs={{0,3},{1,4},{2,5},{3,6},{4,7},{5,0},{6,1},{7,2},{8,11},{9,12},{10,... | collective-permute-start | bytes 552968 | tf_op jit(solution)/shard_map/ppermute | solution.py:106
  295.3 13.7 %collective-permute-start.5 = (bf16[256,360]{0,1:T(8,128)(2,1)S(1)}, bf16[256,360]{0,1:T(8,128)(2,1)}, u32[]{:S(2)}, u32[]{:S(2)}) collective-permute-start(bf16[256,360]{0,1:T(8,128)(2,1)S(1)} %get-tuple-element.25), channel_id=1, source_target_pairs={{0,2},{1,3},{2,4},{3,5},{4,6},{5,7},{6,0},{7,1},{8,10},{9,11},{10,... | collective-permute-start | bytes 552968 | tf_op jit(solution)/shard_map/ppermute | solution.py:106
Sparse Core Ops, SparseCore 0:
  12.1 91.6 all-gather.1
  205.3 76.2 reduce-scatter.2
  284.2 21.6 reduce-scatter.4

commit v2 on v1

--- a/solution.py
+++ b/solution.py
@@ -57,55 +57,36 @@
     return summed.reshape((summed.shape[0] * window,) + summed.shape[2:])
 
 
-def gather_weights(w_query, w_key, w_value, w_out):
-    pieces = (w_query, w_key, w_value, w_out)
-    flat = jnp.concatenate([p.reshape(-1) for p in pieces])
-    gathered = lax.all_gather(flat.reshape(1, -1, LANES), DP_AXES, axis=0, tiled=True)
-    peers = gathered.shape[0]
-    gathered = gathered.reshape(peers, -1)
-    full = []
-    at = 0
-    for p in pieces:
-        size = p.size
-        part = gathered[:, at : at + size].reshape((peers * p.shape[0],) + p.shape[1:])
-        full.append(part)
-        at += size
-    return full
-
-
-def scatter_weight_grads(partials, x_peers, z_peers):
-    rows = []
-    for p in partials:
-        blocked = p.astype(jnp.bfloat16).reshape(x_peers, z_peers, -1)
-        rows.append(jnp.swapaxes(blocked, 0, 1))
-    packed = jnp.concatenate(rows, axis=-1)
-    packed = packed.reshape(z_peers, x_peers, -1, LANES)
-    over_z = lax.psum_scatter(packed, "dz", scatter_dimension=0, tiled=True)[0]
-    over_x = lax.psum_scatter(over_z, "dx", scatter_dimension=0, tiled=True)[0]
-    over_x = over_x.reshape(-1)
-    out = []
-    at = 0
-    for p in partials:
-        size = p.size // (x_peers * z_peers)
-        shape = (p.shape[0] // (x_peers * z_peers),) + p.shape[1:]
-        out.append(over_x[at : at + size].astype(jnp.float32).reshape(shape))
-        at += size
-    return out
+def rows_of(array, lead):
+    return array.reshape(array.shape[:1] + lead + (-1,))
 
 
 def scatter_cols_mp(terms):
     peers = lax.axis_size("mp")
     me = lax.axis_index("mp")
-    width = terms.shape[1] // peers
-    blocks = terms.reshape(terms.shape[0], peers, width)
-    total = lax.dynamic_index_in_dim(blocks, me, axis=1, keepdims=False)
+    total = lax.dynamic_index_in_dim(terms, me, axis=1, keepdims=False)
     for shift in range(1, peers):
         dest = (me + shift) % peers
-        piece = lax.dynamic_index_in_dim(blocks, dest, axis=1, keepdims=False)
+        piece = lax.dynamic_index_in_dim(terms, dest, axis=1, keepdims=False)
         pairs = [(i, (i + shift) % peers) for i in range(peers)]
         got = lax.ppermute(piece.astype(jnp.bfloat16), "mp", pairs)
         total = total + got.astype(jnp.float32)
-    return total.astype(jnp.bfloat16)
+    return total.reshape(total.shape[0], -1).astype(jnp.bfloat16)
+
+
+def contract_by_z(left_side, right_side, x_peers, z_peers):
+    by_z = left_side.reshape(left_side.shape[0], x_peers, z_peers, -1).transpose(0, 2, 1, 3)
+    by_z = by_z.reshape(left_side.shape[0], z_peers, -1)
+    return jnp.einsum(
+        "tzq,tc->zqc", by_z, right_side, preferred_element_type=jnp.float32
+    ).astype(jnp.bfloat16)
+
+
+def scatter_rows_dp(part, x_peers):
+    over_z = lax.psum_scatter(part, "dz", scatter_dimension=0, tiled=True)[0]
+    over_z = over_z.reshape((x_peers, -1) + over_z.shape[1:])
+    over_x = lax.psum_scatter(over_z, "dx", scatter_dimension=0, tiled=True)[0]
+    return over_x.astype(jnp.float32)
 
 
 def shards(tokens, w_query, w_key, w_value, w_out, sinks, grad_out):
@@ -115,14 +96,21 @@
     score_scale = 1.0 / math.sqrt(DH)
     x_peers = lax.axis_size("dx")
     z_peers = lax.axis_size("dz")
-    full_query, full_key, full_value, full_out = gather_weights(w_query, w_key, w_value, w_out)
-    kv_heads = full_key.shape[1] // DH
-    group_size = full_query.shape[1] // DH // kv_heads
-    queries = jnp.dot(tokens, full_query, preferred_element_type=jnp.float32).astype(jnp.bfloat16)
-    key_rows = jnp.dot(tokens, full_key, preferred_element_type=jnp.float32).astype(jnp.bfloat16)
-    value_rows = jnp.dot(tokens, full_value, preferred_element_type=jnp.float32).astype(
+    mp_peers = lax.axis_size("mp")
+    dp_peers = x_peers * z_peers
+    q_cols, k_cols, v_cols = w_query.shape[1], w_key.shape[1], w_value.shape[1]
+    in_proj = jnp.concatenate([w_query, w_key, w_value], axis=1)
+    in_full, out_full = lax.all_gather((in_proj, w_out), DP_AXES, axis=0, tiled=False)
+    full_out = out_full.reshape((-1,) + out_full.shape[2:])
+    kv_heads = k_cols // DH
+    group_size = q_cols // DH // kv_heads
+    tokens_blk = rows_of(tokens, (dp_peers,))
+    qkv = jnp.einsum("tdr,drc->tc", tokens_blk, in_full, preferred_element_type=jnp.float32).astype(
         jnp.bfloat16
     )
+    queries = qkv[:, :q_cols]
+    key_rows = qkv[:, q_cols : q_cols + k_cols]
+    value_rows = qkv[:, q_cols + k_cols :]
     rim_keys, rim_values = passed_along((key_rows[-window:], value_rows[-window:]), DP_AXES, 1)
     grad_attn = contract_cols(grad_out, full_out).astype(jnp.bfloat16)
     first_row = (lax.axis_index("dx") * z_peers + lax.axis_index("dz")) * row_count
@@ -154,7 +142,6 @@
         "bkgij,bjkd->bikgd", prob_round, value_blk, preferred_element_type=jnp.float32
     ).astype(jnp.bfloat16)
     attn_rows = attended.reshape(row_count, -1)
-    grad_out_w = contract_rows(attn_rows, grad_out)
     row_delta = jnp.sum(
         dattn_blk.astype(jnp.float32) * attended.astype(jnp.float32), axis=-1
     ).transpose(0, 2, 3, 1)
@@ -189,25 +176,22 @@
     grad_values = jnp.concatenate(
         [own_values[:-window], own_values[-window:] + back_values], axis=0
     ).astype(jnp.bfloat16)
-    token_terms = (
-        contract_cols(grad_queries, full_query)
-        + contract_cols(grad_keys, full_key)
-        + contract_cols(grad_values, full_value)
+    grad_qkv = jnp.concatenate([grad_queries, grad_keys, grad_values], axis=1)
+    proj_by_mp = in_full.reshape((mp_peers, -1) + in_full.shape[1:])
+    token_terms = jnp.einsum(
+        "tc,mjrc->tmjr", grad_qkv, proj_by_mp, preferred_element_type=jnp.float32
     )
     grad_tokens = scatter_cols_mp(token_terms)
-    grad_q_term = contract_rows(tokens, grad_queries)
-    grad_k_term = contract_rows(tokens, grad_keys)
-    grad_v_term = contract_rows(tokens, grad_values)
-    summed_q, summed_k, summed_v, summed_out = scatter_weight_grads(
-        (grad_q_term, grad_k_term, grad_v_term, grad_out_w), x_peers, z_peers
-    )
-    grad_scale = 1.0 / math.sqrt(row_count * x_peers * z_peers)
+    grad_in = scatter_rows_dp(contract_by_z(tokens, grad_qkv, x_peers, z_peers), x_peers)
+    grad_w_out = scatter_rows_dp(contract_by_z(attn_rows, grad_out, x_peers, z_peers), x_peers)
+    grad_scale = 1.0 / math.sqrt(row_count * dp_peers)
+    grad_in = grad_in * grad_scale
     return (
         grad_tokens,
-        summed_q * grad_scale,
-        summed_k * grad_scale,
-        summed_v * grad_scale,
-        summed_out * grad_scale,
+        grad_in[:, :q_cols],
+        grad_in[:, q_cols : q_cols + k_cols],
+        grad_in[:, q_cols + k_cols :],
+        grad_w_out * grad_scale,
     )
 
 

time: 324 us -> 354 us (1.093)
  waiting for transfers between devices: 182 us -> 262 us
  local copies, waits for them, and re-layouts: 70.5 us -> 26.5 us
  other arithmetic: 12.3 us -> 7.14 us
    all_gather x1 -> x2, waiting for transfers between devices: 90.7 us -> 152 us  [shards(): lax.all_gather((in_proj, w_out), DP_AXES, axis=0, tiled=False)]
    unnamed x3 -> x7, waiting for transfers between devices: 0.05 us -> 36.8 us
    reshape x13 -> x4, local copies, waits for them, and re-layouts: 37.8 us -> 7.1 us  [the longest x2 2.46 us: shards(): grad_queries = jnp.einsum('bkgij,bjkd->bikgd', grad_scores, key_blk, pref...]
    reduce_scatter x2 -> x3, waiting for transfers between devices: 76.3 us -> 64 us  [the longest x2 44.1 us: scatter_rows_dp(): over_x = lax.psum_scatter(over_z, 'dx', scatter_dimension=0, tiled=True)[0]]
    ppermute x7, waiting for transfers between devices: 15.2 us -> 4.68 us  [scatter_cols_mp(): got = lax.ppermute(piece.astype(jnp.bfloat16), 'mp', pairs)]
    convert_element_type x4 -> x1, local copies, waits for them, and re-layouts: 9.13 us -> 0.73 us  [scatter_cols_mp(): return total.reshape(total.shape[0], -1).astype(jnp.bfloat16)]
    ppermute x4, waiting for transfers between devices: 0.01 us -> 4.93 us  [passed_along(): return lax.ppermute(array, axis, pairs)]
    reshape x2 -> x0, other arithmetic: 4.37 us -> none  [the longest x1 3.63 us: scatter_weight_grads(): packed = packed.reshape(z_peers, x_peers, -1, LANES)]
  transfers between devices with their start and end apart: 14 -> 17, of which waited for: 5 -> 9; matrix products, arithmetic and copies ran while one was open for 16% -> 11% of each run, Pallas kernels for 0% -> 0%
where the time goes in v2:
time: 354 us; the launch traced here: 351 us
  waiting for transfers between devices  262 us (74%)
  local copies, waits for them, and re-layouts  26.5 us (7%)
  matrix products  21.7 us (6%)
  starting transfers between devices  18.6 us (5%)
  between operations  14.8 us (4%)
  other arithmetic  7.14 us (2%)
    all_gather x2, waiting for transfers between devices, shards(): lax.all_gather((in_proj, w_out), DP_AXES, axis=0, tiled=False)  152 us
    reduce_scatter x2, waiting for transfers between devices, scatter_rows_dp(): over_x = lax.psum_scatter(over_z, 'dx', scatter_dimension=0, tiled=True)[0]  44.1 us
    unnamed x7, waiting for transfers between devices  36.8 us
    reduce_scatter x1, waiting for transfers between devices, scatter_rows_dp(): over_z = lax.psum_scatter(part, 'dz', scatter_dimension=0, tiled=True)[0]  19.9 us
    ppermute x4, starting transfers between devices, passed_along(): return lax.ppermute(array, axis, pairs)  11.5 us
  transfers between devices with their start and end apart: 17, of which 9 were waited for; matrix products, arithmetic and copies ran while one was open for 11% of the time, Pallas kernels for 0%

profile of v2, /device:TPU:2, one launch (start us, length us, event | category | flops | bytes accessed | tf_op | source)
XLA Modules:
  0.0 351.2 jit_solution(8313091047899712987)
XLA Ops:
  7.2 0.7 all-gather.6.cloned.1.call-update
  8.0 0.8 copy.92
  8.8 0.8 copy.91
  9.6 1.6 maximum_bitcast_fusion
  11.3 2.3 reshape.315
  14.1 77.5 %all-gather.6.cloned.1.call-done = bf16[512,2880]{1,0:T(8,128)(2,1)} async-done(((bf16[16,2880]{1,0:T(8,128)(2,1)}), bf16[512,2880]{1,0:T(8,128)(2,1)}) %all-gather.6.cloned.1.call-update) | async-done | bytes 2949136 | tf_op jit(solution)/shard_map/all_gather | solution.py:103
  91.6 2.9 convolution_convert_fusion.1
  94.5 1.2 reshape.345
  95.7 2.3 copy.102
  98.0 74.4 %all-gather.8.cloned.1.call-done = bf16[32,90,640]{2,1,0:T(8,128)(2,1)} async-done(((bf16[1,90,640]{2,1,0:T(8,128)(2,1)}), bf16[32,90,640]{2,1,0:T(8,128)(2,1)}) %all-gather.8.cloned.1.call-update) | async-done | bytes 3686416 | tf_op jit(solution)/shard_map/all_gather | solution.py:103
  172.5 3.3 fusion.8
  175.9 3.1 collective-permute-start.1
  179.0 2.6 collective-permute-start
  181.8 1.8 collective-permute-done.1
  183.6 3.2 collective-permute-done
  187.4 1.3 copy-done.1
  189.1 2.1 multiply_reduce_fusion
  191.7 2.8 convolution_convert_fusion
  194.5 2.3 reshape.325
  196.8 2.0 copy.114
  198.8 1.3 reshape.348
  200.4 2.2 convolution_bitcast_fusion.1
  202.6 0.6 slice_bitcast_fusion.1
  203.2 2.7 collective-permute-start.3
  206.0 0.6 fusion.6
  207.7 0.6 slice_bitcast_fusion.3
  208.6 3.0 collective-permute-start.2
  211.6 1.1 copy.131
  212.7 1.4 reshape.346
  214.1 0.7 fusion.46
  215.2 3.1 convert_bitcast_fusion
  218.4 19.9 %reduce-scatter.9.cloned.1.call-done = bf16[1,64,2880]{2,1,0:T(8,128)(2,1)} async-done(((bf16[8,64,2880]{2,1,0:T(8,128)(2,1)}), bf16[1,64,2880]{2,1,0:T(8,128)(2,1)}) %reduce-scatter.9.cloned.1.call-update) | async-done | bytes 368656 | tf_op jit(solution)/shard_map/reduce_scatter | solution.py:86
  238.4 3.5 %fusion.19 = f32[256,8,4,90]{0,3,2,1:T(8,128)S(1)} fusion(bf16[8,4,90,640]{3,2,1,0:T(8,128)(2,1)} %bitcast.191, bf16[256,64]{1,0:T(8,128)(2,1)S(1)} %copy.113, bf16[256,64]{1,0:T(8,128)(2,1)S(1)} %copy.112, bf16[256,512]{1,0:T(8,128)(2,1)S(1)} %reshape.346), kind=kOutput, calls=%fused_computation.43 | convolution fusion | flops 944701440 | bytes 6963200 | tf_op jit(solution)/shard_map/tc,mjrc->tmjr/dot_general | solution.py:181
  242.0 1.6 copy-done.3
  243.8 3.0 collective-permute-start.9
  247.2 2.9 collective-permute-start.7
  250.6 4.7 %collective-permute-done.9 = bf16[256,4,90]{0,2,1:T(8,128)(2,1)S(1)} collective-permute-done((bf16[256,4,90]{0,2,1:T(8,128)(2,1)S(1)}, bf16[256,4,90]{0,2,1:T(8,128)(2,1)S(1)}, u32[]{:S(2)}, u32[]{:S(2)}) %collective-permute-start.9) | collective-permute-done | bytes 184352 | tf_op jit(solution)/shard_map/ppermute | solution.py:72
  255.3 36.1 %reduce-scatter.13.cloned.1.call-done = bf16[1,360,640]{2,1,0:T(8,128)(2,1)} async-done(((bf16[8,360,640]{2,1,0:T(8,128)(2,1)}), bf16[1,360,640]{2,1,0:T(8,128)(2,1)}) %reduce-scatter.13.cloned.1.call-update) | async-done | bytes 460816
  291.4 1.9 reshape_squeeze.6
  293.4 1.4 fusion.18
  294.8 0.7 convert_element_type.198
  295.5 19.7 %reduce-scatter.11.cloned.1.call-done = bf16[1,16,2880]{2,1,0:T(8,128)(2,1)} async-done(((bf16[4,16,2880]{2,1,0:T(8,128)(2,1)}), bf16[1,16,2880]{2,1,0:T(8,128)(2,1)}) %reduce-scatter.11.cloned.1.call-update) | async-done | bytes 92176 | tf_op jit(solution)/shard_map/reduce_scatter | solution.py:88
  315.2 1.6 multiply_bitcast_fusion.1
  316.8 24.5 %reduce-scatter.7.cloned.1.call-done = bf16[1,90,640]{2,1,0:T(8,128)(2,1)} async-done(((bf16[4,90,640]{2,1,0:T(8,128)(2,1)}), bf16[1,90,640]{2,1,0:T(8,128)(2,1)}) %reduce-scatter.7.cloned.1.call-update) | async-done | bytes 115216 | tf_op jit(solution)/shard_map/reduce_scatter | solution.py:88
  341.2 0.9 multiply_bitcast_fusion
  342.1 0.7 slice.147
  342.9 0.7 copy.118
  343.6 0.7 copy.119
  (84 shorter events, 5.5 us)
Async XLA Ops:
  7.2 84.4 %copy-start = (bf16[256,2880]{0,1:T(8,128)(2,1)S(1)}, bf16[256,2880]{0,1:T(8,128)(2,1)}, u32[]{:S(2)}) copy-start(bf16[256,2880]{0,1:T(8,128)(2,1)} %param.13) | copy-start | bytes 4423684
  7.2 84.4 %all-gather.6.cloned.1.call-start = ((), (), s32[]{:S(2)}) async-start(), calls=%async_computation.7 | async-start | bytes 3108864 | tf_op jit(solution)/shard_map/all_gather | solution.py:103
  7.9 164.6 %all-gather.8.cloned.1.call-start = ((), (), s32[]{:S(2)}) async-start(), calls=%async_computation.8 | async-start | bytes 4055040 | tf_op jit(solution)/shard_map/all_gather | solution.py:103
  11.3 227.0 %reduce-scatter.9.cloned.1.call-start = ((), (), s32[]{:S(2)}) async-start(), calls=%async_computation.5 | async-start | bytes 3391488 | tf_op jit(solution)/shard_map/reduce_scatter | solution.py:86
  94.5 81.4 %copy-start.6 = (bf16[256,512]{1,0:T(8,128)(2,1)}, bf16[256,512]{1,0:T(8,128)(2,1)S(1)}, u32[]{:S(2)}) copy-start(bf16[256,512]{1,0:T(8,128)(2,1)S(1)} %convolution_convert_fusion.1) | copy-start | bytes 786436
  175.9 7.7 %collective-permute-start.1 = (bf16[128,64]{0,1:T(8,128)(2,1)S(1)}, bf16[128,64]{0,1:T(8,128)(2,1)S(1)}, u32[]{:S(2)}, u32[]{:S(2)}) collective-permute-start(bf16[128,64]{0,1:T(8,128)(2,1)S(1)} %get-tuple-element.32), channel_id=1, source_target_pairs={{0,8},{8,16},{16,24},{24,32},{32,40},{40,48},{48,56},{56,64},{64,7... | collective-permute-start | bytes 49160 | tf_op jit(solution)/shard_map/ppermute | solution.py:21
  179.0 8.3 %copy-start.11 = (f32[8]{0:T(128)S(1)}, f32[8]{0:T(128)}, u32[]{:S(2)}) copy-start(f32[8]{0:T(128)} %param.12) | copy-start | bytes 100
  179.0 7.7 %collective-permute-start = (bf16[128,64]{0,1:T(8,128)(2,1)S(1)}, bf16[128,64]{0,1:T(8,128)(2,1)S(1)}, u32[]{:S(2)}, u32[]{:S(2)}) collective-permute-start(bf16[128,64]{0,1:T(8,128)(2,1)S(1)} %get-tuple-element.33), channel_id=1, source_target_pairs={{0,8},{8,16},{16,24},{24,32},{32,40},{40,48},{48,56},{56,64},{64,7... | collective-permute-start | bytes 49160 | tf_op jit(solution)/shard_map/ppermute | solution.py:21
  186.8 2.2 copy-start.8
  186.8 2.3 copy-start.5
  187.3 1.4 copy-start.1
  194.5 96.9 %reduce-scatter.13.cloned.1.call-start = ((), (), s32[]{:S(2)}) async-start(), calls=%async_computation.9 | async-start | bytes 4147200
  200.4 5.5 %copy-start.2 = (f32[2,1,8,128,256]{3,4,2,0,1:T(8,128)S(1)}, f32[2,1,8,128,256]{3,4,2,0,1:T(8,128)}, u32[]{:S(2)}) copy-start(f32[2,1,8,128,256]{3,4,2,0,1:T(8,128)} %copy-done.1) | copy-start | bytes 6291460
  203.2 10.9 %collective-permute-start.3 = (bf16[128,64]{0,1:T(8,128)(2,1)}, bf16[128,64]{0,1:T(8,128)(2,1)}, u32[]{:S(2)}, u32[]{:S(2)}) collective-permute-start(bf16[128,64]{0,1:T(8,128)(2,1)} %get-tuple-element.45), channel_id=1, source_target_pairs={{8,0},{16,8},{24,16},{32,24},{40,32},{48,40},{56,48},{64,56},{72,6... | collective-permute-start | bytes 49160 | tf_op jit(solution)/shard_map/ppermute | solution.py:21
  205.9 2.4 copy-start.9
  207.0 7.8 %copy-start.10 = (bf16[128,64]{0,1:T(8,128)(2,1)S(1)}, bf16[128,64]{0,1:T(8,128)(2,1)}, u32[]{:S(2)}) copy-start(bf16[128,64]{0,1:T(8,128)(2,1)} %get-tuple-element.44) | copy-start | bytes 49156
  207.1 8.1 %copy-start.4 = (bf16[256,8,4,90]{0,1,3,2:T(8,128)(2,1)S(1)}, bf16[256,8,4,90]{0,1,3,2:T(8,128)(2,1)}, u32[]{:S(2)}) copy-start(bf16[256,8,4,90]{0,1,3,2:T(8,128)(2,1)} %copy.114) | copy-start | bytes 4423684
  207.1 0.6 copy-start.7
  208.6 6.4 %collective-permute-start.2 = (bf16[128,64]{0,1:T(8,128)(2,1)}, bf16[128,64]{0,1:T(8,128)(2,1)S(1)}, u32[]{:S(2)}, u32[]{:S(2)}) collective-permute-start(bf16[128,64]{0,1:T(8,128)(2,1)} %get-tuple-element.43), channel_id=1, source_target_pairs={{8,0},{16,8},{24,16},{32,24},{40,32},{48,40},{56,48},{64,56},{72,6... | collective-permute-start | bytes 49160 | tf_op jit(solution)/shard_map/ppermute | solution.py:21
  218.3 96.9 %reduce-scatter.11.cloned.1.call-start = ((), (), s32[]{:S(2)}) async-start(), calls=%async_computation.6 | async-start | bytes 471040 | tf_op jit(solution)/shard_map/reduce_scatter | solution.py:88
  238.3 102.9 %reduce-scatter.7.cloned.1.call-start = ((), (), s32[]{:S(2)}) async-start(), calls=%async_computation.4 | async-start | bytes 614400 | tf_op jit(solution)/shard_map/reduce_scatter | solution.py:88
  242.0 1.6 copy-start.3
  243.8 6.3 %collective-permute-start.10 = (bf16[256,4,90]{0,2,1:T(8,128)(2,1)S(1)}, bf16[256,4,90]{0,2,1:T(8,128)(2,1)S(1)}, u32[]{:S(2)}, u32[]{:S(2)}) collective-permute-start(bf16[256,4,90]{0,2,1:T(8,128)(2,1)S(1)} %get-tuple-element.26), channel_id=1, source_target_pairs={{0,7},{1,0},{2,1},{3,2},{4,3},{5,4},{6,5},{7,6},{8,15},{9,8},{10,9... | collective-permute-start | bytes 552968 | tf_op jit(solution)/shard_map/ppermute | solution.py:72
  243.8 11.5 %collective-permute-start.9 = (bf16[256,4,90]{0,2,1:T(8,128)(2,1)S(1)}, bf16[256,4,90]{0,2,1:T(8,128)(2,1)S(1)}, u32[]{:S(2)}, u32[]{:S(2)}) collective-permute-start(bf16[256,4,90]{0,2,1:T(8,128)(2,1)S(1)} %get-tuple-element.27), channel_id=1, source_target_pairs={{0,6},{1,7},{2,0},{3,1},{4,2},{5,3},{6,4},{7,5},{8,14},{9,15},{10,... | collective-permute-start | bytes 552968 | tf_op jit(solution)/shard_map/ppermute | solution.py:72
  246.8 46.5 %collective-permute-start.8 = (bf16[256,4,90]{0,2,1:T(8,128)(2,1)S(1)}, bf16[256,4,90]{0,2,1:T(8,128)(2,1)S(1)}, u32[]{:S(2)}, u32[]{:S(2)}) collective-permute-start(bf16[256,4,90]{0,2,1:T(8,128)(2,1)S(1)} %get-tuple-element.28), channel_id=1, source_target_pairs={{0,5},{1,6},{2,7},{3,0},{4,1},{5,2},{6,3},{7,4},{8,13},{9,14},{10,... | collective-permute-start | bytes 552968 | tf_op jit(solution)/shard_map/ppermute | solution.py:72
  247.2 46.1 %collective-permute-start.7 = (bf16[256,4,90]{0,2,1:T(8,128)(2,1)S(1)}, bf16[256,4,90]{0,2,1:T(8,128)(2,1)S(1)}, u32[]{:S(2)}, u32[]{:S(2)}) collective-permute-start(bf16[256,4,90]{0,2,1:T(8,128)(2,1)S(1)} %get-tuple-element.29), channel_id=1, source_target_pairs={{0,4},{1,5},{2,6},{3,7},{4,0},{5,1},{6,2},{7,3},{8,12},{9,13},{10,... | collective-permute-start | bytes 552968 | tf_op jit(solution)/shard_map/ppermute | solution.py:72
  250.1 43.3 %collective-permute-start.6 = (bf16[256,4,90]{0,2,1:T(8,128)(2,1)S(1)}, bf16[256,4,90]{0,2,1:T(8,128)(2,1)S(1)}, u32[]{:S(2)}, u32[]{:S(2)}) collective-permute-start(bf16[256,4,90]{0,2,1:T(8,128)(2,1)S(1)} %get-tuple-element.30), channel_id=1, source_target_pairs={{0,3},{1,4},{2,5},{3,6},{4,7},{5,0},{6,1},{7,2},{8,11},{9,12},{10,... | collective-permute-start | bytes 552968 | tf_op jit(solution)/shard_map/ppermute | solution.py:72
  250.1 43.3 %collective-permute-start.5 = (bf16[256,4,90]{0,2,1:T(8,128)(2,1)S(1)}, bf16[256,4,90]{0,2,1:T(8,128)(2,1)}, u32[]{:S(2)}, u32[]{:S(2)}) collective-permute-start(bf16[256,4,90]{0,2,1:T(8,128)(2,1)S(1)} %get-tuple-element.31), channel_id=1, source_target_pairs={{0,2},{1,3},{2,4},{3,5},{4,6},{5,7},{6,0},{7,1},{8,10},{9,11},{10,... | collective-permute-start | bytes 552968 | tf_op jit(solution)/shard_map/ppermute | solution.py:72
  255.3 38.1 %collective-permute-start.4 = (bf16[256,4,90]{0,2,1:T(8,128)(2,1)S(1)}, bf16[256,4,90]{0,2,1:T(8,128)(2,1)}, u32[]{:S(2)}, u32[]{:S(2)}) collective-permute-start(bf16[256,4,90]{0,2,1:T(8,128)(2,1)S(1)} %get-tuple-element.25), channel_id=1, source_target_pairs={{0,1},{1,2},{2,3},{3,4},{4,5},{5,6},{6,7},{7,0},{8,9},{9,10},{10,1... | collective-permute-start | bytes 552968 | tf_op jit(solution)/shard_map/ppermute | solution.py:72
Sparse Core Ops, SparseCore 0:
  10.6 80.9 all-gather.5
  94.7 77.7 all-gather.7
  194.6 43.7 reduce-scatter.8
  240.8 50.5 reduce-scatter.12
  293.7 21.3 reduce-scatter.10
  317.6 23.5 reduce-scatter.6

commit v3 on v2

--- a/solution.py
+++ b/solution.py
@@ -74,19 +74,9 @@
     return total.reshape(total.shape[0], -1).astype(jnp.bfloat16)
 
 
-def contract_by_z(left_side, right_side, x_peers, z_peers):
-    by_z = left_side.reshape(left_side.shape[0], x_peers, z_peers, -1).transpose(0, 2, 1, 3)
-    by_z = by_z.reshape(left_side.shape[0], z_peers, -1)
-    return jnp.einsum(
-        "tzq,tc->zqc", by_z, right_side, preferred_element_type=jnp.float32
-    ).astype(jnp.bfloat16)
-
-
-def scatter_rows_dp(part, x_peers):
-    over_z = lax.psum_scatter(part, "dz", scatter_dimension=0, tiled=True)[0]
-    over_z = over_z.reshape((x_peers, -1) + over_z.shape[1:])
-    over_x = lax.psum_scatter(over_z, "dx", scatter_dimension=0, tiled=True)[0]
-    return over_x.astype(jnp.float32)
+def by_zx(rows, x_peers, z_peers):
+    split = rows.reshape(rows.shape[0], x_peers, z_peers, -1)
+    return split.transpose(0, 2, 1, 3)
 
 
 def shards(tokens, w_query, w_key, w_value, w_out, sinks, grad_out):
@@ -99,9 +89,14 @@
     mp_peers = lax.axis_size("mp")
     dp_peers = x_peers * z_peers
     q_cols, k_cols, v_cols = w_query.shape[1], w_key.shape[1], w_value.shape[1]
-    in_proj = jnp.concatenate([w_query, w_key, w_value], axis=1)
-    in_full, out_full = lax.all_gather((in_proj, w_out), DP_AXES, axis=0, tiled=False)
-    full_out = out_full.reshape((-1,) + out_full.shape[2:])
+    in_width = q_cols + k_cols + v_cols
+    out_rows = w_out.shape[0]
+    packed = jnp.concatenate(
+        [w_query, w_key, w_value, w_out.reshape(w_query.shape[0], -1)], axis=1
+    )
+    gathered = lax.all_gather(packed, DP_AXES, axis=0, tiled=False)
+    in_full = gathered[:, :, :in_width]
+    full_out = gathered[:, :, in_width:].reshape((-1,) + w_out.shape[1:])
     kv_heads = k_cols // DH
     group_size = q_cols // DH // kv_heads
     tokens_blk = rows_of(tokens, (dp_peers,))
@@ -182,8 +177,21 @@
         "tc,mjrc->tmjr", grad_qkv, proj_by_mp, preferred_element_type=jnp.float32
     )
     grad_tokens = scatter_cols_mp(token_terms)
-    grad_in = scatter_rows_dp(contract_by_z(tokens, grad_qkv, x_peers, z_peers), x_peers)
-    grad_w_out = scatter_rows_dp(contract_by_z(attn_rows, grad_out, x_peers, z_peers), x_peers)
+    tokens_zx = by_zx(tokens, x_peers, z_peers)
+    grad_in_part = jnp.einsum(
+        "tzxr,tc->zxrc", tokens_zx, grad_qkv, preferred_element_type=jnp.float32
+    ).astype(jnp.bfloat16)
+    attn_zx = by_zx(attn_rows, x_peers, z_peers)
+    grad_out_part = jnp.einsum(
+        "tzxi,tc->zxic", attn_zx, grad_out, preferred_element_type=jnp.float32
+    ).astype(jnp.bfloat16)
+    grad_out_part = grad_out_part.reshape(z_peers, x_peers, -1, in_width)
+    both = jnp.concatenate([grad_in_part, grad_out_part], axis=2)
+    over_z = lax.psum_scatter(both, "dz", scatter_dimension=0, tiled=True)[0]
+    over_x = lax.psum_scatter(over_z, "dx", scatter_dimension=0, tiled=True)[0].astype(jnp.float32)
+    in_rows = w_query.shape[0]
+    grad_in = over_x[:in_rows]
+    grad_w_out = over_x[in_rows:].reshape(w_out.shape)
     grad_scale = 1.0 / math.sqrt(row_count * dp_peers)
     grad_in = grad_in * grad_scale
     return (

time: 354 us -> 286 us (0.81)
  waiting for transfers between devices: 262 us -> 187 us
  local copies, waits for them, and re-layouts: 26.5 us -> 36.7 us
  matrix products: 21.7 us -> 16.8 us
    all_gather x2 -> x1, waiting for transfers between devices: 152 us -> 88.4 us  [shards(): gathered = lax.all_gather(packed, DP_AXES, axis=0, tiled=False)]
    unnamed x7 -> x4, waiting for transfers between devices: 36.8 us -> 0.05 us
    ppermute x7, waiting for transfers between devices: 4.68 us -> 20 us  [scatter_cols_mp(): got = lax.ppermute(piece.astype(jnp.bfloat16), 'mp', pairs)]
    reduce_scatter x3 -> x1, waiting for transfers between devices: 64 us -> 78.3 us  [shards(): over_z = lax.psum_scatter(both, 'dz', scatter_dimension=0, tiled=True)[0]]
    reshape x1 -> x4, local copies, waits for them, and re-layouts: 2.32 us -> 16.6 us  [the longest x1 7.16 us: shards(): grad_out_part = grad_out_part.reshape(z_peers, x_peers, -1, in_width)]
    concatenate x0 -> x1, other arithmetic: none -> 6.22 us  [shards(): both = jnp.concatenate([grad_in_part, grad_out_part], axis=2)]
    ppermute x4, waiting for transfers between devices: 4.93 us -> 0.01 us  [passed_along(): return lax.ppermute(array, axis, pairs)]
    slice x0 -> x3, local copies, waits for them, and re-layouts: none -> 4.22 us  [the longest x1 2.11 us: shards(): full_out = gathered[:, :, in_width:].reshape((-1,) + w_out.shape[1:])]
  transfers between devices with their start and end apart: 17 -> 14, of which waited for: 9 -> 6; matrix products, arithmetic and copies ran while one was open for 11% -> 13% of each run, Pallas kernels for 0% -> 0%
where the time goes in v3:
time: 286 us; the launch traced here: 285 us
  waiting for transfers between devices  187 us (65%)
  local copies, waits for them, and re-layouts  36.7 us (13%)
  starting transfers between devices  20.2 us (7%)
  matrix products  16.8 us (6%)
  between operations  14.3 us (5%)
  other arithmetic  10.2 us (4%)
    all_gather x1, waiting for transfers between devices, shards(): gathered = lax.all_gather(packed, DP_AXES, axis=0, tiled=False)  88.4 us
    reduce_scatter x1, waiting for transfers between devices, shards(): over_z = lax.psum_scatter(both, 'dz', scatter_dimension=0, tiled=True)[0]  78.3 us
    ppermute x7, waiting for transfers between devices, scatter_cols_mp(): got = lax.ppermute(piece.astype(jnp.bfloat16), 'mp', pairs)  20 us
    ppermute x4, starting transfers between devices, passed_along(): return lax.ppermute(array, axis, pairs)  14 us
    reshape x1, local copies, waits for them, and re-layouts, shards(): grad_out_part = grad_out_part.reshape(z_peers, x_peers, -1, in_width)  7.16 us
    reshape x1, local copies, waits for them, and re-layouts, shards(): full_out = gathered[:, :, in_width:].reshape((-1,) + w_out.shape[1:])  6.98 us
    concatenate x1, other arithmetic, shards(): both = jnp.concatenate([grad_in_part, grad_out_part], axis=2)  6.22 us
    ppermute x7, starting transfers between devices, scatter_cols_mp(): got = lax.ppermute(piece.astype(jnp.bfloat16), 'mp', pairs)  6.13 us
  transfers between devices with their start and end apart: 14, of which 6 were waited for; matrix products, arithmetic and copies ran while one was open for 13% of the time, Pallas kernels for 0%

profile of v3, /device:TPU:2, one launch (start us, length us, event | category | flops | bytes accessed | tf_op | source)
XLA Modules:
  0.0 285.0 jit_solution(15213676688187044288)
XLA Ops:
  7.2 1.0 copy.60
  8.2 0.8 copy.61
  9.0 1.1 reshape.320
  10.1 1.7 concatenate.29
  11.9 3.4 %reshape.321 = bf16[256,32,90]{0,2,1:T(8,128)(2,1)} reshape(bf16[256,2880]{0,1:T(8,128)(2,1)} %param.7) | data formatting | bytes 2949120 | tf_op jit(solution)/shard_map/reshape | solution.py:61
  15.2 1.4 reshape.331
  17.0 88.4 %all-gather.4.cloned.1.call-done = bf16[32,90,1152]{2,1,0:T(8,128)(2,1)} async-done(((bf16[1,90,1152]{2,1,0:T(8,128)(2,1)}), bf16[32,90,1152]{2,1,0:T(8,128)(2,1)}) %all-gather.4.cloned.1.call-update) | async-done | bytes 6635536 | tf_op jit(solution)/shard_map/all_gather | solution.py:97
  105.4 4.0 %fusion.8 = bf16[256,640]{0,1:T(8,128)(2,1)S(1)} fusion(bf16[256,32,90]{0,2,1:T(8,128)(2,1)} %reshape.321, bf16[32,90,1152]{2,1,0:T(8,128)(2,1)} %all-gather.4.cloned.1.call-done), kind=kOutput, calls=%fused_computation.19 | convolution fusion | flops 943882240 | bytes 5832704 | tf_op jit(solution)/shard_map/tdr,drc->tc/dot_general | solution.py:103
  109.4 2.9 %collective-permute-start.1 = (bf16[128,64]{0,1:T(8,128)(2,1)S(1)}, bf16[128,64]{0,1:T(8,128)(2,1)S(1)}, u32[]{:S(2)}, u32[]{:S(2)}) collective-permute-start(bf16[128,64]{0,1:T(8,128)(2,1)S(1)} %get-tuple-element.27), channel_id=1, source_target_pairs={{0,8},{8,16},{16,24},{24,32},{32,40},{40,48},{48,56},{56,64},{64,7... | collective-permute-start | bytes 49160 | tf_op jit(solution)/shard_map/ppermute | solution.py:21
  112.3 3.0 %collective-permute-start = (bf16[128,64]{0,1:T(8,128)(2,1)S(1)}, bf16[128,64]{0,1:T(8,128)(2,1)S(1)}, u32[]{:S(2)}, u32[]{:S(2)}) collective-permute-start(bf16[128,64]{0,1:T(8,128)(2,1)S(1)} %get-tuple-element.28), channel_id=1, source_target_pairs={{0,8},{8,16},{16,24},{24,32},{32,40},{40,48},{48,56},{56,64},{64,7... | collective-permute-start | bytes 49160 | tf_op jit(solution)/shard_map/ppermute | solution.py:21
  115.4 2.1 slice.154
  117.5 7.0 %reshape.325 = bf16[512,2880]{1,0:T(8,128)(2,1)} reshape(bf16[32,90,512]{2,1,0:T(8,128)(2,1)} %slice.154) | data formatting | bytes 5898240 | tf_op jit(solution)/shard_map/reshape | solution.py:99
  124.5 2.8 fusion.11
  127.9 0.5 fusion.63
  128.9 0.5 convolution_bitcast_fusion.1
  129.3 0.5 copy-done.1
  129.8 0.6 slice_bitcast_fusion.1
  130.4 4.9 %collective-permute-start.3 = (bf16[128,64]{0,1:T(8,128)(2,1)}, bf16[128,64]{0,1:T(8,128)(2,1)S(1)}, u32[]{:S(2)}, u32[]{:S(2)}) collective-permute-start(bf16[128,64]{0,1:T(8,128)(2,1)} %get-tuple-element.40), channel_id=1, source_target_pairs={{8,0},{16,8},{24,16},{32,24},{40,32},{48,40},{56,48},{64,56},{72,6... | collective-permute-start | bytes 49160 | tf_op jit(solution)/shard_map/ppermute | solution.py:21
  135.4 2.2 fusion.13
  137.6 0.6 fusion.6
  138.3 0.4 convolution_bitcast_fusion.2
  138.8 0.6 slice_bitcast_fusion.3
  139.4 3.1 %collective-permute-start.2 = (bf16[128,64]{0,1:T(8,128)(2,1)}, bf16[128,64]{0,1:T(8,128)(2,1)}, u32[]{:S(2)}, u32[]{:S(2)}) collective-permute-start(bf16[128,64]{0,1:T(8,128)(2,1)} %get-tuple-element.38), channel_id=1, source_target_pairs={{8,0},{16,8},{24,16},{32,24},{40,32},{48,40},{56,48},{64,56},{72,6... | collective-permute-start | bytes 49160 | tf_op jit(solution)/shard_map/ppermute | solution.py:21
  142.9 2.7 convolution_convert_fusion
  146.2 0.3 reshape.345
  146.6 7.2 %reshape.332 = bf16[8,4,72,640]{3,2,1,0:T(8,128)(2,1)} reshape(bf16[8,4,16,2880]{3,2,1,0:T(8,128)(2,1)} %convolution_convert_fusion) | data formatting | bytes 5898240 | tf_op jit(solution)/shard_map/reshape | solution.py:188
  153.9 0.7 fusion.46
  154.8 1.4 convert_bitcast_fusion
  156.2 6.2 %pad_maximum_fusion = bf16[8,4,162,640]{3,2,1,0:T(8,128)(2,1)} fusion(bf16[8,4,72,640]{3,2,1,0:T(8,128)(2,1)} %reshape.332, bf16[8,4,90,640]{3,2,1,0:T(8,128)(2,1)S(1)} %convert_bitcast_fusion), kind=kLoop, calls=%fused_computation | loop fusion | flops 13271040 | bytes 13271040 | tf_op jit(solution)/shard_map/concatenate | solution.py:189
  162.4 78.3 %reduce-scatter.5.cloned.1.call-done = bf16[1,4,162,640]{3,2,1,0:T(8,128)(2,1)} async-done(((bf16[8,4,162,640]{3,2,1,0:T(8,128)(2,1)}), bf16[1,4,162,640]{3,2,1,0:T(8,128)(2,1)}) %reduce-scatter.5.cloned.1.call-update) | async-done | bytes 829456 | tf_op jit(solution)/shard_map/reduce_scatter | solution.py:190
  240.9 2.1 slice-done
  243.0 1.4 fusion.38
  244.5 1.6 copy-done.4
  246.2 2.1 collective-permute-start.10
  248.4 0.9 collective-permute-start.9
  249.2 0.4 collective-permute-start.8
  249.7 2.7 collective-permute-start.7
  252.4 1.1 collective-permute-done.10
  253.5 12.5 %collective-permute-done.9 = bf16[256,4,90]{0,2,1:T(8,128)(2,1)S(1)} collective-permute-done((bf16[256,4,90]{0,2,1:T(8,128)(2,1)S(1)}, bf16[256,4,90]{0,2,1:T(8,128)(2,1)S(1)}, u32[]{:S(2)}, u32[]{:S(2)}) %collective-permute-start.9) | collective-permute-done | bytes 184352 | tf_op jit(solution)/shard_map/ppermute | solution.py:72
  266.0 2.7 collective-permute-done.5
  268.8 3.6 %collective-permute-done.4 = bf16[256,4,90]{0,2,1:T(8,128)(2,1)} collective-permute-done((bf16[256,4,90]{0,2,1:T(8,128)(2,1)S(1)}, bf16[256,4,90]{0,2,1:T(8,128)(2,1)}, u32[]{:S(2)}, u32[]{:S(2)}) %collective-permute-start.4) | collective-permute-done | bytes 184352 | tf_op jit(solution)/shard_map/ppermute | solution.py:72
  272.4 1.4 fusion.20
  273.8 0.7 convert_element_type.198
  274.5 1.0 convert_element_type.202
  275.5 0.7 slice.168
  276.3 0.7 copy.84
  277.0 0.7 copy.85
  277.7 0.8 mul.65
  (73 shorter events, 3.2 us)
Async XLA Ops:
  7.2 117.3 %copy-start = (bf16[256,2880]{0,1:T(8,128)(2,1)S(1)}, bf16[256,2880]{0,1:T(8,128)(2,1)}, u32[]{:S(2)}) copy-start(bf16[256,2880]{0,1:T(8,128)(2,1)} %param.13) | copy-start | bytes 4423684
  7.2 8.1 %copy-start.6 = (bf16[256,2880]{0,1:T(8,128)(2,1)S(1)}, bf16[256,2880]{0,1:T(8,128)(2,1)}, u32[]{:S(2)}) copy-start(bf16[256,2880]{0,1:T(8,128)(2,1)} %param.7) | copy-start | bytes 4423684
  7.2 98.2 %all-gather.4.cloned.1.call-start = ((), (), s32[]{:S(2)}) async-start(), calls=%async_computation.3 | async-start | bytes 7299072 | tf_op jit(solution)/shard_map/all_gather | solution.py:97
  11.8 228.9 %reduce-scatter.5.cloned.1.call-start = ((), (), s32[]{:S(2)}) async-start(), calls=%async_computation.2 | async-start | bytes 7741440 | tf_op jit(solution)/shard_map/reduce_scatter | solution.py:190
  105.4 10.0 %copy-start.3 = (bf16[32,90,1152]{2,1,0:T(8,128)(2,1)S(1)}, bf16[32,90,1152]{2,1,0:T(8,128)(2,1)}, u32[]{:S(2)}) copy-start(bf16[32,90,1152]{2,1,0:T(8,128)(2,1)} %all-gather.4.cloned.1.call-done) | copy-start | bytes 19906564
  109.4 18.5 %collective-permute-start.1 = (bf16[128,64]{0,1:T(8,128)(2,1)S(1)}, bf16[128,64]{0,1:T(8,128)(2,1)S(1)}, u32[]{:S(2)}, u32[]{:S(2)}) collective-permute-start(bf16[128,64]{0,1:T(8,128)(2,1)S(1)} %get-tuple-element.27), channel_id=1, source_target_pairs={{0,8},{8,16},{16,24},{24,32},{32,40},{40,48},{48,56},{56,64},{64,7... | collective-permute-start | bytes 49160 | tf_op jit(solution)/shard_map/ppermute | solution.py:21
  112.3 15.5 %collective-permute-start = (bf16[128,64]{0,1:T(8,128)(2,1)S(1)}, bf16[128,64]{0,1:T(8,128)(2,1)S(1)}, u32[]{:S(2)}, u32[]{:S(2)}) collective-permute-start(bf16[128,64]{0,1:T(8,128)(2,1)S(1)} %get-tuple-element.28), channel_id=1, source_target_pairs={{0,8},{8,16},{16,24},{24,32},{32,40},{40,48},{48,56},{56,64},{64,7... | collective-permute-start | bytes 49160 | tf_op jit(solution)/shard_map/ppermute | solution.py:21
  127.4 1.0 copy-start.8
  128.4 1.4 copy-start.1
  130.4 23.3 %collective-permute-start.3 = (bf16[128,64]{0,1:T(8,128)(2,1)}, bf16[128,64]{0,1:T(8,128)(2,1)S(1)}, u32[]{:S(2)}, u32[]{:S(2)}) collective-permute-start(bf16[128,64]{0,1:T(8,128)(2,1)} %get-tuple-element.40), channel_id=1, source_target_pairs={{8,0},{16,8},{24,16},{32,24},{40,32},{48,40},{56,48},{64,56},{72,6... | collective-permute-start | bytes 49160 | tf_op jit(solution)/shard_map/ppermute | solution.py:21
  135.4 2.2 copy-start.2
  138.7 3.7 %copy-start.7 = (f32[2,128,1,64]{1,3,0,2:T(8,128)}, f32[2,128,1,64]{1,3,0,2:T(8,128)S(1)}, u32[]{:S(2)}) copy-start(f32[2,128,1,64]{1,3,0,2:T(8,128)S(1)} %get-tuple-element.34) | copy-start | bytes 196612
  139.4 14.5 %collective-permute-start.2 = (bf16[128,64]{0,1:T(8,128)(2,1)}, bf16[128,64]{0,1:T(8,128)(2,1)}, u32[]{:S(2)}, u32[]{:S(2)}) collective-permute-start(bf16[128,64]{0,1:T(8,128)(2,1)} %get-tuple-element.38), channel_id=1, source_target_pairs={{8,0},{16,8},{24,16},{32,24},{40,32},{48,40},{56,48},{64,56},{72,6... | collective-permute-start | bytes 49160 | tf_op jit(solution)/shard_map/ppermute | solution.py:21
  146.6 8.2 %copy-start.5 = (bf16[256,4,8,90]{0,3,2,1:T(8,128)(2,1)S(1)}, bf16[256,4,8,90]{0,3,2,1:T(8,128)(2,1)}, u32[]{:S(2)}) copy-start(bf16[256,4,8,90]{0,3,2,1:T(8,128)(2,1)} %reshape.331) | copy-start | bytes 4423684
  162.4 112.1 %reduce-scatter.7.cloned.1.call-start = ((), (), s32[]{:S(2)}) async-start(), calls=%async_computation.4 | async-start | bytes 1075200
  240.9 2.1 slice-start
  244.4 1.6 copy-start.4
  246.2 7.2 %collective-permute-start.10 = (bf16[256,4,90]{0,2,1:T(8,128)(2,1)S(1)}, bf16[256,4,90]{0,2,1:T(8,128)(2,1)S(1)}, u32[]{:S(2)}, u32[]{:S(2)}) collective-permute-start(bf16[256,4,90]{0,2,1:T(8,128)(2,1)S(1)} %get-tuple-element.21), channel_id=1, source_target_pairs={{0,7},{1,0},{2,1},{3,2},{4,3},{5,4},{6,5},{7,6},{8,15},{9,8},{10,9... | collective-permute-start | bytes 552968 | tf_op jit(solution)/shard_map/ppermute | solution.py:72
  248.4 17.6 %collective-permute-start.9 = (bf16[256,4,90]{0,2,1:T(8,128)(2,1)S(1)}, bf16[256,4,90]{0,2,1:T(8,128)(2,1)S(1)}, u32[]{:S(2)}, u32[]{:S(2)}) collective-permute-start(bf16[256,4,90]{0,2,1:T(8,128)(2,1)S(1)} %get-tuple-element.22), channel_id=1, source_target_pairs={{0,6},{1,7},{2,0},{3,1},{4,2},{5,3},{6,4},{7,5},{8,14},{9,15},{10,... | collective-permute-start | bytes 552968 | tf_op jit(solution)/shard_map/ppermute | solution.py:72
  249.2 16.8 %collective-permute-start.8 = (bf16[256,4,90]{0,2,1:T(8,128)(2,1)S(1)}, bf16[256,4,90]{0,2,1:T(8,128)(2,1)S(1)}, u32[]{:S(2)}, u32[]{:S(2)}) collective-permute-start(bf16[256,4,90]{0,2,1:T(8,128)(2,1)S(1)} %get-tuple-element.23), channel_id=1, source_target_pairs={{0,5},{1,6},{2,7},{3,0},{4,1},{5,2},{6,3},{7,4},{8,13},{9,14},{10,... | collective-permute-start | bytes 552968 | tf_op jit(solution)/shard_map/ppermute | solution.py:72
  249.7 16.3 %collective-permute-start.7 = (bf16[256,4,90]{0,2,1:T(8,128)(2,1)S(1)}, bf16[256,4,90]{0,2,1:T(8,128)(2,1)S(1)}, u32[]{:S(2)}, u32[]{:S(2)}) collective-permute-start(bf16[256,4,90]{0,2,1:T(8,128)(2,1)S(1)} %get-tuple-element.24), channel_id=1, source_target_pairs={{0,4},{1,5},{2,6},{3,7},{4,0},{5,1},{6,2},{7,3},{8,12},{9,13},{10,... | collective-permute-start | bytes 552968 | tf_op jit(solution)/shard_map/ppermute | solution.py:72
  252.4 13.6 %collective-permute-start.6 = (bf16[256,4,90]{0,2,1:T(8,128)(2,1)S(1)}, bf16[256,4,90]{0,2,1:T(8,128)(2,1)S(1)}, u32[]{:S(2)}, u32[]{:S(2)}) collective-permute-start(bf16[256,4,90]{0,2,1:T(8,128)(2,1)S(1)} %get-tuple-element.25), channel_id=1, source_target_pairs={{0,3},{1,4},{2,5},{3,6},{4,7},{5,0},{6,1},{7,2},{8,11},{9,12},{10,... | collective-permute-start | bytes 552968 | tf_op jit(solution)/shard_map/ppermute | solution.py:72
  253.5 15.3 %collective-permute-start.5 = (bf16[256,4,90]{0,2,1:T(8,128)(2,1)S(1)}, bf16[256,4,90]{0,2,1:T(8,128)(2,1)}, u32[]{:S(2)}, u32[]{:S(2)}) collective-permute-start(bf16[256,4,90]{0,2,1:T(8,128)(2,1)S(1)} %get-tuple-element.26), channel_id=1, source_target_pairs={{0,2},{1,3},{2,4},{3,5},{4,6},{5,7},{6,0},{7,1},{8,10},{9,11},{10,... | collective-permute-start | bytes 552968 | tf_op jit(solution)/shard_map/ppermute | solution.py:72
  266.0 6.4 %collective-permute-start.4 = (bf16[256,4,90]{0,2,1:T(8,128)(2,1)S(1)}, bf16[256,4,90]{0,2,1:T(8,128)(2,1)}, u32[]{:S(2)}, u32[]{:S(2)}) collective-permute-start(bf16[256,4,90]{0,2,1:T(8,128)(2,1)S(1)} %get-tuple-element.20), channel_id=1, source_target_pairs={{0,1},{1,2},{2,3},{3,4},{4,5},{5,6},{6,7},{7,0},{8,9},{9,10},{10,1... | collective-permute-start | bytes 552968 | tf_op jit(solution)/shard_map/ppermute | solution.py:72
Sparse Core Ops, SparseCore 0:
  12.0 93.3 all-gather.3
  162.5 78.2 reduce-scatter.4
  243.3 21.9 reduce-scatter.6

commit v4 on v3

--- a/solution.py
+++ b/solution.py
@@ -137,6 +137,11 @@
         "bkgij,bjkd->bikgd", prob_round, value_blk, preferred_element_type=jnp.float32
     ).astype(jnp.bfloat16)
     attn_rows = attended.reshape(row_count, -1)
+    attn_zx = by_zx(attn_rows, x_peers, z_peers)
+    grad_out_part = jnp.einsum(
+        "tzxi,tc->zxic", attn_zx, grad_out, preferred_element_type=jnp.float32
+    ).astype(jnp.bfloat16)
+    out_over_z = lax.psum_scatter(grad_out_part, "dz", scatter_dimension=0, tiled=True)[0]
     row_delta = jnp.sum(
         dattn_blk.astype(jnp.float32) * attended.astype(jnp.float32), axis=-1
     ).transpose(0, 2, 3, 1)
@@ -181,14 +186,10 @@
     grad_in_part = jnp.einsum(
         "tzxr,tc->zxrc", tokens_zx, grad_qkv, preferred_element_type=jnp.float32
     ).astype(jnp.bfloat16)
-    attn_zx = by_zx(attn_rows, x_peers, z_peers)
-    grad_out_part = jnp.einsum(
-        "tzxi,tc->zxic", attn_zx, grad_out, preferred_element_type=jnp.float32
-    ).astype(jnp.bfloat16)
-    grad_out_part = grad_out_part.reshape(z_peers, x_peers, -1, in_width)
-    both = jnp.concatenate([grad_in_part, grad_out_part], axis=2)
-    over_z = lax.psum_scatter(both, "dz", scatter_dimension=0, tiled=True)[0]
-    over_x = lax.psum_scatter(over_z, "dx", scatter_dimension=0, tiled=True)[0].astype(jnp.float32)
+    in_over_z = lax.psum_scatter(grad_in_part, "dz", scatter_dimension=0, tiled=True)[0]
+    out_over_z = out_over_z.reshape(x_peers, -1, in_width)
+    both = jnp.concatenate([in_over_z, out_over_z], axis=1)
+    over_x = lax.psum_scatter(both, "dx", scatter_dimension=0, tiled=True)[0].astype(jnp.float32)
     in_rows = w_query.shape[0]
     grad_in = over_x[:in_rows]
     grad_w_out = over_x[in_rows:].reshape(w_out.shape)

time: 286 us -> 280 us (0.979); the launches traced: 285 us -> 276 us
  waiting for transfers between devices: 187 us -> 177 us
  other arithmetic: 10.2 us -> 6.81 us
  matrix products: 16.8 us -> 20 us
    reduce_scatter x1 -> x2, waiting for transfers between devices: 78.3 us -> 71 us  [the longest x1 53.9 us: shards(): lax.psum_scatter(grad_in_part, 'dz', scatter_dimension=0, tiled=True)[0]]
    reshape x1 -> x0, local copies, waits for them, and re-layouts: 7.16 us -> none  [shards(): grad_out_part = grad_out_part.reshape(z_peers, x_peers, -1, in_width)]
    ppermute x7, waiting for transfers between devices: 20 us -> 13 us  [scatter_cols_mp(): got = lax.ppermute(piece.astype(jnp.bfloat16), 'mp', pairs)]
    concatenate x1, other arithmetic: 6.22 us -> 2.08 us  [shards(): both = jnp.concatenate([in_over_z, out_over_z], axis=1)]
    another operation x2 -> x3, local copies, waits for them, and re-layouts: 0.13 us -> 3.31 us
    unnamed x22 -> x26, local copies, waits for them, and re-layouts: 5.34 us -> 6.65 us
  transfers between devices with their start and end apart: 14 -> 15, of which waited for: 6 -> 10; matrix products, arithmetic and copies ran while one was open for 13% -> 13% of each run, Pallas kernels for 0% -> 0%
where the time goes in v4:
time: 280 us; the launch traced here: 276 us
  waiting for transfers between devices  177 us (63%)
  local copies, waits for them, and re-layouts  35.9 us (13%)
  starting transfers between devices  21.9 us (8%)
  matrix products  20 us (7%)
  between operations  14.3 us (5%)
  other arithmetic  6.81 us (2%)
    all_gather x1, waiting for transfers between devices, shards(): gathered = lax.all_gather(packed, DP_AXES, axis=0, tiled=False)  90.8 us
    reduce_scatter x1, waiting for transfers between devices, shards(): lax.psum_scatter(grad_in_part, 'dz', scatter_dimension=0, tiled=True)[0]  53.9 us
    reduce_scatter x1, waiting for transfers between devices, shards(): lax.psum_scatter(grad_out_part, 'dz', scatter_dimension=0, tiled=True)[0]  17.1 us
    ppermute x4, starting transfers between devices, passed_along(): return lax.ppermute(array, axis, pairs)  13.8 us
    ppermute x7, waiting for transfers between devices, scatter_cols_mp(): got = lax.ppermute(piece.astype(jnp.bfloat16), 'mp', pairs)  13 us
    ppermute x7, starting transfers between devices, scatter_cols_mp(): got = lax.ppermute(piece.astype(jnp.bfloat16), 'mp', pairs)  7.81 us
    reshape x1, local copies, waits for them, and re-layouts, shards(): full_out = gathered[:, :, in_width:].reshape((-1,) + w_out.shape[1:])  6.99 us
    unnamed x26, local copies, waits for them, and re-layouts  6.65 us
  transfers between devices with their start and end apart: 15, of which 10 were waited for; matrix products, arithmetic and copies ran while one was open for 13% of the time, Pallas kernels for 0%

profile of v4, /device:TPU:2, one launch (start us, length us, event | category | flops | bytes accessed | tf_op | source)
XLA Modules:
  0.0 276.1 jit_solution(4558747894337321354)
XLA Ops:
  7.2 1.2 reshape.317
  8.4 0.8 copy.60
  9.2 0.8 copy.61
  10.1 1.7 concatenate.29
  11.8 2.3 reshape.318
  14.5 90.8 %all-gather.4.cloned.1.call-done = bf16[32,90,1152]{2,1,0:T(8,128)(2,1)} async-done(((bf16[1,90,1152]{2,1,0:T(8,128)(2,1)}), bf16[32,90,1152]{2,1,0:T(8,128)(2,1)}) %all-gather.4.cloned.1.call-update) | async-done | bytes 6635536 | tf_op jit(solution)/shard_map/all_gather | solution.py:97
  105.3 3.5 %fusion.8 = bf16[256,640]{0,1:T(8,128)(2,1)S(1)} fusion(bf16[256,32,90]{0,2,1:T(8,128)(2,1)S(1)} %reshape.318, bf16[32,90,1152]{2,1,0:T(8,128)(2,1)} %all-gather.4.cloned.1.call-done), kind=kOutput, calls=%fused_computation.18 | convolution fusion | flops 943882240 | bytes 5734400 | tf_op jit(solution)/shard_map/tdr,drc->tc/dot_general | solution.py:103
  108.8 2.9 %collective-permute-start = (bf16[128,64]{0,1:T(8,128)(2,1)S(1)}, bf16[128,64]{0,1:T(8,128)(2,1)S(1)}, u32[]{:S(2)}, u32[]{:S(2)}) collective-permute-start(bf16[128,64]{0,1:T(8,128)(2,1)S(1)} %get-tuple-element.28), channel_id=1, source_target_pairs={{0,8},{8,16},{16,24},{24,32},{32,40},{40,48},{48,56},{56,64},{64,7... | collective-permute-start | bytes 49160 | tf_op jit(solution)/shard_map/ppermute | solution.py:21
  111.7 3.0 %collective-permute-start.1 = (bf16[128,64]{0,1:T(8,128)(2,1)S(1)}, bf16[128,64]{0,1:T(8,128)(2,1)S(1)}, u32[]{:S(2)}, u32[]{:S(2)}) collective-permute-start(bf16[128,64]{0,1:T(8,128)(2,1)S(1)} %get-tuple-element.27), channel_id=1, source_target_pairs={{0,8},{8,16},{16,24},{24,32},{32,40},{40,48},{48,56},{56,64},{64,7... | collective-permute-start | bytes 49160 | tf_op jit(solution)/shard_map/ppermute | solution.py:21
  114.8 2.1 slice.154
  116.9 7.0 %reshape.322 = bf16[512,2880]{1,0:T(8,128)(2,1)} reshape(bf16[32,90,512]{2,1,0:T(8,128)(2,1)} %slice.154) | data formatting | bytes 5898240 | tf_op jit(solution)/shard_map/reshape | solution.py:99
  123.9 2.8 %fusion.11 = bf16[256,512]{0,1:T(8,128)(2,1)S(1)} fusion(bf16[512,2880]{1,0:T(8,128)(2,1)} %reshape.322, bf16[256,2880]{0,1:T(8,128)(2,1)S(1)} %copy-done), kind=kOutput, calls=%fused_computation.21 | convolution fusion | flops 755105792 | bytes 4685824 | tf_op jit(solution)/shard_map/dot_general | solution.py:31
  127.9 1.3 copy-done.1
  129.7 2.1 fusion.13
  132.2 2.7 convolution_convert_fusion
  135.0 2.3 reshape.328
  137.3 1.7 reshape.323
  139.0 2.5 fusion.6
  142.6 4.9 %collective-permute-start.2 = (bf16[128,64]{0,1:T(8,128)(2,1)}, bf16[128,64]{0,1:T(8,128)(2,1)}, u32[]{:S(2)}, u32[]{:S(2)}) collective-permute-start(bf16[128,64]{0,1:T(8,128)(2,1)} %get-tuple-element.38), channel_id=1, source_target_pairs={{8,0},{16,8},{24,16},{32,24},{40,32},{48,40},{56,48},{64,56},{72,6... | collective-permute-start | bytes 49160 | tf_op jit(solution)/shard_map/ppermute | solution.py:21
  149.5 1.1 copy.96
  150.6 1.4 reshape.341
  152.0 2.9 %collective-permute-start.3 = (bf16[128,64]{0,1:T(8,128)(2,1)}, bf16[128,64]{0,1:T(8,128)(2,1)S(1)}, u32[]{:S(2)}, u32[]{:S(2)}) collective-permute-start(bf16[128,64]{0,1:T(8,128)(2,1)} %get-tuple-element.40), channel_id=1, source_target_pairs={{8,0},{16,8},{24,16},{32,24},{40,32},{48,40},{56,48},{64,56},{72,6... | collective-permute-start | bytes 49160 | tf_op jit(solution)/shard_map/ppermute | solution.py:21
  154.9 0.7 fusion.46
  155.8 2.2 collective-permute-done.3
  158.0 0.7 pad_maximum_fusion.4
  158.8 3.4 %convert_bitcast_fusion = bf16[8,4,90,640]{3,2,1,0:T(8,128)(2,1)} fusion(bf16[256,64]{1,0:T(8,128)(2,1)S(1)} %copy.80, bf16[256,64]{1,0:T(8,128)(2,1)S(1)} %copy.79, bf16[256,512]{1,0:T(8,128)(2,1)S(1)} %reshape.341, bf16[256,4,8,90]{0,3,2,1:T(8,128)(2,1)S(1)} %reshape.328), kind=kOutput, calls=%fused_computation.1 | convolution fusion | flops 946544640 | bytes 5488640 | tf_op jit(solution)/shard_map/tzxr,tc->zxrc/dot_general | solution.py:186
  162.5 17.1 %reduce-scatter.8.cloned.1.call-done = bf16[1,4,16,2880]{3,2,1,0:T(8,128)(2,1)} async-done(((bf16[8,4,16,2880]{3,2,1,0:T(8,128)(2,1)}), bf16[1,4,16,2880]{3,2,1,0:T(8,128)(2,1)}) %reduce-scatter.8.cloned.1.call-update) | async-done | bytes 368656 | tf_op jit(solution)/shard_map/reduce_scatter | solution.py:144
  179.6 1.5 reshape_squeeze.3
  181.1 53.9 %reduce-scatter.6.cloned.1.call-done = bf16[1,4,90,640]{3,2,1,0:T(8,128)(2,1)} async-done(((bf16[8,4,90,640]{3,2,1,0:T(8,128)(2,1)}), bf16[1,4,90,640]{3,2,1,0:T(8,128)(2,1)}) %reduce-scatter.6.cloned.1.call-update) | async-done | bytes 460816 | tf_op jit(solution)/shard_map/reduce_scatter | solution.py:189
  235.0 2.1 pad_maximum_fusion
  237.2 2.1 slice-done
  239.3 1.4 fusion.38
  240.8 1.6 copy-done.4
  242.6 2.2 collective-permute-start.10
  244.7 1.7 collective-permute-start.6
  246.4 2.7 collective-permute-start.7
  249.2 1.2 collective-permute-start.8
  250.4 2.2 collective-permute-done.4
  252.6 1.2 collective-permute-done.5
  253.7 6.2 %collective-permute-done.6 = bf16[256,4,90]{0,2,1:T(8,128)(2,1)S(1)} collective-permute-done((bf16[256,4,90]{0,2,1:T(8,128)(2,1)S(1)}, bf16[256,4,90]{0,2,1:T(8,128)(2,1)S(1)}, u32[]{:S(2)}, u32[]{:S(2)}) %collective-permute-start.6) | collective-permute-done | bytes 184352 | tf_op jit(solution)/shard_map/ppermute | solution.py:72
  259.9 1.7 collective-permute-done.7
  261.7 1.7 collective-permute-done.9
  263.5 1.4 fusion.20
  264.8 0.7 convert_element_type.198
  265.6 1.0 convert_element_type.202
  267.4 0.7 copy.84
  268.1 0.7 copy.85
  268.8 0.8 mul.65
  (80 shorter events, 7.1 us)
Async XLA Ops:
  7.2 116.8 %copy-start = (bf16[256,2880]{0,1:T(8,128)(2,1)S(1)}, bf16[256,2880]{0,1:T(8,128)(2,1)}, u32[]{:S(2)}) copy-start(bf16[256,2880]{0,1:T(8,128)(2,1)} %param.13) | copy-start | bytes 4423684
  7.2 98.1 %all-gather.4.cloned.1.call-start = ((), (), s32[]{:S(2)}) async-start(), calls=%async_computation.5 | async-start | bytes 7299072 | tf_op jit(solution)/shard_map/all_gather | solution.py:97
  11.7 167.8 %reduce-scatter.8.cloned.1.call-start = ((), (), s32[]{:S(2)}) async-start(), calls=%async_computation.4 | async-start | bytes 3391488 | tf_op jit(solution)/shard_map/reduce_scatter | solution.py:144
  105.3 9.5 %copy-start.3 = (bf16[32,90,1152]{2,1,0:T(8,128)(2,1)S(1)}, bf16[32,90,1152]{2,1,0:T(8,128)(2,1)}, u32[]{:S(2)}) copy-start(bf16[32,90,1152]{2,1,0:T(8,128)(2,1)} %all-gather.4.cloned.1.call-done) | copy-start | bytes 19906564
  108.8 18.4 %collective-permute-start = (bf16[128,64]{0,1:T(8,128)(2,1)S(1)}, bf16[128,64]{0,1:T(8,128)(2,1)S(1)}, u32[]{:S(2)}, u32[]{:S(2)}) collective-permute-start(bf16[128,64]{0,1:T(8,128)(2,1)S(1)} %get-tuple-element.28), channel_id=1, source_target_pairs={{0,8},{8,16},{16,24},{24,32},{32,40},{40,48},{48,56},{56,64},{64,7... | collective-permute-start | bytes 49160 | tf_op jit(solution)/shard_map/ppermute | solution.py:21
  111.7 15.5 %collective-permute-start.1 = (bf16[128,64]{0,1:T(8,128)(2,1)S(1)}, bf16[128,64]{0,1:T(8,128)(2,1)S(1)}, u32[]{:S(2)}, u32[]{:S(2)}) collective-permute-start(bf16[128,64]{0,1:T(8,128)(2,1)S(1)} %get-tuple-element.27), channel_id=1, source_target_pairs={{0,8},{8,16},{16,24},{24,32},{32,40},{40,48},{48,56},{56,64},{64,7... | collective-permute-start | bytes 49160 | tf_op jit(solution)/shard_map/ppermute | solution.py:21
  126.8 1.0 copy-start.6
  126.8 1.0 copy-start.10
  127.3 2.2 copy-start.8
  127.8 1.4 copy-start.1
  134.9 100.1 %reduce-scatter.6.cloned.1.call-start = ((), (), s32[]{:S(2)}) async-start(), calls=%async_computation.3 | async-start | bytes 4423680 | tf_op jit(solution)/shard_map/reduce_scatter | solution.py:189
  139.0 8.5 %copy-start.2 = (f32[2,1,8,128,256]{3,4,2,0,1:T(8,128)S(1)}, f32[2,1,8,128,256]{3,4,2,0,1:T(8,128)}, u32[]{:S(2)}) copy-start(f32[2,1,8,128,256]{3,4,2,0,1:T(8,128)} %copy-done.1) | copy-start | bytes 6291460
  139.0 8.5 %copy-start.5 = (bf16[2,128,8,64]{1,0,3,2:T(2,128)(2,1)S(1)}, bf16[2,128,8,64]{1,0,3,2:T(2,128)(2,1)}, u32[]{:S(2)}) copy-start(bf16[2,128,8,64]{1,0,3,2:T(2,128)(2,1)} %reshape.323) | copy-start | bytes 786436
  141.9 7.3 %copy-start.9 = (bf16[2,128,1,64]{1,3,0,2:T(8,128)(2,1)S(1)}, bf16[2,128,1,64]{1,3,0,2:T(8,128)(2,1)}, u32[]{:S(2)}) copy-start(bf16[2,128,1,64]{1,3,0,2:T(8,128)(2,1)} %copy-done.8) | copy-start | bytes 98308
  142.6 12.3 %collective-permute-start.2 = (bf16[128,64]{0,1:T(8,128)(2,1)}, bf16[128,64]{0,1:T(8,128)(2,1)}, u32[]{:S(2)}, u32[]{:S(2)}) collective-permute-start(bf16[128,64]{0,1:T(8,128)(2,1)} %get-tuple-element.38), channel_id=1, source_target_pairs={{8,0},{16,8},{24,16},{32,24},{40,32},{48,40},{56,48},{64,56},{72,6... | collective-permute-start | bytes 49160 | tf_op jit(solution)/shard_map/ppermute | solution.py:21
  148.0 0.6 copy-start.7
  152.0 6.0 %collective-permute-start.3 = (bf16[128,64]{0,1:T(8,128)(2,1)}, bf16[128,64]{0,1:T(8,128)(2,1)S(1)}, u32[]{:S(2)}, u32[]{:S(2)}) collective-permute-start(bf16[128,64]{0,1:T(8,128)(2,1)} %get-tuple-element.40), channel_id=1, source_target_pairs={{8,0},{16,8},{24,16},{32,24},{40,32},{48,40},{56,48},{64,56},{72,6... | collective-permute-start | bytes 49160 | tf_op jit(solution)/shard_map/ppermute | solution.py:21
  162.3 103.3 %reduce-scatter.10.cloned.1.call-start = ((), (), s32[]{:S(2)}) async-start(), calls=%async_computation.6 | async-start | bytes 1075200
  237.2 2.1 slice-start
  240.8 1.6 copy-start.4
  242.6 6.6 %collective-permute-start.10 = (bf16[256,4,90]{0,2,1:T(8,128)(2,1)S(1)}, bf16[256,4,90]{0,2,1:T(8,128)(2,1)S(1)}, u32[]{:S(2)}, u32[]{:S(2)}) collective-permute-start(bf16[256,4,90]{0,2,1:T(8,128)(2,1)S(1)} %get-tuple-element.21), channel_id=1, source_target_pairs={{0,7},{1,0},{2,1},{3,2},{4,3},{5,4},{6,5},{7,6},{8,15},{9,8},{10,9... | collective-permute-start | bytes 552968 | tf_op jit(solution)/shard_map/ppermute | solution.py:72
  244.7 7.8 %collective-permute-start.4 = (bf16[256,4,90]{0,2,1:T(8,128)(2,1)S(1)}, bf16[256,4,90]{0,2,1:T(8,128)(2,1)S(1)}, u32[]{:S(2)}, u32[]{:S(2)}) collective-permute-start(bf16[256,4,90]{0,2,1:T(8,128)(2,1)S(1)} %get-tuple-element.20), channel_id=1, source_target_pairs={{0,1},{1,2},{2,3},{3,4},{4,5},{5,6},{6,7},{7,0},{8,9},{9,10},{10,1... | collective-permute-start | bytes 552968 | tf_op jit(solution)/shard_map/ppermute | solution.py:72
  244.7 9.0 %collective-permute-start.5 = (bf16[256,4,90]{0,2,1:T(8,128)(2,1)S(1)}, bf16[256,4,90]{0,2,1:T(8,128)(2,1)S(1)}, u32[]{:S(2)}, u32[]{:S(2)}) collective-permute-start(bf16[256,4,90]{0,2,1:T(8,128)(2,1)S(1)} %get-tuple-element.26), channel_id=1, source_target_pairs={{0,2},{1,3},{2,4},{3,5},{4,6},{5,7},{6,0},{7,1},{8,10},{9,11},{10,... | collective-permute-start | bytes 552968 | tf_op jit(solution)/shard_map/ppermute | solution.py:72
  244.7 15.1 %collective-permute-start.6 = (bf16[256,4,90]{0,2,1:T(8,128)(2,1)S(1)}, bf16[256,4,90]{0,2,1:T(8,128)(2,1)S(1)}, u32[]{:S(2)}, u32[]{:S(2)}) collective-permute-start(bf16[256,4,90]{0,2,1:T(8,128)(2,1)S(1)} %get-tuple-element.25), channel_id=1, source_target_pairs={{0,3},{1,4},{2,5},{3,6},{4,7},{5,0},{6,1},{7,2},{8,11},{9,12},{10,... | collective-permute-start | bytes 552968 | tf_op jit(solution)/shard_map/ppermute | solution.py:72
  246.4 15.2 %collective-permute-start.7 = (bf16[256,4,90]{0,2,1:T(8,128)(2,1)S(1)}, bf16[256,4,90]{0,2,1:T(8,128)(2,1)S(1)}, u32[]{:S(2)}, u32[]{:S(2)}) collective-permute-start(bf16[256,4,90]{0,2,1:T(8,128)(2,1)S(1)} %get-tuple-element.24), channel_id=1, source_target_pairs={{0,4},{1,5},{2,6},{3,7},{4,0},{5,1},{6,2},{7,3},{8,12},{9,13},{10,... | collective-permute-start | bytes 552968 | tf_op jit(solution)/shard_map/ppermute | solution.py:72
  249.2 12.5 %collective-permute-start.8 = (bf16[256,4,90]{0,2,1:T(8,128)(2,1)S(1)}, bf16[256,4,90]{0,2,1:T(8,128)(2,1)}, u32[]{:S(2)}, u32[]{:S(2)}) collective-permute-start(bf16[256,4,90]{0,2,1:T(8,128)(2,1)S(1)} %get-tuple-element.23), channel_id=1, source_target_pairs={{0,5},{1,6},{2,7},{3,0},{4,1},{5,2},{6,3},{7,4},{8,13},{9,14},{10,... | collective-permute-start | bytes 552968 | tf_op jit(solution)/shard_map/ppermute | solution.py:72
  252.6 10.9 %collective-permute-start.9 = (bf16[256,4,90]{0,2,1:T(8,128)(2,1)S(1)}, bf16[256,4,90]{0,2,1:T(8,128)(2,1)}, u32[]{:S(2)}, u32[]{:S(2)}) collective-permute-start(bf16[256,4,90]{0,2,1:T(8,128)(2,1)S(1)} %get-tuple-element.22), channel_id=1, source_target_pairs={{0,6},{1,7},{2,0},{3,1},{4,2},{5,3},{6,4},{7,5},{8,14},{9,15},{10,... | collective-permute-start | bytes 552968 | tf_op jit(solution)/shard_map/ppermute | solution.py:72
Sparse Core Ops, SparseCore 0:
  11.9 93.3 all-gather.3
  135.0 44.4 reduce-scatter.7
  182.1 52.8 reduce-scatter.5
  237.4 22.1 reduce-scatter.9

commit v5 on v4

--- a/solution.py
+++ b/solution.py
@@ -96,7 +96,7 @@
     )
     gathered = lax.all_gather(packed, DP_AXES, axis=0, tiled=False)
     in_full = gathered[:, :, :in_width]
-    full_out = gathered[:, :, in_width:].reshape((-1,) + w_out.shape[1:])
+    out_packed = gathered[:, :, in_width:]
     kv_heads = k_cols // DH
     group_size = q_cols // DH // kv_heads
     tokens_blk = rows_of(tokens, (dp_peers,))
@@ -107,7 +107,6 @@
     key_rows = qkv[:, q_cols : q_cols + k_cols]
     value_rows = qkv[:, q_cols + k_cols :]
     rim_keys, rim_values = passed_along((key_rows[-window:], value_rows[-window:]), DP_AXES, 1)
-    grad_attn = contract_cols(grad_out, full_out).astype(jnp.bfloat16)
     first_row = (lax.axis_index("dx") * z_peers + lax.axis_index("dz")) * row_count
     ext_keys = jnp.concatenate([rim_keys, key_rows], axis=0).reshape(
         row_count + window, kv_heads, DH
@@ -118,7 +117,6 @@
     key_blk = paired_blocks(ext_keys, window)
     value_blk = paired_blocks(ext_values, window)
     query_blk = queries.reshape(blocks, window, kv_heads, group_size, DH)
-    dattn_blk = grad_attn.reshape(blocks, window, kv_heads, group_size, DH)
     scores = (
         jnp.einsum("bikgd,bjkd->bkgij", query_blk, key_blk, preferred_element_type=jnp.float32)
         * score_scale
@@ -141,7 +139,11 @@
     grad_out_part = jnp.einsum(
         "tzxi,tc->zxic", attn_zx, grad_out, preferred_element_type=jnp.float32
     ).astype(jnp.bfloat16)
+    out_packed, grad_out_part = lax.optimization_barrier((out_packed, grad_out_part))
     out_over_z = lax.psum_scatter(grad_out_part, "dz", scatter_dimension=0, tiled=True)[0]
+    full_out = out_packed.reshape((-1,) + w_out.shape[1:])
+    grad_attn = contract_cols(grad_out, full_out).astype(jnp.bfloat16)
+    dattn_blk = grad_attn.reshape(blocks, window, kv_heads, group_size, DH)
     row_delta = jnp.sum(
         dattn_blk.astype(jnp.float32) * attended.astype(jnp.float32), axis=-1
     ).transpose(0, 2, 3, 1)
@@ -186,6 +188,7 @@
     grad_in_part = jnp.einsum(
         "tzxr,tc->zxrc", tokens_zx, grad_qkv, preferred_element_type=jnp.float32
     ).astype(jnp.bfloat16)
+    grad_tokens, grad_in_part = lax.optimization_barrier((grad_tokens, grad_in_part))
     in_over_z = lax.psum_scatter(grad_in_part, "dz", scatter_dimension=0, tiled=True)[0]
     out_over_z = out_over_z.reshape(x_peers, -1, in_width)
     both = jnp.concatenate([in_over_z, out_over_z], axis=1)

time: 280 us -> 279 us (level)
    unnamed x5, waiting for transfers between devices: 0.07 us -> 22.6 us
    reduce_scatter x1, waiting for transfers between devices: 17.1 us -> 0.02 us  [shards(): lax.psum_scatter(grad_out_part, 'dz', scatter_dimension=0, tiled=True)[0]]
    reduce_scatter x1, waiting for transfers between devices: 53.9 us -> 47.3 us  [shards(): lax.psum_scatter(grad_in_part, 'dz', scatter_dimension=0, tiled=True)[0]]
    unnamed x26 -> x14, local copies, waits for them, and re-layouts: 6.65 us -> 6.1 us
  transfers between devices with their start and end apart: 15 -> 15, of which waited for: 10 -> 10; matrix products, arithmetic and copies ran while one was open for 13% -> 15% of each run, Pallas kernels for 0% -> 0%
where the time goes in v5:
time: 279 us; the launch traced here: 276 us
  waiting for transfers between devices  178 us (64%)
  local copies, waits for them, and re-layouts  35.7 us (13%)
  matrix products  21.7 us (8%)
  starting transfers between devices  19.9 us (7%)
  between operations  14.3 us (5%)
  other arithmetic  5.74 us (2%)
    all_gather x1, waiting for transfers between devices, shards(): gathered = lax.all_gather(packed, DP_AXES, axis=0, tiled=False)  90.8 us
    reduce_scatter x1, waiting for transfers between devices, shards(): lax.psum_scatter(grad_in_part, 'dz', scatter_dimension=0, tiled=True)[0]  47.3 us
    unnamed x5, waiting for transfers between devices  22.6 us
    ppermute x7, waiting for transfers between devices, scatter_cols_mp(): got = lax.ppermute(piece.astype(jnp.bfloat16), 'mp', pairs)  15 us
    ppermute x4, starting transfers between devices, passed_along(): return lax.ppermute(array, axis, pairs)  13.2 us
    reshape x1, local copies, waits for them, and re-layouts, shards(): full_out = out_packed.reshape((-1,) + w_out.shape[1:])  7.04 us
    ppermute x7, starting transfers between devices, scatter_cols_mp(): got = lax.ppermute(piece.astype(jnp.bfloat16), 'mp', pairs)  6.54 us
    unnamed x14, local copies, waits for them, and re-layouts  6.1 us
  transfers between devices with their start and end apart: 15, of which 10 were waited for; matrix products, arithmetic and copies ran while one was open for 15% of the time, Pallas kernels for 0%

profile of v5, /device:TPU:2, one launch (start us, length us, event | category | flops | bytes accessed | tf_op | source)
XLA Modules:
  0.0 275.8 jit_solution(3184600061365099475)
XLA Ops:
  7.2 0.9 copy.59
  8.2 0.8 copy.60
  9.0 1.1 reshape.317
  10.1 1.7 concatenate.29
  11.8 2.3 reshape.318
  14.5 90.8 %all-gather.4.cloned.1.call-done = bf16[32,90,1152]{2,1,0:T(8,128)(2,1)} async-done(((bf16[1,90,1152]{2,1,0:T(8,128)(2,1)}), bf16[32,90,1152]{2,1,0:T(8,128)(2,1)}) %all-gather.4.cloned.1.call-update) | async-done | bytes 6635536 | tf_op jit(solution)/shard_map/all_gather | solution.py:97
  105.3 3.3 %fusion.8 = bf16[256,640]{0,1:T(8,128)(2,1)S(1)} fusion(bf16[256,32,90]{0,2,1:T(8,128)(2,1)S(1)} %reshape.318, bf16[32,90,1152]{2,1,0:T(8,128)(2,1)} %all-gather.4.cloned.1.call-done), kind=kOutput, calls=%fused_computation.18 | convolution fusion | flops 943882240 | bytes 5734400 | tf_op jit(solution)/shard_map/tdr,drc->tc/dot_general | solution.py:103
  108.7 2.9 %collective-permute-start.1 = (bf16[128,64]{0,1:T(8,128)(2,1)S(1)}, bf16[128,64]{0,1:T(8,128)(2,1)S(1)}, u32[]{:S(2)}, u32[]{:S(2)}) collective-permute-start(bf16[128,64]{0,1:T(8,128)(2,1)S(1)} %get-tuple-element.35), channel_id=1, source_target_pairs={{0,8},{8,16},{16,24},{24,32},{32,40},{40,48},{48,56},{56,64},{64,7... | collective-permute-start | bytes 49160 | tf_op jit(solution)/shard_map/ppermute | solution.py:21
  111.6 3.0 %collective-permute-start = (bf16[128,64]{0,1:T(8,128)(2,1)S(1)}, bf16[128,64]{0,1:T(8,128)(2,1)S(1)}, u32[]{:S(2)}, u32[]{:S(2)}) collective-permute-start(bf16[128,64]{0,1:T(8,128)(2,1)S(1)} %get-tuple-element.36), channel_id=1, source_target_pairs={{0,8},{8,16},{16,24},{24,32},{32,40},{40,48},{48,56},{56,64},{64,7... | collective-permute-start | bytes 49160 | tf_op jit(solution)/shard_map/ppermute | solution.py:21
  114.8 4.0 %slice.154 = bf16[32,90,512]{2,1,0:T(8,128)(2,1)} slice(bf16[32,90,1152]{2,1,0:T(8,128)(2,1)} %all-gather.4.cloned.1.call-done), slice={[0:32], [0:90], [640:1152]} | slice | bytes 5898240 | tf_op jit(solution)/shard_map/slice | solution.py:99
  118.8 0.5 collective-permute-done
  119.4 0.5 fusion.63
  120.0 1.3 copy-done.1
  121.7 2.0 fusion.9
  124.2 2.6 convolution_convert_fusion
  126.9 4.5 %slice.148 = bf16[32,90,640]{2,1,0:T(8,128)(2,1)} slice(bf16[32,90,1152]{2,1,0:T(8,128)(2,1)} %all-gather.4.cloned.1.call-done), slice={[0:32], [0:90], [0:640]} | slice | bytes 7372800 | tf_op jit(solution)/shard_map/slice | solution.py:98
  131.4 7.0 %reshape.323 = bf16[512,2880]{1,0:T(8,128)(2,1)} reshape(bf16[32,90,512]{2,1,0:T(8,128)(2,1)} %slice.154) | data formatting | bytes 5898240 | tf_op jit(solution)/shard_map/reshape | solution.py:144
  138.4 2.8 %fusion.11 = bf16[256,512]{0,1:T(8,128)(2,1)S(1)} fusion(bf16[512,2880]{1,0:T(8,128)(2,1)} %reshape.323, bf16[256,2880]{0,1:T(8,128)(2,1)S(1)} %copy-done), kind=kOutput, calls=%fused_computation.21 | convolution fusion | flops 755105792 | bytes 4685824 | tf_op jit(solution)/shard_map/dot_general | solution.py:31
  141.6 2.2 convolution_bitcast_fusion.1
  143.8 4.3 %collective-permute-start.3 = (bf16[128,64]{0,1:T(8,128)(2,1)S(1)}, bf16[128,64]{0,1:T(8,128)(2,1)S(1)}, u32[]{:S(2)}, u32[]{:S(2)}) collective-permute-start(bf16[128,64]{0,1:T(8,128)(2,1)S(1)} %get-tuple-element.48), channel_id=1, source_target_pairs={{8,0},{16,8},{24,16},{32,24},{40,32},{48,40},{56,48},{64,56},{72,6... | collective-permute-start | bytes 49160 | tf_op jit(solution)/shard_map/ppermute | solution.py:21
  148.3 0.6 fusion.6
  148.9 0.4 convolution_bitcast_fusion.2
  149.7 2.9 %collective-permute-start.2 = (bf16[128,64]{0,1:T(8,128)(2,1)S(1)}, bf16[128,64]{0,1:T(8,128)(2,1)S(1)}, u32[]{:S(2)}, u32[]{:S(2)}) collective-permute-start(bf16[128,64]{0,1:T(8,128)(2,1)S(1)} %get-tuple-element.46), channel_id=1, source_target_pairs={{8,0},{16,8},{24,16},{32,24},{40,32},{48,40},{56,48},{64,56},{72,6... | collective-permute-start | bytes 49160 | tf_op jit(solution)/shard_map/ppermute | solution.py:21
  153.5 2.1 collective-permute-done.2
  155.7 3.6 %fusion.38 = f32[256,8,4,90]{0,3,2,1:T(8,128)S(1)} fusion(bf16[8,4,90,640]{3,2,1,0:T(8,128)(2,1)} %bitcast.192, bf16[256,64]{1,0:T(8,128)(2,1)S(1)} %copy.81, bf16[256,64]{1,0:T(8,128)(2,1)S(1)} %copy.80, bf16[256,512]{1,0:T(8,128)(2,1)S(1)} %reshape.341), kind=kOutput, calls=%fused_computation.63 | convolution fusion | flops 944701440 | bytes 6963200 | tf_op jit(solution)/shard_map/tc,mjrc->tmjr/dot_general | solution.py:183
  159.4 1.7 copy-done.3
  161.0 1.1 fusion.31
  162.1 2.8 %collective-permute-start.9 = (bf16[256,4,90]{0,2,1:T(8,128)(2,1)}, bf16[256,4,90]{0,2,1:T(8,128)(2,1)}, u32[]{:S(2)}, u32[]{:S(2)}) collective-permute-start(bf16[256,4,90]{0,2,1:T(8,128)(2,1)} %get-tuple-element.30), channel_id=1, source_target_pairs={{0,6},{1,7},{2,0},{3,1},{4,2},{5,3},{6,4},{7,5},{8,14},{9,15},{10,... | collective-permute-start | bytes 552968 | tf_op jit(solution)/shard_map/ppermute | solution.py:72
  164.9 2.3 reshape.328
  167.2 0.5 collective-permute-start.8
  167.8 2.8 %collective-permute-start.7 = (bf16[256,4,90]{0,2,1:T(8,128)(2,1)}, bf16[256,4,90]{0,2,1:T(8,128)(2,1)}, u32[]{:S(2)}, u32[]{:S(2)}) collective-permute-start(bf16[256,4,90]{0,2,1:T(8,128)(2,1)} %get-tuple-element.32), channel_id=1, source_target_pairs={{0,4},{1,5},{2,6},{3,7},{4,0},{5,1},{6,2},{7,3},{8,12},{9,13},{10,... | collective-permute-start | bytes 552968 | tf_op jit(solution)/shard_map/ppermute | solution.py:72
  170.6 0.4 collective-permute-start.5
  171.0 1.7 collective-permute-done.9
  172.6 3.3 %convert_bitcast_fusion = bf16[8,4,90,640]{3,2,1,0:T(8,128)(2,1)} fusion(bf16[256,64]{1,0:T(8,128)(2,1)S(1)} %copy.81, bf16[256,64]{1,0:T(8,128)(2,1)S(1)} %copy.80, bf16[256,512]{1,0:T(8,128)(2,1)S(1)} %reshape.341, bf16[256,4,8,90]{0,3,2,1:T(8,128)(2,1)S(1)} %reshape.328), kind=kOutput, calls=%fused_computation.1 | convolution fusion | flops 946544640 | bytes 5488640 | tf_op jit(solution)/shard_map/tzxr,tc->zxrc/dot_general | solution.py:188
  175.9 4.9 %collective-permute-done.7 = bf16[256,4,90]{0,2,1:T(8,128)(2,1)} collective-permute-done((bf16[256,4,90]{0,2,1:T(8,128)(2,1)}, bf16[256,4,90]{0,2,1:T(8,128)(2,1)}, u32[]{:S(2)}, u32[]{:S(2)}) %collective-permute-start.7) | collective-permute-done | bytes 184352 | tf_op jit(solution)/shard_map/ppermute | solution.py:72
  180.8 1.0 collective-permute-done.6
  181.7 7.4 %collective-permute-done.5 = bf16[256,4,90]{0,2,1:T(8,128)(2,1)} collective-permute-done((bf16[256,4,90]{0,2,1:T(8,128)(2,1)}, bf16[256,4,90]{0,2,1:T(8,128)(2,1)}, u32[]{:S(2)}, u32[]{:S(2)}) %collective-permute-start.5) | collective-permute-done | bytes 184352 | tf_op jit(solution)/shard_map/ppermute | solution.py:72
  189.3 1.7 fusion.20
  191.0 0.7 convert_element_type.199
  191.8 1.5 reshape_squeeze.3
  193.3 47.3 %reduce-scatter.6.cloned.1.call-done = bf16[1,4,90,640]{3,2,1,0:T(8,128)(2,1)} async-done(((bf16[8,4,90,640]{3,2,1,0:T(8,128)(2,1)}), bf16[1,4,90,640]{3,2,1,0:T(8,128)(2,1)}) %reduce-scatter.6.cloned.1.call-update) | async-done | bytes 460816 | tf_op jit(solution)/shard_map/reduce_scatter | solution.py:192
  240.6 2.0 pad_maximum_fusion
  242.7 22.6 %reduce-scatter.10.cloned.1.call-done = bf16[1,162,640]{2,1,0:T(8,128)(2,1)} async-done(((bf16[4,162,640]{2,1,0:T(8,128)(2,1)}), bf16[1,162,640]{2,1,0:T(8,128)(2,1)}) %reduce-scatter.10.cloned.1.call-update) | async-done | bytes 207376
  265.3 1.0 convert_element_type.202
  266.3 0.7 slice.168
  267.1 0.7 copy.83
  267.8 0.7 copy.84
  268.5 0.8 mul.65
  (68 shorter events, 3.6 us)
Async XLA Ops:
  7.2 117.0 %copy-start = (bf16[256,2880]{0,1:T(8,128)(2,1)S(1)}, bf16[256,2880]{0,1:T(8,128)(2,1)}, u32[]{:S(2)}) copy-start(bf16[256,2880]{0,1:T(8,128)(2,1)} %param.13) | copy-start | bytes 4423684
  7.2 98.1 %all-gather.4.cloned.1.call-start = ((), (), s32[]{:S(2)}) async-start(), calls=%async_computation.5 | async-start | bytes 7299072 | tf_op jit(solution)/shard_map/all_gather | solution.py:97
  11.8 180.1 %reduce-scatter.8.cloned.1.call-start = ((), (), s32[]{:S(2)}) async-start(), calls=%async_computation.4 | async-start | bytes 3391488 | tf_op jit(solution)/shard_map/reduce_scatter | solution.py:143
  108.7 10.1 %collective-permute-start.1 = (bf16[128,64]{0,1:T(8,128)(2,1)S(1)}, bf16[128,64]{0,1:T(8,128)(2,1)S(1)}, u32[]{:S(2)}, u32[]{:S(2)}) collective-permute-start(bf16[128,64]{0,1:T(8,128)(2,1)S(1)} %get-tuple-element.35), channel_id=1, source_target_pairs={{0,8},{8,16},{16,24},{24,32},{32,40},{40,48},{48,56},{56,64},{64,7... | collective-permute-start | bytes 49160 | tf_op jit(solution)/shard_map/ppermute | solution.py:21
  111.6 7.7 %collective-permute-start = (bf16[128,64]{0,1:T(8,128)(2,1)S(1)}, bf16[128,64]{0,1:T(8,128)(2,1)S(1)}, u32[]{:S(2)}, u32[]{:S(2)}) collective-permute-start(bf16[128,64]{0,1:T(8,128)(2,1)S(1)} %get-tuple-element.36), channel_id=1, source_target_pairs={{0,8},{8,16},{16,24},{24,32},{32,40},{40,48},{48,56},{56,64},{64,7... | collective-permute-start | bytes 49160 | tf_op jit(solution)/shard_map/ppermute | solution.py:21
  118.8 1.1 copy-start.4
  119.9 1.3 copy-start.1
  126.8 113.8 %reduce-scatter.6.cloned.1.call-start = ((), (), s32[]{:S(2)}) async-start(), calls=%async_computation.3 | async-start | bytes 4423680 | tf_op jit(solution)/shard_map/reduce_scatter | solution.py:192
  141.6 6.7 %copy-start.2 = (f32[2,1,8,128,256]{3,4,2,0,1:T(8,128)S(1)}, f32[2,1,8,128,256]{3,4,2,0,1:T(8,128)}, u32[]{:S(2)}) copy-start(f32[2,1,8,128,256]{3,4,2,0,1:T(8,128)} %copy-done.1) | copy-start | bytes 6291460
  143.8 9.5 %collective-permute-start.3 = (bf16[128,64]{0,1:T(8,128)(2,1)S(1)}, bf16[128,64]{0,1:T(8,128)(2,1)S(1)}, u32[]{:S(2)}, u32[]{:S(2)}) collective-permute-start(bf16[128,64]{0,1:T(8,128)(2,1)S(1)} %get-tuple-element.48), channel_id=1, source_target_pairs={{8,0},{16,8},{24,16},{32,24},{40,32},{48,40},{56,48},{64,56},{72,6... | collective-permute-start | bytes 49160 | tf_op jit(solution)/shard_map/ppermute | solution.py:21
  149.7 5.9 %collective-permute-start.2 = (bf16[128,64]{0,1:T(8,128)(2,1)S(1)}, bf16[128,64]{0,1:T(8,128)(2,1)S(1)}, u32[]{:S(2)}, u32[]{:S(2)}) collective-permute-start(bf16[128,64]{0,1:T(8,128)(2,1)S(1)} %get-tuple-element.46), channel_id=1, source_target_pairs={{8,0},{16,8},{24,16},{32,24},{40,32},{48,40},{56,48},{64,56},{72,6... | collective-permute-start | bytes 49160 | tf_op jit(solution)/shard_map/ppermute | solution.py:21
  159.3 1.7 copy-start.3
  162.1 8.5 %collective-permute-start.10 = (bf16[256,4,90]{0,2,1:T(8,128)(2,1)}, bf16[256,4,90]{0,2,1:T(8,128)(2,1)}, u32[]{:S(2)}, u32[]{:S(2)}) collective-permute-start(bf16[256,4,90]{0,2,1:T(8,128)(2,1)} %get-tuple-element.29), channel_id=1, source_target_pairs={{0,7},{1,0},{2,1},{3,2},{4,3},{5,4},{6,5},{7,6},{8,15},{9,8},{10,9... | collective-permute-start | bytes 552968 | tf_op jit(solution)/shard_map/ppermute | solution.py:72
  162.1 10.5 %collective-permute-start.9 = (bf16[256,4,90]{0,2,1:T(8,128)(2,1)}, bf16[256,4,90]{0,2,1:T(8,128)(2,1)}, u32[]{:S(2)}, u32[]{:S(2)}) collective-permute-start(bf16[256,4,90]{0,2,1:T(8,128)(2,1)} %get-tuple-element.30), channel_id=1, source_target_pairs={{0,6},{1,7},{2,0},{3,1},{4,2},{5,3},{6,4},{7,5},{8,14},{9,15},{10,... | collective-permute-start | bytes 552968 | tf_op jit(solution)/shard_map/ppermute | solution.py:72
  167.2 8.7 %collective-permute-start.8 = (bf16[256,4,90]{0,2,1:T(8,128)(2,1)}, bf16[256,4,90]{0,2,1:T(8,128)(2,1)}, u32[]{:S(2)}, u32[]{:S(2)}) collective-permute-start(bf16[256,4,90]{0,2,1:T(8,128)(2,1)} %get-tuple-element.31), channel_id=1, source_target_pairs={{0,5},{1,6},{2,7},{3,0},{4,1},{5,2},{6,3},{7,4},{8,13},{9,14},{10,... | collective-permute-start | bytes 552968 | tf_op jit(solution)/shard_map/ppermute | solution.py:72
  167.8 13.0 %collective-permute-start.7 = (bf16[256,4,90]{0,2,1:T(8,128)(2,1)}, bf16[256,4,90]{0,2,1:T(8,128)(2,1)}, u32[]{:S(2)}, u32[]{:S(2)}) collective-permute-start(bf16[256,4,90]{0,2,1:T(8,128)(2,1)} %get-tuple-element.32), channel_id=1, source_target_pairs={{0,4},{1,5},{2,6},{3,7},{4,0},{5,1},{6,2},{7,3},{8,12},{9,13},{10,... | collective-permute-start | bytes 552968 | tf_op jit(solution)/shard_map/ppermute | solution.py:72
  170.6 11.2 %collective-permute-start.6 = (bf16[256,4,90]{0,2,1:T(8,128)(2,1)}, bf16[256,4,90]{0,2,1:T(8,128)(2,1)}, u32[]{:S(2)}, u32[]{:S(2)}) collective-permute-start(bf16[256,4,90]{0,2,1:T(8,128)(2,1)} %get-tuple-element.33), channel_id=1, source_target_pairs={{0,3},{1,4},{2,5},{3,6},{4,7},{5,0},{6,1},{7,2},{8,11},{9,12},{10,... | collective-permute-start | bytes 552968 | tf_op jit(solution)/shard_map/ppermute | solution.py:72
  170.6 18.6 %collective-permute-start.5 = (bf16[256,4,90]{0,2,1:T(8,128)(2,1)}, bf16[256,4,90]{0,2,1:T(8,128)(2,1)}, u32[]{:S(2)}, u32[]{:S(2)}) collective-permute-start(bf16[256,4,90]{0,2,1:T(8,128)(2,1)} %get-tuple-element.34), channel_id=1, source_target_pairs={{0,2},{1,3},{2,4},{3,5},{4,6},{5,7},{6,0},{7,1},{8,10},{9,11},{10,... | collective-permute-start | bytes 552968 | tf_op jit(solution)/shard_map/ppermute | solution.py:72
  172.6 16.6 %collective-permute-start.4 = (bf16[256,4,90]{0,2,1:T(8,128)(2,1)}, bf16[256,4,90]{0,2,1:T(8,128)(2,1)}, u32[]{:S(2)}, u32[]{:S(2)}) collective-permute-start(bf16[256,4,90]{0,2,1:T(8,128)(2,1)} %get-tuple-element.28), channel_id=1, source_target_pairs={{0,1},{1,2},{2,3},{3,4},{4,5},{5,6},{6,7},{7,0},{8,9},{9,10},{10,1... | collective-permute-start | bytes 552968 | tf_op jit(solution)/shard_map/ppermute | solution.py:72
  191.8 73.5 %reduce-scatter.10.cloned.1.call-start = ((), (), s32[]{:S(2)}) async-start(), calls=%async_computation.6 | async-start | bytes 1075200
Sparse Core Ops, SparseCore 0:
  11.9 93.3 all-gather.3
  126.9 44.1 reduce-scatter.7
  191.9 48.6 reduce-scatter.5
  243.0 22.1 reduce-scatter.9

commit v6 on v5

--- a/solution.py
+++ b/solution.py
@@ -13,6 +13,7 @@
 masked_score = -1e30
 DP_AXES = ("dx", "dz")
 LANES = 128
+CORES = 2
 
 
 def passed_along(array, axis, by):
@@ -61,17 +62,27 @@
     return array.reshape(array.shape[:1] + lead + (-1,))
 
 
-def scatter_cols_mp(terms):
+def scatter_cols_mp(terms, cores):
     peers = lax.axis_size("mp")
+    chips = peers // cores
     me = lax.axis_index("mp")
-    total = lax.dynamic_index_in_dim(terms, me, axis=1, keepdims=False)
-    for shift in range(1, peers):
-        dest = (me + shift) % peers
-        piece = lax.dynamic_index_in_dim(terms, dest, axis=1, keepdims=False)
-        pairs = [(i, (i + shift) % peers) for i in range(peers)]
+    my_chip, my_core = me // cores, me % cores
+    by_core = terms.reshape((terms.shape[0], chips, cores) + terms.shape[2:])
+    total = lax.dynamic_index_in_dim(by_core, my_core, axis=2, keepdims=False).astype(jnp.float32)
+    for shift in range(1, cores):
+        dest = (my_core + shift) % cores
+        piece = lax.dynamic_index_in_dim(by_core, dest, axis=2, keepdims=False)
+        pairs = [(k, k - k % cores + (k % cores + shift) % cores) for k in range(peers)]
         got = lax.ppermute(piece.astype(jnp.bfloat16), "mp", pairs)
         total = total + got.astype(jnp.float32)
-    return total.reshape(total.shape[0], -1).astype(jnp.bfloat16)
+    result = lax.dynamic_index_in_dim(total, my_chip, axis=1, keepdims=False)
+    for shift in range(1, chips):
+        dest = (my_chip + shift) % chips
+        piece = lax.dynamic_index_in_dim(total, dest, axis=1, keepdims=False)
+        pairs = [(k, ((k // cores + shift) % chips) * cores + k % cores) for k in range(peers)]
+        got = lax.ppermute(piece.astype(jnp.bfloat16), "mp", pairs)
+        result = result + got.astype(jnp.float32)
+    return result.reshape(result.shape[0], -1).astype(jnp.bfloat16)
 
 
 def by_zx(rows, x_peers, z_peers):
@@ -96,7 +107,6 @@
     )
     gathered = lax.all_gather(packed, DP_AXES, axis=0, tiled=False)
     in_full = gathered[:, :, :in_width]
-    out_packed = gathered[:, :, in_width:]
     kv_heads = k_cols // DH
     group_size = q_cols // DH // kv_heads
     tokens_blk = rows_of(tokens, (dp_peers,))
@@ -139,9 +149,9 @@
     grad_out_part = jnp.einsum(
         "tzxi,tc->zxic", attn_zx, grad_out, preferred_element_type=jnp.float32
     ).astype(jnp.bfloat16)
-    out_packed, grad_out_part = lax.optimization_barrier((out_packed, grad_out_part))
+    late_gathered, grad_out_part = lax.optimization_barrier((gathered, grad_out_part))
     out_over_z = lax.psum_scatter(grad_out_part, "dz", scatter_dimension=0, tiled=True)[0]
-    full_out = out_packed.reshape((-1,) + w_out.shape[1:])
+    full_out = late_gathered[:, :, in_width:].reshape((-1,) + w_out.shape[1:])
     grad_attn = contract_cols(grad_out, full_out).astype(jnp.bfloat16)
     dattn_blk = grad_attn.reshape(blocks, window, kv_heads, group_size, DH)
     row_delta = jnp.sum(
@@ -179,11 +189,12 @@
         [own_values[:-window], own_values[-window:] + back_values], axis=0
     ).astype(jnp.bfloat16)
     grad_qkv = jnp.concatenate([grad_queries, grad_keys, grad_values], axis=1)
-    proj_by_mp = in_full.reshape((mp_peers, -1) + in_full.shape[1:])
+    grad_wide = jnp.pad(grad_qkv, ((0, 0), (0, gathered.shape[2] - in_width)))
+    proj_by_mp = late_gathered.reshape((mp_peers, -1) + gathered.shape[1:])
     token_terms = jnp.einsum(
-        "tc,mjrc->tmjr", grad_qkv, proj_by_mp, preferred_element_type=jnp.float32
-    )
-    grad_tokens = scatter_cols_mp(token_terms)
+        "tc,mjrc->tmjr", grad_wide, proj_by_mp, preferred_element_type=jnp.float32
+    )
+    grad_tokens = scatter_cols_mp(token_terms, CORES)
     tokens_zx = by_zx(tokens, x_peers, z_peers)
     grad_in_part = jnp.einsum(
         "tzxr,tc->zxrc", tokens_zx, grad_qkv, preferred_element_type=jnp.float32

time: 279 us -> 271 us (0.971)
  waiting for transfers between devices: 178 us -> 174 us
  starting transfers between devices: 19.9 us -> 16.9 us
    ppermute x7 -> x4, waiting for transfers between devices: 15 us -> 5.22 us  [scatter_cols_mp(): got = lax.ppermute(piece.astype(jnp.bfloat16), 'mp', pairs)]
    slice x2 -> x1, local copies, waits for them, and re-layouts: 8.41 us -> 3.92 us  [shards(): full_out = late_gathered[:, :, in_width:].reshape((-1,) + w_out.shape[1:])]
    ppermute x4, waiting for transfers between devices: 2.67 us -> 6.79 us  [passed_along(): return lax.ppermute(array, axis, pairs)]
    ppermute x7 -> x4, starting transfers between devices: 6.54 us -> 5.07 us  [scatter_cols_mp(): got = lax.ppermute(piece.astype(jnp.bfloat16), 'mp', pairs)]
    unnamed x14 -> x16, local copies, waits for them, and re-layouts: 6.1 us -> 4.7 us
  transfers between devices with their start and end apart: 15 -> 12, of which waited for: 10 -> 9; matrix products, arithmetic and copies ran while one was open for 15% -> 16% of each run, Pallas kernels for 0% -> 0%
where the time goes in v6:
time: 271 us; the launch traced here: 268 us
  waiting for transfers between devices  174 us (64%)
  local copies, waits for them, and re-layouts  33.1 us (12%)
  matrix products  21.9 us (8%)
  starting transfers between devices  16.9 us (6%)
  between operations  14.3 us (5%)
  other arithmetic  7.81 us (3%)
    all_gather x1, waiting for transfers between devices, shards(): gathered = lax.all_gather(packed, DP_AXES, axis=0, tiled=False)  90.8 us
    reduce_scatter x1, waiting for transfers between devices, shards(): lax.psum_scatter(grad_in_part, 'dz', scatter_dimension=0, tiled=True)[0]  48.3 us
    unnamed x5, waiting for transfers between devices  22.7 us
    ppermute x4, starting transfers between devices, passed_along(): return lax.ppermute(array, axis, pairs)  11.6 us
    reshape x1, local copies, waits for them, and re-layouts, shards(): full_out = late_gathered[:, :, in_width:].reshape((-1,) + w_out.shape[1:])  7.03 us
    ppermute x4, waiting for transfers between devices, passed_along(): return lax.ppermute(array, axis, pairs)  6.79 us
  transfers between devices with their start and end apart: 12, of which 9 were waited for; matrix products, arithmetic and copies ran while one was open for 16% of the time, Pallas kernels for 0%

profile of v6, /device:TPU:2, one launch (start us, length us, event | category | flops | bytes accessed | tf_op | source)
XLA Modules:
  0.0 267.7 jit_solution(10553724111205392851)
XLA Ops:
  7.2 0.9 copy.87
  8.2 0.8 copy.88
  9.0 1.1 reshape.315
  10.1 1.7 concatenate.29
  11.8 2.3 reshape.316
  14.6 90.8 %all-gather.4.cloned.1.call-done = bf16[32,90,1152]{2,1,0:T(8,128)(2,1)} async-done(((bf16[1,90,1152]{2,1,0:T(8,128)(2,1)}), bf16[32,90,1152]{2,1,0:T(8,128)(2,1)}) %all-gather.4.cloned.1.call-update) | async-done | bytes 6635536 | tf_op jit(solution)/shard_map/all_gather | solution.py:108
  105.3 3.3 %fusion.15 = bf16[256,640]{0,1:T(8,128)(2,1)S(1)} fusion(bf16[256,32,90]{0,2,1:T(8,128)(2,1)S(1)} %reshape.316, bf16[32,90,1152]{2,1,0:T(8,128)(2,1)} %all-gather.4.cloned.1.call-done), kind=kOutput, calls=%fused_computation.22 | convolution fusion | flops 943882240 | bytes 5734400 | tf_op jit(solution)/shard_map/tdr,drc->tc/dot_general | solution.py:113
  108.7 2.9 %collective-permute-start.1 = (bf16[128,64]{0,1:T(8,128)(2,1)S(1)}, bf16[128,64]{0,1:T(8,128)(2,1)S(1)}, u32[]{:S(2)}, u32[]{:S(2)}) collective-permute-start(bf16[128,64]{0,1:T(8,128)(2,1)S(1)} %get-tuple-element.36), channel_id=1, source_target_pairs={{0,8},{8,16},{16,24},{24,32},{32,40},{40,48},{48,56},{56,64},{64,7... | collective-permute-start | bytes 49160 | tf_op jit(solution)/shard_map/ppermute | solution.py:22
  111.6 3.0 %collective-permute-start = (bf16[128,64]{0,1:T(8,128)(2,1)S(1)}, bf16[128,64]{0,1:T(8,128)(2,1)S(1)}, u32[]{:S(2)}, u32[]{:S(2)}) collective-permute-start(bf16[128,64]{0,1:T(8,128)(2,1)S(1)} %get-tuple-element.37), channel_id=1, source_target_pairs={{0,8},{8,16},{16,24},{24,32},{32,40},{40,48},{48,56},{56,64},{64,7... | collective-permute-start | bytes 49160 | tf_op jit(solution)/shard_map/ppermute | solution.py:22
  114.9 1.6 collective-permute-done.1
  116.4 2.9 %collective-permute-done = bf16[128,64]{0,1:T(8,128)(2,1)S(1)} collective-permute-done((bf16[128,64]{0,1:T(8,128)(2,1)S(1)}, bf16[128,64]{0,1:T(8,128)(2,1)S(1)}, u32[]{:S(2)}, u32[]{:S(2)}) %collective-permute-start) | collective-permute-done | bytes 16416 | tf_op jit(solution)/shard_map/ppermute | solution.py:22
  119.4 0.5 fusion.66
  120.4 0.5 fusion.18
  120.9 0.4 copy-done.1
  121.7 2.7 %convolution_convert_fusion = bf16[8,4,16,2880]{3,2,1,0:T(8,128)(2,1)} fusion(bf16[256,2880]{0,1:T(8,128)(2,1)S(1)} %copy-done, bf16[256,4,8,16]{0,3,2,1:T(8,128)(2,1)S(1)} %reshape_reshape.2), kind=kOutput, calls=%fused_computation | convolution fusion | flops 756449280 | bytes 4685824 | tf_op jit(solution)/shard_map/tzxi,tc->zxic/dot_general | solution.py:149
  124.5 3.9 %slice.128 = bf16[32,90,512]{2,1,0:T(8,128)(2,1)} slice(bf16[32,90,1152]{2,1,0:T(8,128)(2,1)} %all-gather.4.cloned.1.call-done), slice={[0:32], [0:90], [640:1152]} | slice | bytes 5898240 | tf_op jit(solution)/shard_map/slice | solution.py:154
  128.4 7.0 %reshape.321 = bf16[512,2880]{1,0:T(8,128)(2,1)} reshape(bf16[32,90,512]{2,1,0:T(8,128)(2,1)} %slice.128) | data formatting | bytes 5898240 | tf_op jit(solution)/shard_map/reshape | solution.py:154
  135.5 2.8 %fusion.20 = bf16[256,512]{0,1:T(8,128)(2,1)S(1)} fusion(bf16[512,2880]{1,0:T(8,128)(2,1)} %reshape.321, bf16[256,2880]{0,1:T(8,128)(2,1)S(1)} %copy-done), kind=kOutput, calls=%fused_computation.25 | convolution fusion | flops 755105792 | bytes 4685824 | tf_op jit(solution)/shard_map/dot_general | solution.py:32
  138.7 2.2 convolution_bitcast_fusion
  140.9 2.9 %collective-permute-start.3 = (bf16[128,64]{0,1:T(8,128)(2,1)S(1)}, bf16[128,64]{0,1:T(8,128)(2,1)S(1)}, u32[]{:S(2)}, u32[]{:S(2)}) collective-permute-start(bf16[128,64]{0,1:T(8,128)(2,1)S(1)} %get-tuple-element.49), channel_id=1, source_target_pairs={{8,0},{16,8},{24,16},{32,24},{40,32},{48,40},{56,48},{64,56},{72,6... | collective-permute-start | bytes 49160 | tf_op jit(solution)/shard_map/ppermute | solution.py:22
  143.9 0.6 fusion.8
  144.6 0.4 convolution_bitcast_fusion.1
  145.4 2.7 %collective-permute-start.2 = (bf16[128,64]{0,1:T(8,128)(2,1)S(1)}, bf16[128,64]{0,1:T(8,128)(2,1)S(1)}, u32[]{:S(2)}, u32[]{:S(2)}) collective-permute-start(bf16[128,64]{0,1:T(8,128)(2,1)S(1)} %get-tuple-element.47), channel_id=1, source_target_pairs={{8,0},{16,8},{24,16},{32,24},{40,32},{48,40},{56,48},{64,56},{72,6... | collective-permute-start | bytes 49160 | tf_op jit(solution)/shard_map/ppermute | solution.py:22
  148.9 2.3 collective-permute-done.2
  151.5 5.3 %fusion.23 = f32[256,4,2,4,90]{0,4,3,2,1:T(8,128)S(1)} fusion(bf16[4,2,4,90,1152]{4,3,2,1,0:T(8,128)(2,1)} %bitcast.184, bf16[256,640]{1,0:T(8,128)(2,1)S(1)} %pad_maximum_fusion.1), kind=kOutput, calls=%fused_computation.31 | convolution fusion | flops 1698693120 | bytes 9912320 | tf_op jit(solution)/shard_map/tc,mjrc->tmjr/dot_general | solution.py:194
  156.9 1.7 copy.111
  158.6 2.3 reshape.325
  161.0 1.6 constant_dynamic-slice_fusion
  162.6 2.3 bitcast_add_fusion
  164.9 1.1 copy-done.3
  166.0 0.9 fusion.41
  166.9 1.5 collective-permute-start.5
  168.4 1.8 collective-permute-start.7
  170.1 1.8 collective-permute-start.6
  172.0 3.2 %convert_bitcast_fusion = bf16[8,4,90,640]{3,2,1,0:T(8,128)(2,1)} fusion(bf16[256,640]{1,0:T(8,128)(2,1)S(1)} %pad_maximum_fusion.1, bf16[256,4,8,90]{0,3,2,1:T(8,128)(2,1)S(1)} %reshape.325), kind=kOutput, calls=%fused_computation.3 | convolution fusion | flops 945561600 | bytes 5488640 | tf_op jit(solution)/shard_map/tzxr,tc->zxrc/dot_general | solution.py:199
  175.5 3.2 %collective-permute-done.7 = bf16[256,4,90]{0,1,2:T(4,128)(2,1)} collective-permute-done((bf16[256,4,90]{0,1,2:T(4,128)(2,1)}, bf16[256,4,90]{0,1,2:T(4,128)(2,1)}, u32[]{:S(2)}, u32[]{:S(2)}) %collective-permute-start.7) | collective-permute-done | bytes 184352 | tf_op jit(solution)/shard_map/ppermute | solution.py:83
  178.7 1.7 collective-permute-done.6
  180.4 1.4 fusion.29
  181.9 0.7 convert_element_type.165
  182.7 1.5 reshape_squeeze.3
  184.2 48.3 %reduce-scatter.6.cloned.1.call-done = bf16[1,4,90,640]{3,2,1,0:T(8,128)(2,1)} async-done(((bf16[8,4,90,640]{3,2,1,0:T(8,128)(2,1)}), bf16[1,4,90,640]{3,2,1,0:T(8,128)(2,1)}) %reduce-scatter.6.cloned.1.call-update) | async-done | bytes 460816 | tf_op jit(solution)/shard_map/reduce_scatter | solution.py:203
  232.5 2.0 pad_maximum_fusion
  234.6 22.6 %reduce-scatter.10.cloned.1.call-done = bf16[1,162,640]{2,1,0:T(8,128)(2,1)} async-done(((bf16[4,162,640]{2,1,0:T(8,128)(2,1)}), bf16[1,162,640]{2,1,0:T(8,128)(2,1)}) %reduce-scatter.10.cloned.1.call-update) | async-done | bytes 207376
  257.2 1.0 convert_element_type.168
  258.3 0.7 slice.167
  259.0 0.8 mul.65
  259.8 0.7 copy.115
  260.5 0.7 copy.114
  (69 shorter events, 4.0 us)
Async XLA Ops:
  7.2 114.6 %copy-start = (bf16[256,2880]{0,1:T(8,128)(2,1)S(1)}, bf16[256,2880]{0,1:T(8,128)(2,1)}, u32[]{:S(2)}) copy-start(bf16[256,2880]{0,1:T(8,128)(2,1)} %param.13) | copy-start | bytes 4423684
  7.2 98.1 %all-gather.4.cloned.1.call-start = ((), (), s32[]{:S(2)}) async-start(), calls=%async_computation.5 | async-start | bytes 7299072 | tf_op jit(solution)/shard_map/all_gather | solution.py:108
  11.8 171.0 %reduce-scatter.8.cloned.1.call-start = ((), (), s32[]{:S(2)}) async-start(), calls=%async_computation.4 | async-start | bytes 3391488 | tf_op jit(solution)/shard_map/reduce_scatter | solution.py:153
  108.7 7.7 %collective-permute-start.1 = (bf16[128,64]{0,1:T(8,128)(2,1)S(1)}, bf16[128,64]{0,1:T(8,128)(2,1)S(1)}, u32[]{:S(2)}, u32[]{:S(2)}) collective-permute-start(bf16[128,64]{0,1:T(8,128)(2,1)S(1)} %get-tuple-element.36), channel_id=1, source_target_pairs={{0,8},{8,16},{16,24},{24,32},{32,40},{40,48},{48,56},{56,64},{64,7... | collective-permute-start | bytes 49160 | tf_op jit(solution)/shard_map/ppermute | solution.py:22
  111.6 7.7 %collective-permute-start = (bf16[128,64]{0,1:T(8,128)(2,1)S(1)}, bf16[128,64]{0,1:T(8,128)(2,1)S(1)}, u32[]{:S(2)}, u32[]{:S(2)}) collective-permute-start(bf16[128,64]{0,1:T(8,128)(2,1)S(1)} %get-tuple-element.37), channel_id=1, source_target_pairs={{0,8},{8,16},{16,24},{24,32},{32,40},{40,48},{48,56},{56,64},{64,7... | collective-permute-start | bytes 49160 | tf_op jit(solution)/shard_map/ppermute | solution.py:22
  114.7 5.3 %copy-start.5 = (f32[8]{0:T(128)S(1)}, f32[8]{0:T(128)}, u32[]{:S(2)}) copy-start(f32[8]{0:T(128)} %param.12) | copy-start | bytes 100
  119.9 1.3 copy-start.1
  124.5 108.0 %reduce-scatter.6.cloned.1.call-start = ((), (), s32[]{:S(2)}) async-start(), calls=%async_computation.3 | async-start | bytes 4423680 | tf_op jit(solution)/shard_map/reduce_scatter | solution.py:203
  138.6 5.3 %copy-start.2 = (f32[2,1,8,128,256]{3,4,2,0,1:T(8,128)S(1)}, f32[2,1,8,128,256]{3,4,2,0,1:T(8,128)}, u32[]{:S(2)}) copy-start(f32[2,1,8,128,256]{3,4,2,0,1:T(8,128)} %copy-done.1) | copy-start | bytes 6291460
  140.9 7.9 %collective-permute-start.3 = (bf16[128,64]{0,1:T(8,128)(2,1)S(1)}, bf16[128,64]{0,1:T(8,128)(2,1)S(1)}, u32[]{:S(2)}, u32[]{:S(2)}) collective-permute-start(bf16[128,64]{0,1:T(8,128)(2,1)S(1)} %get-tuple-element.49), channel_id=1, source_target_pairs={{8,0},{16,8},{24,16},{32,24},{40,32},{48,40},{56,48},{64,56},{72,6... | collective-permute-start | bytes 49160 | tf_op jit(solution)/shard_map/ppermute | solution.py:22
  145.4 5.8 %collective-permute-start.2 = (bf16[128,64]{0,1:T(8,128)(2,1)S(1)}, bf16[128,64]{0,1:T(8,128)(2,1)S(1)}, u32[]{:S(2)}, u32[]{:S(2)}) collective-permute-start(bf16[128,64]{0,1:T(8,128)(2,1)S(1)} %get-tuple-element.47), channel_id=1, source_target_pairs={{8,0},{16,8},{24,16},{32,24},{40,32},{48,40},{56,48},{64,56},{72,6... | collective-permute-start | bytes 49160 | tf_op jit(solution)/shard_map/ppermute | solution.py:22
  156.7 1.9 copy-start.4
  158.6 4.0 %collective-permute-start.4 = (bf16[256,4,4,90]{0,2,3,1:T(4,128)(2,1)}, bf16[256,4,4,90]{0,2,3,1:T(4,128)(2,1)}, u32[]{:S(2)}, u32[]{:S(2)}) collective-permute-start(bf16[256,4,4,90]{0,2,3,1:T(4,128)(2,1)} %copy.111), channel_id=1, source_target_pairs={{0,1},{1,0},{2,3},{3,2},{4,5},{5,4},{6,7},{7,6},{8,9},{9,8},{10,11... | collective-permute-start | bytes 2211848 | tf_op jit(solution)/shard_map/ppermute | solution.py:76
  164.8 1.1 copy-start.3
  166.9 8.6 %collective-permute-start.5 = (bf16[256,4,90]{0,1,2:T(4,128)(2,1)}, bf16[256,4,90]{0,1,2:T(4,128)(2,1)}, u32[]{:S(2)}, u32[]{:S(2)}) collective-permute-start(bf16[256,4,90]{0,1,2:T(4,128)(2,1)} %get-tuple-element.33), channel_id=1, source_target_pairs={{0,2},{1,3},{2,4},{3,5},{4,6},{5,7},{6,0},{7,1},{8,10},{9,11},{10,... | collective-permute-start | bytes 552968 | tf_op jit(solution)/shard_map/ppermute | solution.py:83
  168.4 10.3 %collective-permute-start.7 = (bf16[256,4,90]{0,1,2:T(4,128)(2,1)}, bf16[256,4,90]{0,1,2:T(4,128)(2,1)}, u32[]{:S(2)}, u32[]{:S(2)}) collective-permute-start(bf16[256,4,90]{0,1,2:T(4,128)(2,1)} %get-tuple-element.34), channel_id=1, source_target_pairs={{0,6},{1,7},{2,0},{3,1},{4,2},{5,3},{6,4},{7,5},{8,14},{9,15},{10,... | collective-permute-start | bytes 552968 | tf_op jit(solution)/shard_map/ppermute | solution.py:83
  170.1 10.3 %collective-permute-start.6 = (bf16[256,4,90]{0,1,2:T(4,128)(2,1)}, bf16[256,4,90]{0,1,2:T(4,128)(2,1)}, u32[]{:S(2)}, u32[]{:S(2)}) collective-permute-start(bf16[256,4,90]{0,1,2:T(4,128)(2,1)} %get-tuple-element.35), channel_id=1, source_target_pairs={{0,4},{1,5},{2,6},{3,7},{4,0},{5,1},{6,2},{7,3},{8,12},{9,13},{10,... | collective-permute-start | bytes 552968 | tf_op jit(solution)/shard_map/ppermute | solution.py:83
  182.7 74.5 %reduce-scatter.10.cloned.1.call-start = ((), (), s32[]{:S(2)}) async-start(), calls=%async_computation.6 | async-start | bytes 1075200
Sparse Core Ops, SparseCore 0:
  11.9 93.3 all-gather.3
  124.6 44.0 reduce-scatter.7
  182.8 49.6 reduce-scatter.5
  234.9 22.1 reduce-scatter.9

commit v7 on v6

--- a/solution.py
+++ b/solution.py
@@ -85,6 +85,18 @@
     return result.reshape(result.shape[0], -1).astype(jnp.bfloat16)
 
 
+def scatter_rows_x(parts):
+    peers = lax.axis_size("dx")
+    me = lax.axis_index("dx")
+    total = lax.dynamic_index_in_dim(parts, me, axis=0, keepdims=False).astype(jnp.float32)
+    for shift in range(1, peers):
+        dest = (me + shift) % peers
+        piece = lax.dynamic_index_in_dim(parts, dest, axis=0, keepdims=False)
+        pairs = [(i, (i + shift) % peers) for i in range(peers)]
+        total = total + lax.ppermute(piece, "dx", pairs).astype(jnp.float32)
+    return total
+
+
 def by_zx(rows, x_peers, z_peers):
     split = rows.reshape(rows.shape[0], x_peers, z_peers, -1)
     return split.transpose(0, 2, 1, 3)
@@ -116,7 +128,8 @@
     queries = qkv[:, :q_cols]
     key_rows = qkv[:, q_cols : q_cols + k_cols]
     value_rows = qkv[:, q_cols + k_cols :]
-    rim_keys, rim_values = passed_along((key_rows[-window:], value_rows[-window:]), DP_AXES, 1)
+    rim = passed_along(qkv[-window:, q_cols:], DP_AXES, 1)
+    rim_keys, rim_values = rim[:, :k_cols], rim[:, k_cols:]
     first_row = (lax.axis_index("dx") * z_peers + lax.axis_index("dz")) * row_count
     ext_keys = jnp.concatenate([rim_keys, key_rows], axis=0).reshape(
         row_count + window, kv_heads, DH
@@ -176,10 +189,9 @@
     )
     grad_key_ext = fold_blocks(grad_key_blk, window).reshape(row_count + window, -1)
     grad_value_ext = fold_blocks(grad_value_blk, window).reshape(row_count + window, -1)
-    back_keys, back_values = (
-        passed_along(grad_key_ext[:window].astype(jnp.bfloat16), DP_AXES, -1).astype(jnp.float32),
-        passed_along(grad_value_ext[:window].astype(jnp.bfloat16), DP_AXES, -1).astype(jnp.float32),
-    )
+    back_rim = jnp.concatenate([grad_key_ext[:window], grad_value_ext[:window]], axis=1)
+    back_rim = passed_along(back_rim.astype(jnp.bfloat16), DP_AXES, -1).astype(jnp.float32)
+    back_keys, back_values = back_rim[:, :k_cols], back_rim[:, k_cols:]
     own_keys = grad_key_ext[window:]
     own_values = grad_value_ext[window:]
     grad_keys = jnp.concatenate(
@@ -203,7 +215,7 @@
     in_over_z = lax.psum_scatter(grad_in_part, "dz", scatter_dimension=0, tiled=True)[0]
     out_over_z = out_over_z.reshape(x_peers, -1, in_width)
     both = jnp.concatenate([in_over_z, out_over_z], axis=1)
-    over_x = lax.psum_scatter(both, "dx", scatter_dimension=0, tiled=True)[0].astype(jnp.float32)
+    over_x = scatter_rows_x(both)
     in_rows = w_query.shape[0]
     grad_in = over_x[:in_rows]
     grad_w_out = over_x[in_rows:].reshape(w_out.shape)

time: 271 us -> 253 us (0.934); the launches traced: 268 us -> 252 us
  waiting for transfers between devices: 174 us -> 161 us
    unnamed x5 -> x3, waiting for transfers between devices: 22.7 us -> 0.05 us
    ppermute x0 -> x3, waiting for transfers between devices: none -> 8.93 us  [scatter_rows_x(): total = total + lax.ppermute(piece, 'dx', pairs).astype(jnp.float32)]
    ppermute x4 -> x2, starting transfers between devices: 11.6 us -> 5.68 us  [passed_along(): return lax.ppermute(array, axis, pairs)]
    ppermute x0 -> x3, starting transfers between devices: none -> 4.78 us  [scatter_rows_x(): total = total + lax.ppermute(piece, 'dx', pairs).astype(jnp.float32)]
    ppermute x4 -> x2, waiting for transfers between devices: 6.79 us -> 7.63 us  [passed_along(): return lax.ppermute(array, axis, pairs)]
  transfers between devices with their start and end apart: 12 -> 12, of which waited for: 9 -> 10; matrix products, arithmetic and copies ran while one was open for 16% -> 17% of each run, Pallas kernels for 0% -> 0%
where the time goes in v7:
time: 253 us; the launch traced here: 252 us
  waiting for transfers between devices  161 us (64%)
  local copies, waits for them, and re-layouts  33.1 us (13%)
  matrix products  21.9 us (9%)
  starting transfers between devices  15.4 us (6%)
  between operations  14.3 us (6%)
  other arithmetic  6.95 us (3%)
    all_gather x1, waiting for transfers between devices, shards(): gathered = lax.all_gather(packed, DP_AXES, axis=0, tiled=False)  90.8 us
    reduce_scatter x1, waiting for transfers between devices, shards(): lax.psum_scatter(grad_in_part, 'dz', scatter_dimension=0, tiled=True)[0]  48 us
    ppermute x3, waiting for transfers between devices, scatter_rows_x(): total = total + lax.ppermute(piece, 'dx', pairs).astype(jnp.float32)  8.93 us
    ppermute x2, waiting for transfers between devices, passed_along(): return lax.ppermute(array, axis, pairs)  7.63 us
    reshape x1, local copies, waits for them, and re-layouts, shards(): full_out = late_gathered[:, :, in_width:].reshape((-1,) + w_out.shape[1:])  7.02 us
    ppermute x2, starting transfers between devices, passed_along(): return lax.ppermute(array, axis, pairs)  5.68 us
    ppermute x4, waiting for transfers between devices, scatter_cols_mp(): got = lax.ppermute(piece.astype(jnp.bfloat16), 'mp', pairs)  5.38 us
    dot_general x1, matrix products, shards(): jnp.einsum('tc,mjrc->tmjr', grad_wide, proj_by_mp, preferred_element_type...  5.24 us
  transfers between devices with their start and end apart: 12, of which 10 were waited for; matrix products, arithmetic and copies ran while one was open for 17% of the time, Pallas kernels for 0%

profile of v7, /device:TPU:2, one launch (start us, length us, event | category | flops | bytes accessed | tf_op | source)
XLA Modules:
  0.0 252.5 jit_solution(12845696876878103452)
XLA Ops:
  7.2 0.9 copy.84
  8.2 0.8 copy.85
  9.0 1.1 reshape.309
  10.1 1.7 concatenate.33
  11.8 2.3 reshape.310
  14.5 90.8 %all-gather.4.cloned.1.call-done = bf16[32,90,1152]{2,1,0:T(8,128)(2,1)} async-done(((bf16[1,90,1152]{2,1,0:T(8,128)(2,1)}), bf16[32,90,1152]{2,1,0:T(8,128)(2,1)}) %all-gather.4.cloned.1.call-update) | async-done | bytes 6635536 | tf_op jit(solution)/shard_map/all_gather | solution.py:120
  105.3 3.3 %fusion.15 = bf16[256,640]{0,1:T(8,128)(2,1)S(1)} fusion(bf16[256,32,90]{0,2,1:T(8,128)(2,1)S(1)} %reshape.310, bf16[32,90,1152]{2,1,0:T(8,128)(2,1)} %all-gather.4.cloned.1.call-done), kind=kOutput, calls=%fused_computation.26 | convolution fusion | flops 943882240 | bytes 5734400 | tf_op jit(solution)/shard_map/tdr,drc->tc/dot_general | solution.py:125
  108.7 2.9 %collective-permute-start = (bf16[128,128]{0,1:T(8,128)(2,1)S(1)}, bf16[128,128]{0,1:T(8,128)(2,1)S(1)}, u32[]{:S(2)}, u32[]{:S(2)}) collective-permute-start(bf16[128,128]{0,1:T(8,128)(2,1)S(1)} %slice.163), channel_id=1, source_target_pairs={{0,8},{8,16},{16,24},{24,32},{32,40},{40,48},{48,56},{56,64},{64,7... | collective-permute-start | bytes 98312 | tf_op jit(solution)/shard_map/ppermute | solution.py:22
  111.8 4.8 %collective-permute-done = bf16[128,128]{0,1:T(8,128)(2,1)S(1)} collective-permute-done((bf16[128,128]{0,1:T(8,128)(2,1)S(1)}, bf16[128,128]{0,1:T(8,128)(2,1)S(1)}, u32[]{:S(2)}, u32[]{:S(2)}) %collective-permute-start) | collective-permute-done | bytes 32800 | tf_op jit(solution)/shard_map/ppermute | solution.py:22
  116.7 0.5 fusion.74
  119.0 2.7 %convolution_convert_fusion = bf16[8,4,16,2880]{3,2,1,0:T(8,128)(2,1)} fusion(bf16[256,2880]{0,1:T(8,128)(2,1)S(1)} %copy-done, bf16[256,4,8,16]{0,3,2,1:T(8,128)(2,1)S(1)} %reshape_reshape.2), kind=kOutput, calls=%fused_computation | convolution fusion | flops 756449280 | bytes 4685824 | tf_op jit(solution)/shard_map/tzxi,tc->zxic/dot_general | solution.py:162
  121.8 3.9 %slice.138 = bf16[32,90,512]{2,1,0:T(8,128)(2,1)} slice(bf16[32,90,1152]{2,1,0:T(8,128)(2,1)} %all-gather.4.cloned.1.call-done), slice={[0:32], [0:90], [640:1152]} | slice | bytes 5898240 | tf_op jit(solution)/shard_map/slice | solution.py:167
  125.7 7.0 %reshape.315 = bf16[512,2880]{1,0:T(8,128)(2,1)} reshape(bf16[32,90,512]{2,1,0:T(8,128)(2,1)} %slice.138) | data formatting | bytes 5898240 | tf_op jit(solution)/shard_map/reshape | solution.py:167
  132.7 2.8 %fusion.20 = bf16[256,512]{0,1:T(8,128)(2,1)S(1)} fusion(bf16[512,2880]{1,0:T(8,128)(2,1)} %reshape.315, bf16[256,2880]{0,1:T(8,128)(2,1)S(1)} %copy-done), kind=kOutput, calls=%fused_computation.29 | convolution fusion | flops 755105792 | bytes 4685824 | tf_op jit(solution)/shard_map/dot_general | solution.py:32
  135.9 2.2 convolution_bitcast_fusion
  138.2 0.6 fusion.8
  139.4 2.8 %collective-permute-start.1 = (bf16[128,128]{0,1:T(8,128)(2,1)S(1)}, bf16[128,128]{0,1:T(8,128)(2,1)S(1)}, u32[]{:S(2)}, u32[]{:S(2)}) collective-permute-start(bf16[128,128]{0,1:T(8,128)(2,1)S(1)} %pad_maximum_fusion.3), channel_id=1, source_target_pairs={{8,0},{16,8},{24,16},{32,24},{40,32},{48,40},{56,48},{64,56},{72,6... | collective-permute-start | bytes 98312 | tf_op jit(solution)/shard_map/ppermute | solution.py:22
  143.1 2.8 %collective-permute-done.1 = bf16[128,128]{0,1:T(8,128)(2,1)S(1)} collective-permute-done((bf16[128,128]{0,1:T(8,128)(2,1)S(1)}, bf16[128,128]{0,1:T(8,128)(2,1)S(1)}, u32[]{:S(2)}, u32[]{:S(2)}) %collective-permute-start.1) | collective-permute-done | bytes 32800 | tf_op jit(solution)/shard_map/ppermute | solution.py:22
  146.3 5.2 %fusion.23 = f32[256,4,2,4,90]{0,4,3,2,1:T(8,128)S(1)} fusion(bf16[4,2,4,90,1152]{4,3,2,1,0:T(8,128)(2,1)} %bitcast.190, bf16[256,640]{1,0:T(8,128)(2,1)S(1)} %pad_maximum_fusion), kind=kOutput, calls=%fused_computation.38 | convolution fusion | flops 1698693120 | bytes 9912320 | tf_op jit(solution)/shard_map/tc,mjrc->tmjr/dot_general | solution.py:206
  151.7 1.7 copy.107
  153.4 2.3 reshape.319
  155.8 1.6 constant_dynamic-slice_fusion
  157.4 2.3 bitcast_add_fusion
  159.7 1.1 copy-done.3
  160.8 0.9 fusion.50
  161.8 1.3 collective-permute-start.3
  163.0 2.0 collective-permute-start.5
  165.0 1.6 collective-permute-start.4
  166.6 3.3 %convert_bitcast_fusion = bf16[8,4,90,640]{3,2,1,0:T(8,128)(2,1)} fusion(bf16[256,640]{1,0:T(8,128)(2,1)S(1)} %pad_maximum_fusion, bf16[256,4,8,90]{0,3,2,1:T(8,128)(2,1)S(1)} %reshape.319), kind=kOutput, calls=%fused_computation.3 | convolution fusion | flops 945561600 | bytes 5488640 | tf_op jit(solution)/shard_map/tzxr,tc->zxrc/dot_general | solution.py:211
  169.9 0.5 collective-permute-done.3
  170.4 3.2 %collective-permute-done.5 = bf16[256,4,90]{0,1,2:T(4,128)(2,1)} collective-permute-done((bf16[256,4,90]{0,1,2:T(4,128)(2,1)}, bf16[256,4,90]{0,1,2:T(4,128)(2,1)}, u32[]{:S(2)}, u32[]{:S(2)}) %collective-permute-start.5) | collective-permute-done | bytes 184352 | tf_op jit(solution)/shard_map/ppermute | solution.py:83
  173.6 1.6 collective-permute-done.4
  175.2 1.4 fusion.31
  176.7 0.7 convert_element_type.163
  177.5 1.5 reshape_squeeze.3
  179.0 48.0 %reduce-scatter.3.cloned.1.call-done = bf16[1,4,90,640]{3,2,1,0:T(8,128)(2,1)} async-done(((bf16[8,4,90,640]{3,2,1,0:T(8,128)(2,1)}), bf16[1,4,90,640]{3,2,1,0:T(8,128)(2,1)}) %reduce-scatter.3.cloned.1.call-update) | async-done | bytes 460816 | tf_op jit(solution)/shard_map/reduce_scatter | solution.py:215
  227.1 1.1 fusion.47
  228.2 1.5 collective-permute-start.6
  229.7 1.2 collective-permute-start.7
  230.9 2.1 collective-permute-start.8
  233.0 3.5 %collective-permute-done.6 = bf16[162,640]{1,0:T(8,128)(2,1)S(1)} collective-permute-done((bf16[162,640]{1,0:T(8,128)(2,1)S(1)}, bf16[162,640]{1,0:T(8,128)(2,1)S(1)}, u32[]{:S(2)}, u32[]{:S(2)}) %collective-permute-start.6) | collective-permute-done | bytes 207392 | tf_op jit(solution)/shard_map/ppermute | solution.py:96
  236.4 3.0 %collective-permute-done.7 = bf16[162,640]{1,0:T(8,128)(2,1)S(1)} collective-permute-done((bf16[162,640]{1,0:T(8,128)(2,1)S(1)}, bf16[162,640]{1,0:T(8,128)(2,1)S(1)}, u32[]{:S(2)}, u32[]{:S(2)}) %collective-permute-start.7) | collective-permute-done | bytes 207392 | tf_op jit(solution)/shard_map/ppermute | solution.py:96
  239.4 2.5 collective-permute-done.8
  241.9 1.0 fusion.28
  243.1 0.7 slice.184
  243.8 0.8 mul.60
  244.5 0.7 copy.111
  245.2 0.7 copy.110
  (70 shorter events, 5.0 us)
Async XLA Ops:
  7.2 111.8 %copy-start = (bf16[256,2880]{0,1:T(8,128)(2,1)S(1)}, bf16[256,2880]{0,1:T(8,128)(2,1)}, u32[]{:S(2)}) copy-start(bf16[256,2880]{0,1:T(8,128)(2,1)} %param.13) | copy-start | bytes 4423684
  7.2 98.1 %all-gather.4.cloned.1.call-start = ((), (), s32[]{:S(2)}) async-start(), calls=%async_computation.4 | async-start | bytes 7299072 | tf_op jit(solution)/shard_map/all_gather | solution.py:120
  11.8 165.8 %reduce-scatter.5.cloned.1.call-start = ((), (), s32[]{:S(2)}) async-start(), calls=%async_computation.3 | async-start | bytes 3391488 | tf_op jit(solution)/shard_map/reduce_scatter | solution.py:166
  108.7 7.9 %collective-permute-start = (bf16[128,128]{0,1:T(8,128)(2,1)S(1)}, bf16[128,128]{0,1:T(8,128)(2,1)S(1)}, u32[]{:S(2)}, u32[]{:S(2)}) collective-permute-start(bf16[128,128]{0,1:T(8,128)(2,1)S(1)} %slice.163), channel_id=1, source_target_pairs={{0,8},{8,16},{16,24},{24,32},{32,40},{40,48},{48,56},{56,64},{64,7... | collective-permute-start | bytes 98312 | tf_op jit(solution)/shard_map/ppermute | solution.py:22
  111.6 5.6 %copy-start.5 = (f32[8]{0:T(128)S(1)}, f32[8]{0:T(128)}, u32[]{:S(2)}) copy-start(f32[8]{0:T(128)} %param.12) | copy-start | bytes 100
  117.2 1.3 copy-start.1
  121.7 105.3 %reduce-scatter.3.cloned.1.call-start = ((), (), s32[]{:S(2)}) async-start(), calls=%async_computation.2 | async-start | bytes 4423680 | tf_op jit(solution)/shard_map/reduce_scatter | solution.py:215
  135.9 2.3 copy-start.2
  139.4 6.6 %collective-permute-start.1 = (bf16[128,128]{0,1:T(8,128)(2,1)S(1)}, bf16[128,128]{0,1:T(8,128)(2,1)S(1)}, u32[]{:S(2)}, u32[]{:S(2)}) collective-permute-start(bf16[128,128]{0,1:T(8,128)(2,1)S(1)} %pad_maximum_fusion.3), channel_id=1, source_target_pairs={{8,0},{16,8},{24,16},{32,24},{40,32},{48,40},{56,48},{64,56},{72,6... | collective-permute-start | bytes 98312 | tf_op jit(solution)/shard_map/ppermute | solution.py:22
  151.6 1.9 copy-start.4
  153.4 4.0 %collective-permute-start.2 = (bf16[256,4,4,90]{0,2,3,1:T(4,128)(2,1)}, bf16[256,4,4,90]{0,2,3,1:T(4,128)(2,1)}, u32[]{:S(2)}, u32[]{:S(2)}) collective-permute-start(bf16[256,4,4,90]{0,2,3,1:T(4,128)(2,1)} %copy.107), channel_id=1, source_target_pairs={{0,1},{1,0},{2,3},{3,2},{4,5},{5,4},{6,7},{7,6},{8,9},{9,8},{10,11... | collective-permute-start | bytes 2211848 | tf_op jit(solution)/shard_map/ppermute | solution.py:76
  159.7 1.2 copy-start.3
  161.8 8.6 %collective-permute-start.3 = (bf16[256,4,90]{0,1,2:T(4,128)(2,1)}, bf16[256,4,90]{0,1,2:T(4,128)(2,1)}, u32[]{:S(2)}, u32[]{:S(2)}) collective-permute-start(bf16[256,4,90]{0,1,2:T(4,128)(2,1)} %get-tuple-element.33), channel_id=1, source_target_pairs={{0,2},{1,3},{2,4},{3,5},{4,6},{5,7},{6,0},{7,1},{8,10},{9,11},{10,... | collective-permute-start | bytes 552968 | tf_op jit(solution)/shard_map/ppermute | solution.py:83
  163.0 10.6 %collective-permute-start.5 = (bf16[256,4,90]{0,1,2:T(4,128)(2,1)}, bf16[256,4,90]{0,1,2:T(4,128)(2,1)}, u32[]{:S(2)}, u32[]{:S(2)}) collective-permute-start(bf16[256,4,90]{0,1,2:T(4,128)(2,1)} %get-tuple-element.34), channel_id=1, source_target_pairs={{0,6},{1,7},{2,0},{3,1},{4,2},{5,3},{6,4},{7,5},{8,14},{9,15},{10,... | collective-permute-start | bytes 552968 | tf_op jit(solution)/shard_map/ppermute | solution.py:83
  165.0 10.2 %collective-permute-start.4 = (bf16[256,4,90]{0,1,2:T(4,128)(2,1)}, bf16[256,4,90]{0,1,2:T(4,128)(2,1)}, u32[]{:S(2)}, u32[]{:S(2)}) collective-permute-start(bf16[256,4,90]{0,1,2:T(4,128)(2,1)} %get-tuple-element.35), channel_id=1, source_target_pairs={{0,4},{1,5},{2,6},{3,7},{4,0},{5,1},{6,2},{7,3},{8,12},{9,13},{10,... | collective-permute-start | bytes 552968 | tf_op jit(solution)/shard_map/ppermute | solution.py:83
  228.2 8.2 %collective-permute-start.6 = (bf16[162,640]{1,0:T(8,128)(2,1)S(1)}, bf16[162,640]{1,0:T(8,128)(2,1)S(1)}, u32[]{:S(2)}, u32[]{:S(2)}) collective-permute-start(bf16[162,640]{1,0:T(8,128)(2,1)S(1)} %get-tuple-element.36), channel_id=1, source_target_pairs={{0,64},{64,128},{128,192},{192,0},{1,65},{65,129},{129,193},{193,1... | collective-permute-start | bytes 622088 | tf_op jit(solution)/shard_map/ppermute | solution.py:96
  229.7 9.7 %collective-permute-start.7 = (bf16[162,640]{1,0:T(8,128)(2,1)S(1)}, bf16[162,640]{1,0:T(8,128)(2,1)S(1)}, u32[]{:S(2)}, u32[]{:S(2)}) collective-permute-start(bf16[162,640]{1,0:T(8,128)(2,1)S(1)} %get-tuple-element.37), channel_id=1, source_target_pairs={{0,128},{64,192},{128,0},{192,64},{1,129},{65,193},{129,1},{193,65... | collective-permute-start | bytes 622088 | tf_op jit(solution)/shard_map/ppermute | solution.py:96
  230.9 11.0 %collective-permute-start.8 = (bf16[162,640]{1,0:T(8,128)(2,1)S(1)}, bf16[162,640]{1,0:T(8,128)(2,1)S(1)}, u32[]{:S(2)}, u32[]{:S(2)}) collective-permute-start(bf16[162,640]{1,0:T(8,128)(2,1)S(1)} %get-tuple-element.38), channel_id=1, source_target_pairs={{0,192},{64,0},{128,64},{192,128},{1,193},{65,1},{129,65},{193,129... | collective-permute-start | bytes 622088 | tf_op jit(solution)/shard_map/ppermute | solution.py:96
Sparse Core Ops, SparseCore 0:
  11.9 93.3 all-gather.3
  121.8 44.3 reduce-scatter.4
  177.6 49.4 reduce-scatter.2

commit v8 on v7

--- a/solution.py
+++ b/solution.py
@@ -201,18 +201,18 @@
         [own_values[:-window], own_values[-window:] + back_values], axis=0
     ).astype(jnp.bfloat16)
     grad_qkv = jnp.concatenate([grad_queries, grad_keys, grad_values], axis=1)
-    grad_wide = jnp.pad(grad_qkv, ((0, 0), (0, gathered.shape[2] - in_width)))
-    proj_by_mp = late_gathered.reshape((mp_peers, -1) + gathered.shape[1:])
-    token_terms = jnp.einsum(
-        "tc,mjrc->tmjr", grad_wide, proj_by_mp, preferred_element_type=jnp.float32
-    )
-    grad_tokens = scatter_cols_mp(token_terms, CORES)
     tokens_zx = by_zx(tokens, x_peers, z_peers)
     grad_in_part = jnp.einsum(
         "tzxr,tc->zxrc", tokens_zx, grad_qkv, preferred_element_type=jnp.float32
     ).astype(jnp.bfloat16)
-    grad_tokens, grad_in_part = lax.optimization_barrier((grad_tokens, grad_in_part))
+    token_src, grad_in_part = lax.optimization_barrier((late_gathered, grad_in_part))
     in_over_z = lax.psum_scatter(grad_in_part, "dz", scatter_dimension=0, tiled=True)[0]
+    grad_wide = jnp.pad(grad_qkv, ((0, 0), (0, gathered.shape[2] - in_width)))
+    proj_by_mp = token_src.reshape((mp_peers, -1) + gathered.shape[1:])
+    token_terms = jnp.einsum(
+        "tc,mjrc->tmjr", grad_wide, proj_by_mp, preferred_element_type=jnp.float32
+    )
+    grad_tokens = scatter_cols_mp(token_terms, CORES)
     out_over_z = out_over_z.reshape(x_peers, -1, in_width)
     both = jnp.concatenate([in_over_z, out_over_z], axis=1)
     over_x = scatter_rows_x(both)

time: 253 us -> 248 us (0.980)
  waiting for transfers between devices: 161 us -> 145 us
  local copies, waits for them, and re-layouts: 33.1 us -> 38.6 us
  other arithmetic: 6.95 us -> 11.6 us
    reduce_scatter x1, waiting for transfers between devices: 48 us -> 40.6 us  [shards(): lax.psum_scatter(grad_in_part, 'dz', scatter_dimension=0, tiled=True)[0]]
    ppermute x4, waiting for transfers between devices: 5.38 us -> 0.79 us  [scatter_cols_mp(): got = lax.ppermute(piece.astype(jnp.bfloat16), 'mp', pairs)]
  transfers between devices with their start and end apart: 12 -> 12, of which waited for: 10 -> 8; matrix products, arithmetic and copies ran while one was open for 17% -> 22% of each run, Pallas kernels for 0% -> 0%
where the time goes in v8:
time: 248 us; the launch traced here: 247 us
  waiting for transfers between devices  145 us (58%)
  local copies, waits for them, and re-layouts  38.6 us (16%)
  matrix products  22.8 us (9%)
  starting transfers between devices  15.3 us (6%)
  between operations  14.2 us (6%)
  other arithmetic  11.6 us (5%)
    all_gather x1, waiting for transfers between devices, shards(): gathered = lax.all_gather(packed, DP_AXES, axis=0, tiled=False)  90.8 us
    reduce_scatter x1, waiting for transfers between devices, shards(): lax.psum_scatter(grad_in_part, 'dz', scatter_dimension=0, tiled=True)[0]  40.6 us
    ppermute x3, waiting for transfers between devices, scatter_rows_x(): total = total + lax.ppermute(piece, 'dx', pairs).astype(jnp.float32)  7.22 us
    reshape x1, local copies, waits for them, and re-layouts, shards(): full_out = late_gathered[:, :, in_width:].reshape((-1,) + w_out.shape[1:])  7.04 us
    ppermute x2, waiting for transfers between devices, passed_along(): return lax.ppermute(array, axis, pairs)  5.52 us
    ppermute x2, starting transfers between devices, passed_along(): return lax.ppermute(array, axis, pairs)  5.43 us
    dot_general x1, matrix products, shards(): jnp.einsum('tc,mjrc->tmjr', grad_wide, proj_by_mp, preferred_element_type...  5.23 us
    ppermute x4, starting transfers between devices, scatter_cols_mp(): got = lax.ppermute(piece.astype(jnp.bfloat16), 'mp', pairs)  4.99 us
  transfers between devices with their start and end apart: 12, of which 8 were waited for; matrix products, arithmetic and copies ran while one was open for 22% of the time, Pallas kernels for 0%

profile of v8, /device:TPU:2, one launch (start us, length us, event | category | flops | bytes accessed | tf_op | source)
XLA Modules:
  0.0 247.4 jit_solution(3602290320868107571)
XLA Ops:
  7.2 0.9 copy.84
  8.2 0.8 copy.85
  9.0 1.1 reshape.309
  10.1 1.7 concatenate.33
  11.8 2.3 reshape.310
  14.5 90.8 %all-gather.4.cloned.1.call-done = bf16[32,90,1152]{2,1,0:T(8,128)(2,1)} async-done(((bf16[1,90,1152]{2,1,0:T(8,128)(2,1)}), bf16[32,90,1152]{2,1,0:T(8,128)(2,1)}) %all-gather.4.cloned.1.call-update) | async-done | bytes 6635536 | tf_op jit(solution)/shard_map/all_gather | solution.py:120
  105.3 3.3 %fusion.15 = bf16[256,640]{0,1:T(8,128)(2,1)S(1)} fusion(bf16[256,32,90]{0,2,1:T(8,128)(2,1)S(1)} %reshape.310, bf16[32,90,1152]{2,1,0:T(8,128)(2,1)} %all-gather.4.cloned.1.call-done), kind=kOutput, calls=%fused_computation.26 | convolution fusion | flops 943882240 | bytes 5734400 | tf_op jit(solution)/shard_map/tdr,drc->tc/dot_general | solution.py:125
  108.7 2.9 %collective-permute-start = (bf16[128,128]{0,1:T(8,128)(2,1)S(1)}, bf16[128,128]{0,1:T(8,128)(2,1)S(1)}, u32[]{:S(2)}, u32[]{:S(2)}) collective-permute-start(bf16[128,128]{0,1:T(8,128)(2,1)S(1)} %slice.163), channel_id=1, source_target_pairs={{0,8},{8,16},{16,24},{24,32},{32,40},{40,48},{48,56},{56,64},{64,7... | collective-permute-start | bytes 98312 | tf_op jit(solution)/shard_map/ppermute | solution.py:22
  111.8 4.8 %collective-permute-done = bf16[128,128]{0,1:T(8,128)(2,1)S(1)} collective-permute-done((bf16[128,128]{0,1:T(8,128)(2,1)S(1)}, bf16[128,128]{0,1:T(8,128)(2,1)S(1)}, u32[]{:S(2)}, u32[]{:S(2)}) %collective-permute-start) | collective-permute-done | bytes 32800 | tf_op jit(solution)/shard_map/ppermute | solution.py:22
  119.0 2.7 %convolution_convert_fusion = bf16[8,4,16,2880]{3,2,1,0:T(8,128)(2,1)} fusion(bf16[256,2880]{0,1:T(8,128)(2,1)S(1)} %copy-done, bf16[256,4,8,16]{0,3,2,1:T(8,128)(2,1)S(1)} %reshape_reshape.2), kind=kOutput, calls=%fused_computation | convolution fusion | flops 756449280 | bytes 4685824 | tf_op jit(solution)/shard_map/tzxi,tc->zxic/dot_general | solution.py:162
  121.8 2.3 reshape.319
  124.1 3.9 %slice.138 = bf16[32,90,512]{2,1,0:T(8,128)(2,1)} slice(bf16[32,90,1152]{2,1,0:T(8,128)(2,1)} %all-gather.4.cloned.1.call-done), slice={[0:32], [0:90], [640:1152]} | slice | bytes 5898240 | tf_op jit(solution)/shard_map/slice | solution.py:167
  128.0 7.0 %reshape.315 = bf16[512,2880]{1,0:T(8,128)(2,1)} reshape(bf16[32,90,512]{2,1,0:T(8,128)(2,1)} %slice.138) | data formatting | bytes 5898240 | tf_op jit(solution)/shard_map/reshape | solution.py:167
  135.1 3.5 %fusion.20 = bf16[256,512]{0,1:T(8,128)(2,1)} fusion(bf16[512,2880]{1,0:T(8,128)(2,1)} %reshape.315, bf16[256,2880]{0,1:T(8,128)(2,1)S(1)} %copy-done), kind=kOutput, calls=%fused_computation.29 | convolution fusion | flops 755105792 | bytes 4685824 | tf_op jit(solution)/shard_map/dot_general | solution.py:32
  138.6 1.7 reshape.316
  140.3 2.0 reshape.320
  142.4 2.3 convolution_bitcast_fusion
  147.4 2.5 %collective-permute-start.1 = (bf16[128,128]{0,1:T(8,128)(2,1)}, bf16[128,128]{0,1:T(8,128)(2,1)}, u32[]{:S(2)}, u32[]{:S(2)}) collective-permute-start(bf16[128,128]{0,1:T(8,128)(2,1)} %pad_maximum_fusion.3), channel_id=1, source_target_pairs={{8,0},{16,8},{24,16},{32,24},{40,32},{48,40},{56,48},{64,56},{72,6... | collective-permute-start | bytes 98312 | tf_op jit(solution)/shard_map/ppermute | solution.py:22
  150.3 1.1 copy.123
  151.3 2.1 reshape.334
  153.4 0.7 collective-permute-done.1
  154.2 0.8 convert_element_type.149
  154.9 0.8 fusion.59
  155.7 0.7 pad_maximum_fusion.5
  156.7 1.0 pad_maximum_fusion
  157.7 3.4 %convert_bitcast_fusion = bf16[8,4,90,640]{3,2,1,0:T(8,128)(2,1)} fusion(bf16[256,640]{1,0:T(8,128)(2,1)S(1)} %pad_maximum_fusion, bf16[256,4,8,90]{0,3,2,1:T(8,128)(2,1)S(1)} %reshape.319), kind=kOutput, calls=%fused_computation.3 | convolution fusion | flops 945561600 | bytes 5488640 | tf_op jit(solution)/shard_map/tzxr,tc->zxrc/dot_general | solution.py:205
  161.2 5.2 %fusion.23 = f32[256,4,2,4,90]{0,4,3,2,1:T(8,128)S(1)} fusion(bf16[4,2,4,90,1152]{4,3,2,1,0:T(8,128)(2,1)} %bitcast.190, bf16[256,640]{1,0:T(8,128)(2,1)S(1)} %pad_maximum_fusion), kind=kOutput, calls=%fused_computation.38 | convolution fusion | flops 1698693120 | bytes 9912320 | tf_op jit(solution)/shard_map/tc,mjrc->tmjr/dot_general | solution.py:212
  167.1 0.9 copy-done.7
  168.0 1.6 constant_dynamic-slice_fusion
  169.6 0.8 collective-permute-done.2
  170.4 2.3 bitcast_add_fusion
  172.6 0.9 fusion.50
  173.6 1.4 collective-permute-start.3
  175.0 1.8 collective-permute-start.5
  176.8 1.7 collective-permute-start.4
  178.6 1.6 reshape_squeeze.3
  180.2 40.6 %reduce-scatter.3.cloned.1.call-done = bf16[1,4,90,640]{3,2,1,0:T(8,128)(2,1)} async-done(((bf16[8,4,90,640]{3,2,1,0:T(8,128)(2,1)}), bf16[1,4,90,640]{3,2,1,0:T(8,128)(2,1)}) %reduce-scatter.3.cloned.1.call-update) | async-done | bytes 460816 | tf_op jit(solution)/shard_map/reduce_scatter | solution.py:209
  220.7 1.9 fusion.47
  222.6 1.5 collective-permute-start.6
  224.1 1.2 collective-permute-start.7
  225.2 2.1 collective-permute-start.8
  227.3 1.3 fusion.31
  228.6 0.7 convert_element_type.165
  229.4 1.6 collective-permute-done.6
  231.0 3.1 %collective-permute-done.7 = bf16[162,640]{1,0:T(8,128)(2,1)} collective-permute-done((bf16[162,640]{1,0:T(8,128)(2,1)}, bf16[162,640]{1,0:T(8,128)(2,1)}, u32[]{:S(2)}, u32[]{:S(2)}) %collective-permute-start.7) | collective-permute-done | bytes 207392 | tf_op jit(solution)/shard_map/ppermute | solution.py:96
  234.1 2.5 %collective-permute-done.8 = bf16[162,640]{1,0:T(8,128)(2,1)} collective-permute-done((bf16[162,640]{1,0:T(8,128)(2,1)}, bf16[162,640]{1,0:T(8,128)(2,1)}, u32[]{:S(2)}, u32[]{:S(2)}) %collective-permute-start.8) | collective-permute-done | bytes 207392 | tf_op jit(solution)/shard_map/ppermute | solution.py:96
  236.6 1.2 fusion.28
  238.7 0.8 mul.60
  (82 shorter events, 9.2 us)
Async XLA Ops:
  7.2 111.8 %copy-start = (bf16[256,2880]{0,1:T(8,128)(2,1)S(1)}, bf16[256,2880]{0,1:T(8,128)(2,1)}, u32[]{:S(2)}) copy-start(bf16[256,2880]{0,1:T(8,128)(2,1)} %param.13) | copy-start | bytes 4423684
  7.2 98.1 %all-gather.4.cloned.1.call-start = ((), (), s32[]{:S(2)}) async-start(), calls=%async_computation.4 | async-start | bytes 7299072 | tf_op jit(solution)/shard_map/all_gather | solution.py:120
  11.7 166.8 %reduce-scatter.5.cloned.1.call-start = ((), (), s32[]{:S(2)}) async-start(), calls=%async_computation.3 | async-start | bytes 3391488 | tf_op jit(solution)/shard_map/reduce_scatter | solution.py:166
  108.7 7.9 %collective-permute-start = (bf16[128,128]{0,1:T(8,128)(2,1)S(1)}, bf16[128,128]{0,1:T(8,128)(2,1)S(1)}, u32[]{:S(2)}, u32[]{:S(2)}) collective-permute-start(bf16[128,128]{0,1:T(8,128)(2,1)S(1)} %slice.163), channel_id=1, source_target_pairs={{0,8},{8,16},{16,24},{24,32},{32,40},{40,48},{48,56},{56,64},{64,7... | collective-permute-start | bytes 98312 | tf_op jit(solution)/shard_map/ppermute | solution.py:22
  111.6 5.6 %copy-start.11 = (f32[8]{0:T(128)S(1)}, f32[8]{0:T(128)}, u32[]{:S(2)}) copy-start(f32[8]{0:T(128)} %param.12) | copy-start | bytes 100
  111.7 5.9 %copy-start.3 = (bf16[2,128,8,64]{1,0,3,2:T(2,128)(2,1)}, bf16[2,128,8,64]{1,0,3,2:T(2,128)(2,1)S(1)}, u32[]{:S(2)}) copy-start(bf16[2,128,8,64]{1,0,3,2:T(2,128)(2,1)S(1)} %reshape.312) | copy-start | bytes 786436
  116.7 0.9 copy-start.9
  117.2 1.4 copy-start.1
  121.7 99.0 %reduce-scatter.3.cloned.1.call-start = ((), (), s32[]{:S(2)}) async-start(), calls=%async_computation.2 | async-start | bytes 4423680 | tf_op jit(solution)/shard_map/reduce_scatter | solution.py:209
  142.4 2.3 copy-start.6
  142.4 2.5 %copy-start.2 = (f32[2,1,8,128,256]{3,4,2,0,1:T(8,128)S(1)}, f32[2,1,8,128,256]{3,4,2,0,1:T(8,128)}, u32[]{:S(2)}) copy-start(f32[2,1,8,128,256]{3,4,2,0,1:T(8,128)} %copy-done.1) | copy-start | bytes 6291460
  142.4 2.5 %copy-start.5 = (bf16[2,128,8,64]{1,0,3,2:T(2,128)(2,1)S(1)}, bf16[2,128,8,64]{1,0,3,2:T(2,128)(2,1)}, u32[]{:S(2)}) copy-start(bf16[2,128,8,64]{1,0,3,2:T(2,128)(2,1)} %reshape.316) | copy-start | bytes 786436
  144.7 1.0 copy-start.4
  144.9 5.1 %copy-start.10 = (bf16[2,128,1,64]{1,3,0,2:T(8,128)(2,1)S(1)}, bf16[2,128,1,64]{1,3,0,2:T(8,128)(2,1)}, u32[]{:S(2)}) copy-start(bf16[2,128,1,64]{1,3,0,2:T(8,128)(2,1)} %copy-done.9) | copy-start | bytes 98308
  146.2 1.3 copy-start.8
  147.4 6.7 %collective-permute-start.1 = (bf16[128,128]{0,1:T(8,128)(2,1)}, bf16[128,128]{0,1:T(8,128)(2,1)}, u32[]{:S(2)}, u32[]{:S(2)}) collective-permute-start(bf16[128,128]{0,1:T(8,128)(2,1)} %pad_maximum_fusion.3), channel_id=1, source_target_pairs={{8,0},{16,8},{24,16},{32,24},{40,32},{48,40},{56,48},{64,56},{72,6... | collective-permute-start | bytes 98312 | tf_op jit(solution)/shard_map/ppermute | solution.py:22
  166.4 1.6 copy-start.7
  168.0 2.3 collective-permute-start.2
  173.6 51.6 %collective-permute-start.3 = (bf16[256,4,90]{0,1,2:T(4,128)(2,1)}, bf16[256,4,90]{0,1,2:T(4,128)(2,1)}, u32[]{:S(2)}, u32[]{:S(2)}) collective-permute-start(bf16[256,4,90]{0,1,2:T(4,128)(2,1)} %get-tuple-element.33), channel_id=1, source_target_pairs={{0,2},{1,3},{2,4},{3,5},{4,6},{5,7},{6,0},{7,1},{8,10},{9,11},{10,... | collective-permute-start | bytes 552968 | tf_op jit(solution)/shard_map/ppermute | solution.py:83
  175.0 52.3 %collective-permute-start.5 = (bf16[256,4,90]{0,1,2:T(4,128)(2,1)}, bf16[256,4,90]{0,1,2:T(4,128)(2,1)}, u32[]{:S(2)}, u32[]{:S(2)}) collective-permute-start(bf16[256,4,90]{0,1,2:T(4,128)(2,1)} %get-tuple-element.34), channel_id=1, source_target_pairs={{0,6},{1,7},{2,0},{3,1},{4,2},{5,3},{6,4},{7,5},{8,14},{9,15},{10,... | collective-permute-start | bytes 552968 | tf_op jit(solution)/shard_map/ppermute | solution.py:83
  176.8 50.5 %collective-permute-start.4 = (bf16[256,4,90]{0,1,2:T(4,128)(2,1)}, bf16[256,4,90]{0,1,2:T(4,128)(2,1)}, u32[]{:S(2)}, u32[]{:S(2)}) collective-permute-start(bf16[256,4,90]{0,1,2:T(4,128)(2,1)} %get-tuple-element.35), channel_id=1, source_target_pairs={{0,4},{1,5},{2,6},{3,7},{4,0},{5,1},{6,2},{7,3},{8,12},{9,13},{10,... | collective-permute-start | bytes 552968 | tf_op jit(solution)/shard_map/ppermute | solution.py:83
  222.6 8.4 %collective-permute-start.6 = (bf16[162,640]{1,0:T(8,128)(2,1)}, bf16[162,640]{1,0:T(8,128)(2,1)S(1)}, u32[]{:S(2)}, u32[]{:S(2)}) collective-permute-start(bf16[162,640]{1,0:T(8,128)(2,1)} %get-tuple-element.36), channel_id=1, source_target_pairs={{0,64},{64,128},{128,192},{192,0},{1,65},{65,129},{129,193},{193,1... | collective-permute-start | bytes 622088 | tf_op jit(solution)/shard_map/ppermute | solution.py:96
  224.1 10.0 %collective-permute-start.7 = (bf16[162,640]{1,0:T(8,128)(2,1)}, bf16[162,640]{1,0:T(8,128)(2,1)}, u32[]{:S(2)}, u32[]{:S(2)}) collective-permute-start(bf16[162,640]{1,0:T(8,128)(2,1)} %get-tuple-element.37), channel_id=1, source_target_pairs={{0,128},{64,192},{128,0},{192,64},{1,129},{65,193},{129,1},{193,65... | collective-permute-start | bytes 622088 | tf_op jit(solution)/shard_map/ppermute | solution.py:96
  225.2 11.4 %collective-permute-start.8 = (bf16[162,640]{1,0:T(8,128)(2,1)}, bf16[162,640]{1,0:T(8,128)(2,1)}, u32[]{:S(2)}, u32[]{:S(2)}) collective-permute-start(bf16[162,640]{1,0:T(8,128)(2,1)} %get-tuple-element.38), channel_id=1, source_target_pairs={{0,192},{64,0},{128,64},{192,128},{1,193},{65,1},{129,65},{193,129... | collective-permute-start | bytes 622088 | tf_op jit(solution)/shard_map/ppermute | solution.py:96
Sparse Core Ops, SparseCore 0:
  11.9 93.3 all-gather.3
  121.8 44.1 reduce-scatter.4
  168.6 52.0 reduce-scatter.2

commit v9 on v8

--- a/solution.py
+++ b/solution.py
@@ -205,7 +205,9 @@
     grad_in_part = jnp.einsum(
         "tzxr,tc->zxrc", tokens_zx, grad_qkv, preferred_element_type=jnp.float32
     ).astype(jnp.bfloat16)
-    token_src, grad_in_part = lax.optimization_barrier((late_gathered, grad_in_part))
+    token_src, out_over_z, grad_in_part = lax.optimization_barrier(
+        (late_gathered, out_over_z, grad_in_part)
+    )
     in_over_z = lax.psum_scatter(grad_in_part, "dz", scatter_dimension=0, tiled=True)[0]
     grad_wide = jnp.pad(grad_qkv, ((0, 0), (0, gathered.shape[2] - in_width)))
     proj_by_mp = token_src.reshape((mp_peers, -1) + gathered.shape[1:])
@@ -213,12 +215,8 @@
         "tc,mjrc->tmjr", grad_wide, proj_by_mp, preferred_element_type=jnp.float32
     )
     grad_tokens = scatter_cols_mp(token_terms, CORES)
-    out_over_z = out_over_z.reshape(x_peers, -1, in_width)
-    both = jnp.concatenate([in_over_z, out_over_z], axis=1)
-    over_x = scatter_rows_x(both)
-    in_rows = w_query.shape[0]
-    grad_in = over_x[:in_rows]
-    grad_w_out = over_x[in_rows:].reshape(w_out.shape)
+    grad_w_out = scatter_rows_x(out_over_z)
+    grad_in = scatter_rows_x(in_over_z)
     grad_scale = 1.0 / math.sqrt(row_count * dp_peers)
     grad_in = grad_in * grad_scale
     return (

time: 248 us -> 248 us (level); the launches traced: 247 us -> 244 us
  waiting for transfers between devices: 145 us -> 137 us
  starting transfers between devices: 15.3 us -> 19.7 us
    reduce_scatter x1, waiting for transfers between devices: 40.6 us -> 33.2 us  [shards(): lax.psum_scatter(grad_in_part, 'dz', scatter_dimension=0, tiled=True)[0]]
    ppermute x3 -> x6, starting transfers between devices: 4.72 us -> 9.73 us  [scatter_rows_x(): total = total + lax.ppermute(piece, 'dx', pairs).astype(jnp.float32)]
    reduce_scatter x1, waiting for transfers between devices: 0.01 us -> 4.71 us  [shards(): lax.psum_scatter(grad_out_part, 'dz', scatter_dimension=0, tiled=True)[0]]
    ppermute x3 -> x6, waiting for transfers between devices: 7.22 us -> 2.79 us  [scatter_rows_x(): total = total + lax.ppermute(piece, 'dx', pairs).astype(jnp.float32)]
    unnamed x28 -> x30, local copies, waits for them, and re-layouts: 4.8 us -> 5.75 us
  transfers between devices with their start and end apart: 12 -> 15, of which waited for: 8 -> 7; matrix products, arithmetic and copies ran while one was open for 22% -> 22% of each run, Pallas kernels for 0% -> 0%
where the time goes in v9:
time: 248 us; the launch traced here: 244 us
  waiting for transfers between devices  137 us (55%)
  local copies, waits for them, and re-layouts  38.8 us (16%)
  matrix products  24.3 us (10%)
  starting transfers between devices  19.7 us (8%)
  between operations  14.2 us (6%)
  other arithmetic  10.2 us (4%)
    all_gather x1, waiting for transfers between devices, shards(): gathered = lax.all_gather(packed, DP_AXES, axis=0, tiled=False)  90.8 us
    reduce_scatter x1, waiting for transfers between devices, shards(): lax.psum_scatter(grad_in_part, 'dz', scatter_dimension=0, tiled=True)[0]  33.2 us
    ppermute x6, starting transfers between devices, scatter_rows_x(): total = total + lax.ppermute(piece, 'dx', pairs).astype(jnp.float32)  9.73 us
    reshape x1, local copies, waits for them, and re-layouts, shards(): full_out = late_gathered[:, :, in_width:].reshape((-1,) + w_out.shape[1:])  7.04 us
    unnamed x30, local copies, waits for them, and re-layouts  5.75 us
    ppermute x2, waiting for transfers between devices, passed_along(): return lax.ppermute(array, axis, pairs)  5.5 us
    ppermute x2, starting transfers between devices, passed_along(): return lax.ppermute(array, axis, pairs)  5.43 us
    dot_general x1, matrix products, shards(): jnp.einsum('tc,mjrc->tmjr', grad_wide, proj_by_mp, preferred_element_type...  5.17 us
  transfers between devices with their start and end apart: 15, of which 7 were waited for; matrix products, arithmetic and copies ran while one was open for 22% of the time, Pallas kernels for 0%

profile of v9, /device:TPU:2, one launch (start us, length us, event | category | flops | bytes accessed | tf_op | source)
XLA Modules:
  0.0 244.3 jit_solution(3898025305565943967)
XLA Ops:
  7.2 0.9 copy.84
  8.2 0.8 copy.85
  9.0 1.1 reshape.316
  10.1 1.7 concatenate.30
  11.8 2.3 reshape.317
  14.5 90.8 %all-gather.4.cloned.1.call-done = bf16[32,90,1152]{2,1,0:T(8,128)(2,1)} async-done(((bf16[1,90,1152]{2,1,0:T(8,128)(2,1)}), bf16[32,90,1152]{2,1,0:T(8,128)(2,1)}) %all-gather.4.cloned.1.call-update) | async-done | bytes 6635536 | tf_op jit(solution)/shard_map/all_gather | solution.py:120
  105.3 3.3 %fusion.15 = bf16[256,640]{0,1:T(8,128)(2,1)S(1)} fusion(bf16[256,32,90]{0,2,1:T(8,128)(2,1)S(1)} %reshape.317, bf16[32,90,1152]{2,1,0:T(8,128)(2,1)} %all-gather.4.cloned.1.call-done), kind=kOutput, calls=%fused_computation.22 | convolution fusion | flops 943882240 | bytes 5734400 | tf_op jit(solution)/shard_map/tdr,drc->tc/dot_general | solution.py:125
  108.7 2.9 %collective-permute-start = (bf16[128,128]{0,1:T(8,128)(2,1)S(1)}, bf16[128,128]{0,1:T(8,128)(2,1)S(1)}, u32[]{:S(2)}, u32[]{:S(2)}) collective-permute-start(bf16[128,128]{0,1:T(8,128)(2,1)S(1)} %slice.155), channel_id=1, source_target_pairs={{0,8},{8,16},{16,24},{24,32},{32,40},{40,48},{48,56},{56,64},{64,7... | collective-permute-start | bytes 98312 | tf_op jit(solution)/shard_map/ppermute | solution.py:22
  111.8 4.8 %collective-permute-done = bf16[128,128]{0,1:T(8,128)(2,1)S(1)} collective-permute-done((bf16[128,128]{0,1:T(8,128)(2,1)S(1)}, bf16[128,128]{0,1:T(8,128)(2,1)S(1)}, u32[]{:S(2)}, u32[]{:S(2)}) %collective-permute-start) | collective-permute-done | bytes 32800 | tf_op jit(solution)/shard_map/ppermute | solution.py:22
  117.2 1.3 copy-done.1
  119.0 2.0 fusion.18
  121.5 2.7 %convolution_convert_fusion = bf16[8,4,16,2880]{3,2,1,0:T(8,128)(2,1)} fusion(bf16[256,2880]{0,1:T(8,128)(2,1)S(1)} %copy-done, bf16[256,4,8,16]{0,3,2,1:T(8,128)(2,1)S(1)} %reshape_reshape.2), kind=kOutput, calls=%fused_computation | convolution fusion | flops 756449280 | bytes 4685824 | tf_op jit(solution)/shard_map/tzxi,tc->zxic/dot_general | solution.py:162
  124.3 2.3 reshape.326
  126.6 3.9 %slice.132 = bf16[32,90,512]{2,1,0:T(8,128)(2,1)} slice(bf16[32,90,1152]{2,1,0:T(8,128)(2,1)} %all-gather.4.cloned.1.call-done), slice={[0:32], [0:90], [640:1152]} | slice | bytes 5898240 | tf_op jit(solution)/shard_map/slice | solution.py:167
  130.5 7.0 %reshape.322 = bf16[512,2880]{1,0:T(8,128)(2,1)} reshape(bf16[32,90,512]{2,1,0:T(8,128)(2,1)} %slice.132) | data formatting | bytes 5898240 | tf_op jit(solution)/shard_map/reshape | solution.py:167
  137.5 3.5 %fusion.20 = bf16[256,512]{0,1:T(8,128)(2,1)} fusion(bf16[512,2880]{1,0:T(8,128)(2,1)} %reshape.322, bf16[256,2880]{0,1:T(8,128)(2,1)S(1)} %copy-done), kind=kOutput, calls=%fused_computation.25 | convolution fusion | flops 755105792 | bytes 4685824 | tf_op jit(solution)/shard_map/dot_general | solution.py:32
  141.1 2.0 reshape.327
  143.1 1.7 reshape.323
  144.8 2.3 convolution_bitcast_fusion
  149.9 2.5 %collective-permute-start.1 = (bf16[128,128]{0,1:T(8,128)(2,1)}, bf16[128,128]{0,1:T(8,128)(2,1)}, u32[]{:S(2)}, u32[]{:S(2)}) collective-permute-start(bf16[128,128]{0,1:T(8,128)(2,1)} %pad_maximum_fusion.3), channel_id=1, source_target_pairs={{8,0},{16,8},{24,16},{32,24},{40,32},{48,40},{56,48},{64,56},{72,6... | collective-permute-start | bytes 98312 | tf_op jit(solution)/shard_map/ppermute | solution.py:22
  152.7 1.1 copy.123
  153.8 2.1 reshape.342
  155.9 0.7 collective-permute-done.1
  156.6 0.8 convert_element_type.164
  157.4 0.8 fusion.55
  158.1 0.7 pad_maximum_fusion.5
  159.1 1.0 pad_maximum_fusion
  160.2 3.4 %convert_bitcast_fusion = bf16[8,4,90,640]{3,2,1,0:T(8,128)(2,1)} fusion(bf16[256,640]{1,0:T(8,128)(2,1)S(1)} %pad_maximum_fusion, bf16[256,4,8,90]{0,3,2,1:T(8,128)(2,1)S(1)} %reshape.326), kind=kOutput, calls=%fused_computation.3 | convolution fusion | flops 945561600 | bytes 5488640 | tf_op jit(solution)/shard_map/tzxr,tc->zxrc/dot_general | solution.py:205
  163.5 4.7 %reduce-scatter.3.cloned.1.call-done = bf16[1,4,16,2880]{3,2,1,0:T(8,128)(2,1)} async-done(((bf16[8,4,16,2880]{3,2,1,0:T(8,128)(2,1)}), bf16[1,4,16,2880]{3,2,1,0:T(8,128)(2,1)}) %reduce-scatter.3.cloned.1.call-update) | async-done | bytes 368656 | tf_op jit(solution)/shard_map/reduce_scatter | solution.py:166
  168.3 5.2 %fusion.23 = f32[256,4,2,4,90]{0,4,3,2,1:T(8,128)S(1)} fusion(bf16[4,2,4,90,1152]{4,3,2,1,0:T(8,128)(2,1)} %bitcast.193, bf16[256,640]{1,0:T(8,128)(2,1)S(1)} %pad_maximum_fusion), kind=kOutput, calls=%fused_computation.30 | convolution fusion | flops 1698693120 | bytes 9912320 | tf_op jit(solution)/shard_map/tc,mjrc->tmjr/dot_general | solution.py:214
  174.2 0.9 copy-done.7
  175.8 2.6 %collective-permute-start.10 = (bf16[16,2880]{1,0:T(8,128)(2,1)S(1)}, bf16[16,2880]{1,0:T(8,128)(2,1)S(1)}, u32[]{:S(2)}, u32[]{:S(2)}) collective-permute-start(bf16[16,2880]{1,0:T(8,128)(2,1)S(1)} %get-tuple-element.43), channel_id=1, source_target_pairs={{0,128},{64,192},{128,0},{192,64},{1,129},{65,193},{129,1},{193,65... | collective-permute-start | bytes 276488 | tf_op jit(solution)/shard_map/ppermute | solution.py:96
  178.4 1.7 collective-permute-start.9
  180.2 1.6 constant_dynamic-slice_fusion
  181.8 2.3 bitcast_add_fusion
  184.0 0.9 fusion.46
  185.0 2.7 %collective-permute-start.5 = (bf16[256,4,90]{0,1,2:T(4,128)(2,1)}, bf16[256,4,90]{0,1,2:T(4,128)(2,1)}, u32[]{:S(2)}, u32[]{:S(2)}) collective-permute-start(bf16[256,4,90]{0,1,2:T(4,128)(2,1)} %get-tuple-element.36), channel_id=1, source_target_pairs={{0,6},{1,7},{2,0},{3,1},{4,2},{5,3},{6,4},{7,5},{8,14},{9,15},{10,... | collective-permute-start | bytes 552968 | tf_op jit(solution)/shard_map/ppermute | solution.py:83
  187.7 0.9 collective-permute-start.4
  188.5 0.8 collective-permute-start.3
  189.4 0.7 fusion.45
  190.1 33.2 %reduce-scatter.5.cloned.1.call-done = bf16[1,4,90,640]{3,2,1,0:T(8,128)(2,1)} async-done(((bf16[8,4,90,640]{3,2,1,0:T(8,128)(2,1)}), bf16[1,4,90,640]{3,2,1,0:T(8,128)(2,1)}) %reduce-scatter.5.cloned.1.call-update) | async-done | bytes 460816 | tf_op jit(solution)/shard_map/reduce_scatter | solution.py:211
  223.3 1.7 dynamic-slice_bitcast_fusion.2
  225.5 2.4 collective-permute-start.7
  227.9 1.8 collective-permute-start.6
  229.7 1.3 fusion.29
  231.0 0.7 convert_element_type.180
  231.7 2.1 collective-permute-done.7
  234.5 1.1 fusion.38
  (88 shorter events, 10.3 us)
Async XLA Ops:
  7.2 114.3 %copy-start = (bf16[256,2880]{0,1:T(8,128)(2,1)S(1)}, bf16[256,2880]{0,1:T(8,128)(2,1)}, u32[]{:S(2)}) copy-start(bf16[256,2880]{0,1:T(8,128)(2,1)} %param.13) | copy-start | bytes 4423684
  7.2 98.1 %all-gather.4.cloned.1.call-start = ((), (), s32[]{:S(2)}) async-start(), calls=%async_computation.4 | async-start | bytes 7299072 | tf_op jit(solution)/shard_map/all_gather | solution.py:120
  11.7 156.5 %reduce-scatter.3.cloned.1.call-start = ((), (), s32[]{:S(2)}) async-start(), calls=%async_computation.2 | async-start | bytes 3391488 | tf_op jit(solution)/shard_map/reduce_scatter | solution.py:166
  108.7 7.9 %collective-permute-start = (bf16[128,128]{0,1:T(8,128)(2,1)S(1)}, bf16[128,128]{0,1:T(8,128)(2,1)S(1)}, u32[]{:S(2)}, u32[]{:S(2)}) collective-permute-start(bf16[128,128]{0,1:T(8,128)(2,1)S(1)} %slice.155), channel_id=1, source_target_pairs={{0,8},{8,16},{16,24},{24,32},{32,40},{40,48},{48,56},{56,64},{64,7... | collective-permute-start | bytes 98312 | tf_op jit(solution)/shard_map/ppermute | solution.py:22
  111.6 5.5 %copy-start.12 = (f32[8]{0:T(128)S(1)}, f32[8]{0:T(128)}, u32[]{:S(2)}) copy-start(f32[8]{0:T(128)} %param.12) | copy-start | bytes 100
  111.7 7.1 %copy-start.3 = (bf16[2,128,8,64]{1,0,3,2:T(2,128)(2,1)}, bf16[2,128,8,64]{1,0,3,2:T(2,128)(2,1)S(1)}, u32[]{:S(2)}) copy-start(bf16[2,128,8,64]{1,0,3,2:T(2,128)(2,1)S(1)} %reshape.319) | copy-start | bytes 786436
  116.6 2.2 copy-start.10
  117.1 1.4 copy-start.1
  124.2 99.0 %reduce-scatter.5.cloned.1.call-start = ((), (), s32[]{:S(2)}) async-start(), calls=%async_computation.3 | async-start | bytes 4423680 | tf_op jit(solution)/shard_map/reduce_scatter | solution.py:211
  144.8 2.3 copy-start.6
  144.8 2.5 %copy-start.2 = (f32[2,1,8,128,256]{3,4,2,0,1:T(8,128)S(1)}, f32[2,1,8,128,256]{3,4,2,0,1:T(8,128)}, u32[]{:S(2)}) copy-start(f32[2,1,8,128,256]{3,4,2,0,1:T(8,128)} %copy-done.1) | copy-start | bytes 6291460
  144.8 2.5 %copy-start.5 = (bf16[2,128,8,64]{1,0,3,2:T(2,128)(2,1)S(1)}, bf16[2,128,8,64]{1,0,3,2:T(2,128)(2,1)}, u32[]{:S(2)}) copy-start(bf16[2,128,8,64]{1,0,3,2:T(2,128)(2,1)} %reshape.323) | copy-start | bytes 786436
  147.2 1.0 copy-start.4
  147.4 5.1 %copy-start.11 = (bf16[2,128,1,64]{1,3,0,2:T(8,128)(2,1)S(1)}, bf16[2,128,1,64]{1,3,0,2:T(8,128)(2,1)}, u32[]{:S(2)}) copy-start(bf16[2,128,1,64]{1,3,0,2:T(8,128)(2,1)} %copy-done.10) | copy-start | bytes 98308
  148.6 1.3 copy-start.8
  149.9 6.7 %collective-permute-start.1 = (bf16[128,128]{0,1:T(8,128)(2,1)}, bf16[128,128]{0,1:T(8,128)(2,1)}, u32[]{:S(2)}, u32[]{:S(2)}) collective-permute-start(bf16[128,128]{0,1:T(8,128)(2,1)} %pad_maximum_fusion.3), channel_id=1, source_target_pairs={{8,0},{16,8},{24,16},{32,24},{40,32},{48,40},{56,48},{64,56},{72,6... | collective-permute-start | bytes 98312 | tf_op jit(solution)/shard_map/ppermute | solution.py:22
  173.5 1.6 copy-start.7
  173.5 1.6 copy-start.9
  175.1 6.6 %collective-permute-start.2 = (bf16[256,4,4,90]{0,2,3,1:T(4,128)(2,1)S(1)}, bf16[256,4,4,90]{0,2,3,1:T(4,128)(2,1)}, u32[]{:S(2)}, u32[]{:S(2)}) collective-permute-start(bf16[256,4,4,90]{0,2,3,1:T(4,128)(2,1)S(1)} %copy.108), channel_id=1, source_target_pairs={{0,1},{1,0},{2,3},{3,2},{4,5},{5,4},{6,7},{7,6},{8,9},{9,8},{10,11... | collective-permute-start | bytes 2211848 | tf_op jit(solution)/shard_map/ppermute | solution.py:76
  175.2 13.4 %collective-permute-start.11 = (bf16[16,2880]{1,0:T(8,128)(2,1)S(1)}, bf16[16,2880]{1,0:T(8,128)(2,1)S(1)}, u32[]{:S(2)}, u32[]{:S(2)}) collective-permute-start(bf16[16,2880]{1,0:T(8,128)(2,1)S(1)} %get-tuple-element.42), channel_id=1, source_target_pairs={{0,192},{64,0},{128,64},{192,128},{1,193},{65,1},{129,65},{193,129... | collective-permute-start | bytes 276488 | tf_op jit(solution)/shard_map/ppermute | solution.py:96
  175.8 13.5 %collective-permute-start.10 = (bf16[16,2880]{1,0:T(8,128)(2,1)S(1)}, bf16[16,2880]{1,0:T(8,128)(2,1)S(1)}, u32[]{:S(2)}, u32[]{:S(2)}) collective-permute-start(bf16[16,2880]{1,0:T(8,128)(2,1)S(1)} %get-tuple-element.43), channel_id=1, source_target_pairs={{0,128},{64,192},{128,0},{192,64},{1,129},{65,193},{129,1},{193,65... | collective-permute-start | bytes 276488 | tf_op jit(solution)/shard_map/ppermute | solution.py:96
  178.4 10.9 %collective-permute-start.9 = (bf16[16,2880]{1,0:T(8,128)(2,1)S(1)}, bf16[16,2880]{1,0:T(8,128)(2,1)S(1)}, u32[]{:S(2)}, u32[]{:S(2)}) collective-permute-start(bf16[16,2880]{1,0:T(8,128)(2,1)S(1)} %get-tuple-element.41), channel_id=1, source_target_pairs={{0,64},{64,128},{128,192},{192,0},{1,65},{65,129},{129,193},{193,1... | collective-permute-start | bytes 276488 | tf_op jit(solution)/shard_map/ppermute | solution.py:96
  185.0 42.9 %collective-permute-start.5 = (bf16[256,4,90]{0,1,2:T(4,128)(2,1)}, bf16[256,4,90]{0,1,2:T(4,128)(2,1)}, u32[]{:S(2)}, u32[]{:S(2)}) collective-permute-start(bf16[256,4,90]{0,1,2:T(4,128)(2,1)} %get-tuple-element.36), channel_id=1, source_target_pairs={{0,6},{1,7},{2,0},{3,1},{4,2},{5,3},{6,4},{7,5},{8,14},{9,15},{10,... | collective-permute-start | bytes 552968 | tf_op jit(solution)/shard_map/ppermute | solution.py:83
  187.7 42.0 %collective-permute-start.4 = (bf16[256,4,90]{0,1,2:T(4,128)(2,1)}, bf16[256,4,90]{0,1,2:T(4,128)(2,1)}, u32[]{:S(2)}, u32[]{:S(2)}) collective-permute-start(bf16[256,4,90]{0,1,2:T(4,128)(2,1)} %get-tuple-element.37), channel_id=1, source_target_pairs={{0,4},{1,5},{2,6},{3,7},{4,0},{5,1},{6,2},{7,3},{8,12},{9,13},{10,... | collective-permute-start | bytes 552968 | tf_op jit(solution)/shard_map/ppermute | solution.py:83
  188.5 41.1 %collective-permute-start.3 = (bf16[256,4,90]{0,1,2:T(4,128)(2,1)S(1)}, bf16[256,4,90]{0,1,2:T(4,128)(2,1)}, u32[]{:S(2)}, u32[]{:S(2)}) collective-permute-start(bf16[256,4,90]{0,1,2:T(4,128)(2,1)S(1)} %get-tuple-element.35), channel_id=1, source_target_pairs={{0,2},{1,3},{2,4},{3,5},{4,6},{5,7},{6,0},{7,1},{8,10},{9,11},{10,... | collective-permute-start | bytes 552968 | tf_op jit(solution)/shard_map/ppermute | solution.py:83
  225.0 6.7 %collective-permute-start.8 = (bf16[90,640]{1,0:T(8,128)(2,1)}, bf16[90,640]{1,0:T(8,128)(2,1)S(1)}, u32[]{:S(2)}, u32[]{:S(2)}) collective-permute-start(bf16[90,640]{1,0:T(8,128)(2,1)} %get-tuple-element.39), channel_id=1, source_target_pairs={{0,192},{64,0},{128,64},{192,128},{1,193},{65,1},{129,65},{193,129... | collective-permute-start | bytes 345608 | tf_op jit(solution)/shard_map/ppermute | solution.py:96
  225.5 8.3 %collective-permute-start.7 = (bf16[90,640]{1,0:T(8,128)(2,1)S(1)}, bf16[90,640]{1,0:T(8,128)(2,1)}, u32[]{:S(2)}, u32[]{:S(2)}) collective-permute-start(bf16[90,640]{1,0:T(8,128)(2,1)S(1)} %get-tuple-element.40), channel_id=1, source_target_pairs={{0,128},{64,192},{128,0},{192,64},{1,129},{65,193},{129,1},{193,65... | collective-permute-start | bytes 345608 | tf_op jit(solution)/shard_map/ppermute | solution.py:96
  227.9 6.6 %collective-permute-start.6 = (bf16[90,640]{1,0:T(8,128)(2,1)S(1)}, bf16[90,640]{1,0:T(8,128)(2,1)}, u32[]{:S(2)}, u32[]{:S(2)}) collective-permute-start(bf16[90,640]{1,0:T(8,128)(2,1)S(1)} %get-tuple-element.38), channel_id=1, source_target_pairs={{0,64},{64,128},{128,192},{192,0},{1,65},{65,129},{129,193},{193,1... | collective-permute-start | bytes 345608 | tf_op jit(solution)/shard_map/ppermute | solution.py:96
Sparse Core Ops, SparseCore 0:
  11.9 93.3 all-gather.3
  124.4 43.8 reduce-scatter.2
  170.8 52.3 reduce-scatter.4

commit v10 on v9

--- a/solution.py
+++ b/solution.py
@@ -216,7 +216,9 @@
     )
     grad_tokens = scatter_cols_mp(token_terms, CORES)
     grad_w_out = scatter_rows_x(out_over_z)
-    grad_in = scatter_rows_x(in_over_z)
+    grad_in = jnp.sum(
+        lax.all_to_all(in_over_z, "dx", 0, 0, tiled=True).astype(jnp.float32), axis=0
+    )
     grad_scale = 1.0 / math.sqrt(row_count * dp_peers)
     grad_in = grad_in * grad_scale
     return (

time: 248 us -> 247 us (level); the launches traced: 244 us -> 246 us
    ppermute x6 -> x3, starting transfers between devices: 9.73 us -> 4.86 us  [scatter_rows_x(): total = total + lax.ppermute(piece, 'dx', pairs).astype(jnp.float32)]
    all_to_all x0 -> x1, starting transfers between devices: none -> 4.79 us  [shards(): lax.all_to_all(in_over_z, 'dx', 0, 0, tiled=True).astype(jnp.float32)]
    ppermute x4, waiting for transfers between devices: 0.01 us -> 3.95 us  [scatter_cols_mp(): got = lax.ppermute(piece.astype(jnp.bfloat16), 'mp', pairs)]
    ppermute x6 -> x3, waiting for transfers between devices: 2.79 us -> 0.01 us  [scatter_rows_x(): total = total + lax.ppermute(piece, 'dx', pairs).astype(jnp.float32)]
  transfers between devices with their start and end apart: 15 -> 13, of which waited for: 7 -> 6; matrix products, arithmetic and copies ran while one was open for 22% -> 22% of each run, Pallas kernels for 0% -> 0%
where the time goes in v10:
time: 247 us; the launch traced here: 246 us
  waiting for transfers between devices  139 us (56%)
  local copies, waits for them, and re-layouts  38.1 us (15%)
  matrix products  24.3 us (10%)
  starting transfers between devices  20.3 us (8%)
  between operations  14.2 us (6%)
  other arithmetic  10.2 us (4%)
    all_gather x1, waiting for transfers between devices, shards(): gathered = lax.all_gather(packed, DP_AXES, axis=0, tiled=False)  90.8 us
    reduce_scatter x1, waiting for transfers between devices, shards(): lax.psum_scatter(grad_in_part, 'dz', scatter_dimension=0, tiled=True)[0]  33.6 us
    reshape x1, local copies, waits for them, and re-layouts, shards(): full_out = late_gathered[:, :, in_width:].reshape((-1,) + w_out.shape[1:])  7.03 us
    unnamed x30, local copies, waits for them, and re-layouts  5.7 us
    ppermute x2, starting transfers between devices, passed_along(): return lax.ppermute(array, axis, pairs)  5.41 us
    ppermute x2, waiting for transfers between devices, passed_along(): return lax.ppermute(array, axis, pairs)  5.4 us
    dot_general x1, matrix products, shards(): jnp.einsum('tc,mjrc->tmjr', grad_wide, proj_by_mp, preferred_element_type...  5.18 us
    ppermute x4, starting transfers between devices, scatter_cols_mp(): got = lax.ppermute(piece.astype(jnp.bfloat16), 'mp', pairs)  5.14 us
  transfers between devices with their start and end apart: 13, of which 6 were waited for; matrix products, arithmetic and copies ran while one was open for 22% of the time, Pallas kernels for 0%

profile of v10, /device:TPU:2, one launch (start us, length us, event | category | flops | bytes accessed | tf_op | source)
XLA Modules:
  0.0 245.8 jit_solution(1969681536173681439)
XLA Ops:
  7.2 0.9 copy.82
  8.2 0.8 copy.83
  9.0 1.1 reshape.306
  10.1 1.7 concatenate.30
  11.8 2.3 reshape.307
  14.5 90.8 %all-gather.4.cloned.1.call-done = bf16[32,90,1152]{2,1,0:T(8,128)(2,1)} async-done(((bf16[1,90,1152]{2,1,0:T(8,128)(2,1)}), bf16[32,90,1152]{2,1,0:T(8,128)(2,1)}) %all-gather.4.cloned.1.call-update) | async-done | bytes 6635536 | tf_op jit(solution)/shard_map/all_gather | solution.py:120
  105.3 3.3 %fusion.15 = bf16[256,640]{0,1:T(8,128)(2,1)S(1)} fusion(bf16[256,32,90]{0,2,1:T(8,128)(2,1)S(1)} %reshape.307, bf16[32,90,1152]{2,1,0:T(8,128)(2,1)} %all-gather.4.cloned.1.call-done), kind=kOutput, calls=%fused_computation.22 | convolution fusion | flops 943882240 | bytes 5734400 | tf_op jit(solution)/shard_map/tdr,drc->tc/dot_general | solution.py:125
  108.7 2.9 %collective-permute-start = (bf16[128,128]{0,1:T(8,128)(2,1)S(1)}, bf16[128,128]{0,1:T(8,128)(2,1)S(1)}, u32[]{:S(2)}, u32[]{:S(2)}) collective-permute-start(bf16[128,128]{0,1:T(8,128)(2,1)S(1)} %slice.155), channel_id=1, source_target_pairs={{0,8},{8,16},{16,24},{24,32},{32,40},{40,48},{48,56},{56,64},{64,7... | collective-permute-start | bytes 98312 | tf_op jit(solution)/shard_map/ppermute | solution.py:22
  111.8 4.8 %collective-permute-done = bf16[128,128]{0,1:T(8,128)(2,1)S(1)} collective-permute-done((bf16[128,128]{0,1:T(8,128)(2,1)S(1)}, bf16[128,128]{0,1:T(8,128)(2,1)S(1)}, u32[]{:S(2)}, u32[]{:S(2)}) %collective-permute-start) | collective-permute-done | bytes 32800 | tf_op jit(solution)/shard_map/ppermute | solution.py:22
  117.2 1.3 copy-done.1
  119.0 2.0 fusion.18
  121.5 2.7 %convolution_convert_fusion = bf16[8,4,16,2880]{3,2,1,0:T(8,128)(2,1)} fusion(bf16[256,2880]{0,1:T(8,128)(2,1)S(1)} %copy-done, bf16[256,4,8,16]{0,3,2,1:T(8,128)(2,1)S(1)} %reshape_reshape.2), kind=kOutput, calls=%fused_computation | convolution fusion | flops 756449280 | bytes 4685824 | tf_op jit(solution)/shard_map/tzxi,tc->zxic/dot_general | solution.py:162
  124.3 2.3 reshape.316
  126.6 3.9 %slice.132 = bf16[32,90,512]{2,1,0:T(8,128)(2,1)} slice(bf16[32,90,1152]{2,1,0:T(8,128)(2,1)} %all-gather.4.cloned.1.call-done), slice={[0:32], [0:90], [640:1152]} | slice | bytes 5898240 | tf_op jit(solution)/shard_map/slice | solution.py:167
  130.5 7.0 %reshape.312 = bf16[512,2880]{1,0:T(8,128)(2,1)} reshape(bf16[32,90,512]{2,1,0:T(8,128)(2,1)} %slice.132) | data formatting | bytes 5898240 | tf_op jit(solution)/shard_map/reshape | solution.py:167
  137.5 3.5 %fusion.20 = bf16[256,512]{0,1:T(8,128)(2,1)} fusion(bf16[512,2880]{1,0:T(8,128)(2,1)} %reshape.312, bf16[256,2880]{0,1:T(8,128)(2,1)S(1)} %copy-done), kind=kOutput, calls=%fused_computation.25 | convolution fusion | flops 755105792 | bytes 4685824 | tf_op jit(solution)/shard_map/dot_general | solution.py:32
  141.1 2.0 reshape.317
  143.1 1.7 reshape.313
  144.8 2.3 convolution_bitcast_fusion
  149.9 2.5 %collective-permute-start.1 = (bf16[128,128]{0,1:T(8,128)(2,1)}, bf16[128,128]{0,1:T(8,128)(2,1)}, u32[]{:S(2)}, u32[]{:S(2)}) collective-permute-start(bf16[128,128]{0,1:T(8,128)(2,1)} %pad_maximum_fusion.3), channel_id=1, source_target_pairs={{8,0},{16,8},{24,16},{32,24},{40,32},{48,40},{56,48},{64,56},{72,6... | collective-permute-start | bytes 98312 | tf_op jit(solution)/shard_map/ppermute | solution.py:22
  152.7 1.1 copy.121
  153.8 2.1 reshape.331
  156.5 0.8 convert_element_type.152
  157.3 0.8 fusion.52
  158.0 0.7 pad_maximum_fusion.5
  159.0 1.1 pad_maximum_fusion
  160.1 3.4 %convert_bitcast_fusion = bf16[8,4,90,640]{3,2,1,0:T(8,128)(2,1)} fusion(bf16[256,640]{1,0:T(8,128)(2,1)S(1)} %pad_maximum_fusion, bf16[256,4,8,90]{0,3,2,1:T(8,128)(2,1)S(1)} %reshape.316), kind=kOutput, calls=%fused_computation.3 | convolution fusion | flops 945561600 | bytes 5488640 | tf_op jit(solution)/shard_map/tzxr,tc->zxrc/dot_general | solution.py:205
  163.4 5.0 %reduce-scatter.3.cloned.1.call-done = bf16[1,4,16,2880]{3,2,1,0:T(8,128)(2,1)} async-done(((bf16[8,4,16,2880]{3,2,1,0:T(8,128)(2,1)}), bf16[1,4,16,2880]{3,2,1,0:T(8,128)(2,1)}) %reduce-scatter.3.cloned.1.call-update) | async-done | bytes 368656 | tf_op jit(solution)/shard_map/reduce_scatter | solution.py:166
  168.4 5.2 %fusion.23 = f32[256,4,2,4,90]{0,4,3,2,1:T(8,128)S(1)} fusion(bf16[4,2,4,90,1152]{4,3,2,1,0:T(8,128)(2,1)} %bitcast.185, bf16[256,640]{1,0:T(8,128)(2,1)S(1)} %pad_maximum_fusion), kind=kOutput, calls=%fused_computation.31 | convolution fusion | flops 1698693120 | bytes 9912320 | tf_op jit(solution)/shard_map/tc,mjrc->tmjr/dot_general | solution.py:214
  174.3 0.9 copy-done.7
  175.2 0.7 dynamic-slice_bitcast_fusion.2
  176.5 2.5 %collective-permute-start.7 = (bf16[16,2880]{1,0:T(8,128)(2,1)}, bf16[16,2880]{1,0:T(8,128)(2,1)}, u32[]{:S(2)}, u32[]{:S(2)}) collective-permute-start(bf16[16,2880]{1,0:T(8,128)(2,1)} %get-tuple-element.40), channel_id=1, source_target_pairs={{0,128},{64,192},{128,0},{192,64},{1,129},{65,193},{129,1},{193,65... | collective-permute-start | bytes 276488 | tf_op jit(solution)/shard_map/ppermute | solution.py:96
  179.0 1.8 collective-permute-start.6
  180.8 1.8 constant_dynamic-slice_fusion
  182.7 2.3 bitcast_add_fusion
  184.9 0.9 fusion.43
  185.9 2.8 %collective-permute-start.5 = (bf16[256,4,90]{0,1,2:T(4,128)(2,1)}, bf16[256,4,90]{0,1,2:T(4,128)(2,1)}, u32[]{:S(2)}, u32[]{:S(2)}) collective-permute-start(bf16[256,4,90]{0,1,2:T(4,128)(2,1)} %get-tuple-element.36), channel_id=1, source_target_pairs={{0,6},{1,7},{2,0},{3,1},{4,2},{5,3},{6,4},{7,5},{8,14},{9,15},{10,... | collective-permute-start | bytes 552968 | tf_op jit(solution)/shard_map/ppermute | solution.py:83
  188.6 0.9 collective-permute-start.4
  189.5 33.6 %reduce-scatter.5.cloned.1.call-done = bf16[1,4,90,640]{3,2,1,0:T(8,128)(2,1)} async-done(((bf16[8,4,90,640]{3,2,1,0:T(8,128)(2,1)}), bf16[1,4,90,640]{3,2,1,0:T(8,128)(2,1)}) %reduce-scatter.5.cloned.1.call-update) | async-done | bytes 460816 | tf_op jit(solution)/shard_map/reduce_scatter | solution.py:211
  223.1 4.8 %all-to-all-start = ((bf16[4,90,640]{2,1,0:T(8,128)(2,1)}), bf16[4,90,640]{2,1,0:T(8,128)(2,1)S(1)}, u32[]{:S(2)}, u32[]{:S(2)}) async-start(bf16[4,90,640]{2,1,0:T(8,128)(2,1)} %bitcast.187), calls=%async_computation.2 | async-start | bytes 983040 | tf_op jit(solution)/shard_map/all_to_all | solution.py:220
  227.9 1.5 collective-permute-start.3
  229.4 1.8 fusion.42
  231.1 3.9 %collective-permute-done.3 = bf16[256,4,90]{0,1,2:T(4,128)(2,1)S(1)} collective-permute-done((bf16[256,4,90]{0,1,2:T(4,128)(2,1)}, bf16[256,4,90]{0,1,2:T(4,128)(2,1)S(1)}, u32[]{:S(2)}, u32[]{:S(2)}) %collective-permute-start.3) | collective-permute-done | bytes 184352 | tf_op jit(solution)/shard_map/ppermute | solution.py:83
  235.1 1.2 fusion.29
  236.3 0.7 convert_element_type.168
  237.1 0.7 slice.175
  237.9 0.7 copy.108
  238.6 0.7 copy.109
  (84 shorter events, 7.5 us)
Async XLA Ops:
  7.2 114.3 %copy-start = (bf16[256,2880]{0,1:T(8,128)(2,1)S(1)}, bf16[256,2880]{0,1:T(8,128)(2,1)}, u32[]{:S(2)}) copy-start(bf16[256,2880]{0,1:T(8,128)(2,1)} %param.13) | copy-start | bytes 4423684
  7.2 98.1 %all-gather.4.cloned.1.call-start = ((), (), s32[]{:S(2)}) async-start(), calls=%async_computation.5 | async-start | bytes 7299072 | tf_op jit(solution)/shard_map/all_gather | solution.py:120
  11.8 156.6 %reduce-scatter.3.cloned.1.call-start = ((), (), s32[]{:S(2)}) async-start(), calls=%async_computation.3 | async-start | bytes 3391488 | tf_op jit(solution)/shard_map/reduce_scatter | solution.py:166
  108.7 7.9 %collective-permute-start = (bf16[128,128]{0,1:T(8,128)(2,1)S(1)}, bf16[128,128]{0,1:T(8,128)(2,1)S(1)}, u32[]{:S(2)}, u32[]{:S(2)}) collective-permute-start(bf16[128,128]{0,1:T(8,128)(2,1)S(1)} %slice.155), channel_id=1, source_target_pairs={{0,8},{8,16},{16,24},{24,32},{32,40},{40,48},{48,56},{56,64},{64,7... | collective-permute-start | bytes 98312 | tf_op jit(solution)/shard_map/ppermute | solution.py:22
  111.6 5.5 %copy-start.12 = (f32[8]{0:T(128)S(1)}, f32[8]{0:T(128)}, u32[]{:S(2)}) copy-start(f32[8]{0:T(128)} %param.12) | copy-start | bytes 100
  111.7 7.1 %copy-start.3 = (bf16[2,128,8,64]{1,0,3,2:T(2,128)(2,1)}, bf16[2,128,8,64]{1,0,3,2:T(2,128)(2,1)S(1)}, u32[]{:S(2)}) copy-start(bf16[2,128,8,64]{1,0,3,2:T(2,128)(2,1)S(1)} %reshape.309) | copy-start | bytes 786436
  116.6 2.2 copy-start.10
  117.1 1.4 copy-start.1
  124.2 98.9 %reduce-scatter.5.cloned.1.call-start = ((), (), s32[]{:S(2)}) async-start(), calls=%async_computation.4 | async-start | bytes 4423680 | tf_op jit(solution)/shard_map/reduce_scatter | solution.py:211
  144.8 2.3 copy-start.6
  144.8 2.5 %copy-start.2 = (f32[2,1,8,128,256]{3,4,2,0,1:T(8,128)S(1)}, f32[2,1,8,128,256]{3,4,2,0,1:T(8,128)}, u32[]{:S(2)}) copy-start(f32[2,1,8,128,256]{3,4,2,0,1:T(8,128)} %copy-done.1) | copy-start | bytes 6291460
  144.8 2.5 %copy-start.5 = (bf16[2,128,8,64]{1,0,3,2:T(2,128)(2,1)S(1)}, bf16[2,128,8,64]{1,0,3,2:T(2,128)(2,1)}, u32[]{:S(2)}) copy-start(bf16[2,128,8,64]{1,0,3,2:T(2,128)(2,1)} %reshape.313) | copy-start | bytes 786436
  147.1 1.0 copy-start.4
  147.3 5.0 %copy-start.11 = (bf16[2,128,1,64]{1,3,0,2:T(8,128)(2,1)S(1)}, bf16[2,128,1,64]{1,3,0,2:T(8,128)(2,1)}, u32[]{:S(2)}) copy-start(bf16[2,128,1,64]{1,3,0,2:T(8,128)(2,1)} %copy-done.10) | copy-start | bytes 98308
  148.6 1.3 copy-start.8
  149.9 6.6 %collective-permute-start.1 = (bf16[128,128]{0,1:T(8,128)(2,1)}, bf16[128,128]{0,1:T(8,128)(2,1)}, u32[]{:S(2)}, u32[]{:S(2)}) collective-permute-start(bf16[128,128]{0,1:T(8,128)(2,1)} %pad_maximum_fusion.3), channel_id=1, source_target_pairs={{8,0},{16,8},{24,16},{32,24},{40,32},{48,40},{56,48},{64,56},{72,6... | collective-permute-start | bytes 98312 | tf_op jit(solution)/shard_map/ppermute | solution.py:22
  173.6 1.6 copy-start.7
  173.6 1.6 copy-start.9
  175.2 7.4 %collective-permute-start.2 = (bf16[256,4,4,90]{0,2,3,1:T(4,128)(2,1)S(1)}, bf16[256,4,4,90]{0,2,3,1:T(4,128)(2,1)}, u32[]{:S(2)}, u32[]{:S(2)}) collective-permute-start(bf16[256,4,4,90]{0,2,3,1:T(4,128)(2,1)S(1)} %copy.106), channel_id=1, source_target_pairs={{0,1},{1,0},{2,3},{3,2},{4,5},{5,4},{6,7},{7,6},{8,9},{9,8},{10,11... | collective-permute-start | bytes 2211848 | tf_op jit(solution)/shard_map/ppermute | solution.py:76
  175.9 51.9 %collective-permute-start.8 = (bf16[16,2880]{1,0:T(8,128)(2,1)}, bf16[16,2880]{1,0:T(8,128)(2,1)}, u32[]{:S(2)}, u32[]{:S(2)}) collective-permute-start(bf16[16,2880]{1,0:T(8,128)(2,1)} %get-tuple-element.39), channel_id=1, source_target_pairs={{0,192},{64,0},{128,64},{192,128},{1,193},{65,1},{129,65},{193,129... | collective-permute-start | bytes 276488 | tf_op jit(solution)/shard_map/ppermute | solution.py:96
  176.5 52.9 %collective-permute-start.7 = (bf16[16,2880]{1,0:T(8,128)(2,1)}, bf16[16,2880]{1,0:T(8,128)(2,1)}, u32[]{:S(2)}, u32[]{:S(2)}) collective-permute-start(bf16[16,2880]{1,0:T(8,128)(2,1)} %get-tuple-element.40), channel_id=1, source_target_pairs={{0,128},{64,192},{128,0},{192,64},{1,129},{65,193},{129,1},{193,65... | collective-permute-start | bytes 276488 | tf_op jit(solution)/shard_map/ppermute | solution.py:96
  179.0 50.3 %collective-permute-start.6 = (bf16[16,2880]{1,0:T(8,128)(2,1)S(1)}, bf16[16,2880]{1,0:T(8,128)(2,1)}, u32[]{:S(2)}, u32[]{:S(2)}) collective-permute-start(bf16[16,2880]{1,0:T(8,128)(2,1)S(1)} %get-tuple-element.38), channel_id=1, source_target_pairs={{0,64},{64,128},{128,192},{192,0},{1,65},{65,129},{129,193},{193,1... | collective-permute-start | bytes 276488 | tf_op jit(solution)/shard_map/ppermute | solution.py:96
  185.9 45.3 %collective-permute-start.5 = (bf16[256,4,90]{0,1,2:T(4,128)(2,1)}, bf16[256,4,90]{0,1,2:T(4,128)(2,1)}, u32[]{:S(2)}, u32[]{:S(2)}) collective-permute-start(bf16[256,4,90]{0,1,2:T(4,128)(2,1)} %get-tuple-element.36), channel_id=1, source_target_pairs={{0,6},{1,7},{2,0},{3,1},{4,2},{5,3},{6,4},{7,5},{8,14},{9,15},{10,... | collective-permute-start | bytes 552968 | tf_op jit(solution)/shard_map/ppermute | solution.py:83
  188.6 42.5 %collective-permute-start.4 = (bf16[256,4,90]{0,1,2:T(4,128)(2,1)}, bf16[256,4,90]{0,1,2:T(4,128)(2,1)}, u32[]{:S(2)}, u32[]{:S(2)}) collective-permute-start(bf16[256,4,90]{0,1,2:T(4,128)(2,1)} %get-tuple-element.37), channel_id=1, source_target_pairs={{0,4},{1,5},{2,6},{3,7},{4,0},{5,1},{6,2},{7,3},{8,12},{9,13},{10,... | collective-permute-start | bytes 552968 | tf_op jit(solution)/shard_map/ppermute | solution.py:83
  223.1 13.9 %all-to-all-start = ((bf16[4,90,640]{2,1,0:T(8,128)(2,1)}), bf16[4,90,640]{2,1,0:T(8,128)(2,1)S(1)}, u32[]{:S(2)}, u32[]{:S(2)}) async-start(bf16[4,90,640]{2,1,0:T(8,128)(2,1)} %bitcast.187), calls=%async_computation.2 | async-start | bytes 983040 | tf_op jit(solution)/shard_map/all_to_all | solution.py:220
  227.9 7.2 %collective-permute-start.3 = (bf16[256,4,90]{0,1,2:T(4,128)(2,1)}, bf16[256,4,90]{0,1,2:T(4,128)(2,1)S(1)}, u32[]{:S(2)}, u32[]{:S(2)}) collective-permute-start(bf16[256,4,90]{0,1,2:T(4,128)(2,1)} %get-tuple-element.35), channel_id=1, source_target_pairs={{0,2},{1,3},{2,4},{3,5},{4,6},{5,7},{6,0},{7,1},{8,10},{9,11},{10,... | collective-permute-start | bytes 552968 | tf_op jit(solution)/shard_map/ppermute | solution.py:83
Sparse Core Ops, SparseCore 0:
  11.9 93.3 all-gather.3
  124.4 43.9 reduce-scatter.2
  171.0 52.0 reduce-scatter.4

commit v11 on v10

--- a/solution.py
+++ b/solution.py
@@ -215,7 +215,9 @@
         "tc,mjrc->tmjr", grad_wide, proj_by_mp, preferred_element_type=jnp.float32
     )
     grad_tokens = scatter_cols_mp(token_terms, CORES)
-    grad_w_out = scatter_rows_x(out_over_z)
+    grad_w_out = jnp.sum(
+        lax.all_to_all(out_over_z, "dx", 0, 0, tiled=True).astype(jnp.float32), axis=0
+    )
     grad_in = jnp.sum(
         lax.all_to_all(in_over_z, "dx", 0, 0, tiled=True).astype(jnp.float32), axis=0
     )

time: 247 us -> 247 us (level)
    reduce_scatter x1, waiting for transfers between devices: 33.6 us -> 26.7 us  [shards(): lax.psum_scatter(grad_in_part, 'dz', scatter_dimension=0, tiled=True)[0]]
    all_to_all x0 -> x1, waiting for transfers between devices: none -> 5.46 us  [shards(): lax.all_to_all(out_over_z, 'dx', 0, 0, tiled=True).astype(jnp.float32)]
    all_to_all x1, waiting for transfers between devices: 0.01 us -> 4.96 us  [shards(): lax.all_to_all(in_over_z, 'dx', 0, 0, tiled=True).astype(jnp.float32)]
    all_to_all x0 -> x1, starting transfers between devices: none -> 4.95 us  [shards(): lax.all_to_all(out_over_z, 'dx', 0, 0, tiled=True).astype(jnp.float32)]
    ppermute x3 -> x0, starting transfers between devices: 4.86 us -> none  [scatter_rows_x(): total = total + lax.ppermute(piece, 'dx', pairs).astype(jnp.float32)]
    ppermute x4, waiting for transfers between devices: 3.95 us -> 0.01 us  [scatter_cols_mp(): got = lax.ppermute(piece.astype(jnp.bfloat16), 'mp', pairs)]
    unnamed x30 -> x32, local copies, waits for them, and re-layouts: 5.7 us -> 5.99 us
  transfers between devices with their start and end apart: 13 -> 11, of which waited for: 6 -> 7; matrix products, arithmetic and copies ran while one was open for 22% -> 22% of each run, Pallas kernels for 0% -> 0%
where the time goes in v11:
time: 247 us; the launch traced here: 244 us
  waiting for transfers between devices  138 us (56%)
  local copies, waits for them, and re-layouts  38 us (15%)
  matrix products  24.3 us (10%)
  starting transfers between devices  19.8 us (8%)
  between operations  14.2 us (6%)
  other arithmetic  9.85 us (4%)
    all_gather x1, waiting for transfers between devices, shards(): gathered = lax.all_gather(packed, DP_AXES, axis=0, tiled=False)  90.8 us
    reduce_scatter x1, waiting for transfers between devices, shards(): lax.psum_scatter(grad_in_part, 'dz', scatter_dimension=0, tiled=True)[0]  26.7 us
    reshape x1, local copies, waits for them, and re-layouts, shards(): full_out = late_gathered[:, :, in_width:].reshape((-1,) + w_out.shape[1:])  7.04 us
    unnamed x32, local copies, waits for them, and re-layouts  5.99 us
    ppermute x2, waiting for transfers between devices, passed_along(): return lax.ppermute(array, axis, pairs)  5.47 us
    all_to_all x1, waiting for transfers between devices, shards(): lax.all_to_all(out_over_z, 'dx', 0, 0, tiled=True).astype(jnp.float32)  5.46 us
    ppermute x2, starting transfers between devices, passed_along(): return lax.ppermute(array, axis, pairs)  5.43 us
    dot_general x1, matrix products, shards(): jnp.einsum('tc,mjrc->tmjr', grad_wide, proj_by_mp, preferred_element_type...  5.19 us
  transfers between devices with their start and end apart: 11, of which 7 were waited for; matrix products, arithmetic and copies ran while one was open for 22% of the time, Pallas kernels for 0%

profile of v11, /device:TPU:2, one launch (start us, length us, event | category | flops | bytes accessed | tf_op | source)
XLA Modules:
  0.0 244.5 jit_solution(4904700132341262651)
XLA Ops:
  7.2 0.9 copy.82
  8.2 0.8 copy.83
  9.0 1.1 reshape.304
  10.1 1.7 concatenate.30
  11.8 2.3 reshape.305
  14.5 90.8 %all-gather.4.cloned.1.call-done = bf16[32,90,1152]{2,1,0:T(8,128)(2,1)} async-done(((bf16[1,90,1152]{2,1,0:T(8,128)(2,1)}), bf16[32,90,1152]{2,1,0:T(8,128)(2,1)}) %all-gather.4.cloned.1.call-update) | async-done | bytes 6635536 | tf_op jit(solution)/shard_map/all_gather | solution.py:120
  105.3 3.3 %fusion.15 = bf16[256,640]{0,1:T(8,128)(2,1)S(1)} fusion(bf16[256,32,90]{0,2,1:T(8,128)(2,1)S(1)} %reshape.305, bf16[32,90,1152]{2,1,0:T(8,128)(2,1)} %all-gather.4.cloned.1.call-done), kind=kOutput, calls=%fused_computation.22 | convolution fusion | flops 943882240 | bytes 5734400 | tf_op jit(solution)/shard_map/tdr,drc->tc/dot_general | solution.py:125
  108.7 2.9 %collective-permute-start = (bf16[128,128]{0,1:T(8,128)(2,1)S(1)}, bf16[128,128]{0,1:T(8,128)(2,1)S(1)}, u32[]{:S(2)}, u32[]{:S(2)}) collective-permute-start(bf16[128,128]{0,1:T(8,128)(2,1)S(1)} %slice.155), channel_id=1, source_target_pairs={{0,8},{8,16},{16,24},{24,32},{32,40},{40,48},{48,56},{56,64},{64,7... | collective-permute-start | bytes 98312 | tf_op jit(solution)/shard_map/ppermute | solution.py:22
  111.8 4.8 %collective-permute-done = bf16[128,128]{0,1:T(8,128)(2,1)S(1)} collective-permute-done((bf16[128,128]{0,1:T(8,128)(2,1)S(1)}, bf16[128,128]{0,1:T(8,128)(2,1)S(1)}, u32[]{:S(2)}, u32[]{:S(2)}) %collective-permute-start) | collective-permute-done | bytes 32800 | tf_op jit(solution)/shard_map/ppermute | solution.py:22
  117.2 1.3 copy-done.1
  119.0 2.0 fusion.18
  121.5 2.7 %convolution_convert_fusion = bf16[8,4,16,2880]{3,2,1,0:T(8,128)(2,1)} fusion(bf16[256,2880]{0,1:T(8,128)(2,1)S(1)} %copy-done, bf16[256,4,8,16]{0,3,2,1:T(8,128)(2,1)S(1)} %reshape_reshape.2), kind=kOutput, calls=%fused_computation | convolution fusion | flops 756449280 | bytes 4685824 | tf_op jit(solution)/shard_map/tzxi,tc->zxic/dot_general | solution.py:162
  124.3 2.3 reshape.314
  126.6 3.9 %slice.132 = bf16[32,90,512]{2,1,0:T(8,128)(2,1)} slice(bf16[32,90,1152]{2,1,0:T(8,128)(2,1)} %all-gather.4.cloned.1.call-done), slice={[0:32], [0:90], [640:1152]} | slice | bytes 5898240 | tf_op jit(solution)/shard_map/slice | solution.py:167
  130.5 7.0 %reshape.310 = bf16[512,2880]{1,0:T(8,128)(2,1)} reshape(bf16[32,90,512]{2,1,0:T(8,128)(2,1)} %slice.132) | data formatting | bytes 5898240 | tf_op jit(solution)/shard_map/reshape | solution.py:167
  137.5 3.5 %fusion.20 = bf16[256,512]{0,1:T(8,128)(2,1)} fusion(bf16[512,2880]{1,0:T(8,128)(2,1)} %reshape.310, bf16[256,2880]{0,1:T(8,128)(2,1)S(1)} %copy-done), kind=kOutput, calls=%fused_computation.25 | convolution fusion | flops 755105792 | bytes 4685824 | tf_op jit(solution)/shard_map/dot_general | solution.py:32
  141.1 2.0 reshape.315
  143.1 1.7 reshape.311
  144.8 2.3 convolution_bitcast_fusion
  149.9 2.5 %collective-permute-start.1 = (bf16[128,128]{0,1:T(8,128)(2,1)}, bf16[128,128]{0,1:T(8,128)(2,1)}, u32[]{:S(2)}, u32[]{:S(2)}) collective-permute-start(bf16[128,128]{0,1:T(8,128)(2,1)} %pad_maximum_fusion.3), channel_id=1, source_target_pairs={{8,0},{16,8},{24,16},{32,24},{40,32},{48,40},{56,48},{64,56},{72,6... | collective-permute-start | bytes 98312 | tf_op jit(solution)/shard_map/ppermute | solution.py:22
  152.7 1.1 copy.121
  153.8 2.1 reshape.328
  156.6 0.8 convert_element_type.140
  157.3 0.8 fusion.49
  158.1 0.7 pad_maximum_fusion.5
  159.1 1.1 pad_maximum_fusion
  160.1 3.4 %convert_bitcast_fusion = bf16[8,4,90,640]{3,2,1,0:T(8,128)(2,1)} fusion(bf16[256,640]{1,0:T(8,128)(2,1)S(1)} %pad_maximum_fusion, bf16[256,4,8,90]{0,3,2,1:T(8,128)(2,1)S(1)} %reshape.314), kind=kOutput, calls=%fused_computation.3 | convolution fusion | flops 945561600 | bytes 5488640 | tf_op jit(solution)/shard_map/tzxr,tc->zxrc/dot_general | solution.py:205
  163.5 4.9 %reduce-scatter.3.cloned.1.call-done = bf16[1,4,16,2880]{3,2,1,0:T(8,128)(2,1)} async-done(((bf16[8,4,16,2880]{3,2,1,0:T(8,128)(2,1)}), bf16[1,4,16,2880]{3,2,1,0:T(8,128)(2,1)}) %reduce-scatter.3.cloned.1.call-update) | async-done | bytes 368656 | tf_op jit(solution)/shard_map/reduce_scatter | solution.py:166
  168.4 5.2 %fusion.23 = f32[256,4,2,4,90]{0,4,3,2,1:T(8,128)S(1)} fusion(bf16[4,2,4,90,1152]{4,3,2,1,0:T(8,128)(2,1)} %bitcast.176, bf16[256,640]{1,0:T(8,128)(2,1)S(1)} %pad_maximum_fusion), kind=kOutput, calls=%fused_computation.32 | convolution fusion | flops 1698693120 | bytes 9912320 | tf_op jit(solution)/shard_map/tc,mjrc->tmjr/dot_general | solution.py:214
  173.7 1.8 copy.106
  175.6 5.0 %all-to-all-start.1 = ((bf16[4,16,2880]{2,1,0:T(8,128)(2,1)}), bf16[4,16,2880]{2,1,0:T(8,128)(2,1)S(1)}, u32[]{:S(2)}, u32[]{:S(2)}) async-start(bf16[4,16,2880]{2,1,0:T(8,128)(2,1)} %bitcast.48), calls=%async_computation.3 | async-start | bytes 753664 | tf_op jit(solution)/shard_map/all_to_all | solution.py:219
  180.5 1.6 constant_dynamic-slice_fusion
  182.2 5.5 %all-to-all-done.1 = bf16[4,16,2880]{2,1,0:T(8,128)(2,1)S(1)} async-done(((bf16[4,16,2880]{2,1,0:T(8,128)(2,1)}), bf16[4,16,2880]{2,1,0:T(8,128)(2,1)S(1)}, u32[]{:S(2)}, u32[]{:S(2)}) %all-to-all-start.1) | async-done | bytes 368672 | tf_op jit(solution)/shard_map/all_to_all | solution.py:219
  187.7 0.7 convert_reduce_fusion.1
  188.4 2.3 bitcast_add_fusion
  190.7 1.2 copy-done.3
  192.1 2.8 %collective-permute-start.5 = (bf16[256,4,90]{0,1,2:T(4,128)(2,1)S(1)}, bf16[256,4,90]{0,1,2:T(4,128)(2,1)S(1)}, u32[]{:S(2)}, u32[]{:S(2)}) collective-permute-start(bf16[256,4,90]{0,1,2:T(4,128)(2,1)S(1)} %get-tuple-element.36), channel_id=1, source_target_pairs={{0,6},{1,7},{2,0},{3,1},{4,2},{5,3},{6,4},{7,5},{8,14},{9,15},{10,... | collective-permute-start | bytes 552968 | tf_op jit(solution)/shard_map/ppermute | solution.py:83
  194.9 0.7 collective-permute-start.4
  195.6 0.9 collective-permute-start.3
  196.5 26.7 %reduce-scatter.5.cloned.1.call-done = bf16[1,4,90,640]{3,2,1,0:T(8,128)(2,1)} async-done(((bf16[8,4,90,640]{3,2,1,0:T(8,128)(2,1)}), bf16[1,4,90,640]{3,2,1,0:T(8,128)(2,1)}) %reduce-scatter.5.cloned.1.call-update) | async-done | bytes 460816 | tf_op jit(solution)/shard_map/reduce_scatter | solution.py:211
  223.3 4.8 %all-to-all-start = ((bf16[4,90,640]{2,1,0:T(8,128)(2,1)}), bf16[4,90,640]{2,1,0:T(8,128)(2,1)S(1)}, u32[]{:S(2)}, u32[]{:S(2)}) async-start(bf16[4,90,640]{2,1,0:T(8,128)(2,1)} %bitcast.178), calls=%async_computation.2 | async-start | bytes 983040 | tf_op jit(solution)/shard_map/all_to_all | solution.py:222
  228.1 0.7 broadcast_multiply_fusion.1
  228.8 1.2 fusion.29
  230.0 0.7 convert_element_type.156
  230.7 5.0 %all-to-all-done = bf16[4,90,640]{2,1,0:T(8,128)(2,1)S(1)} async-done(((bf16[4,90,640]{2,1,0:T(8,128)(2,1)}), bf16[4,90,640]{2,1,0:T(8,128)(2,1)S(1)}, u32[]{:S(2)}, u32[]{:S(2)}) %all-to-all-start) | async-done | bytes 460832 | tf_op jit(solution)/shard_map/all_to_all | solution.py:222
  235.8 0.7 slice.175
  236.6 0.7 copy.108
  237.3 0.7 copy.109
  (82 shorter events, 6.6 us)
Async XLA Ops:
  7.2 114.3 %copy-start = (bf16[256,2880]{0,1:T(8,128)(2,1)S(1)}, bf16[256,2880]{0,1:T(8,128)(2,1)}, u32[]{:S(2)}) copy-start(bf16[256,2880]{0,1:T(8,128)(2,1)} %param.13) | copy-start | bytes 4423684
  7.2 98.1 %all-gather.4.cloned.1.call-start = ((), (), s32[]{:S(2)}) async-start(), calls=%async_computation.6 | async-start | bytes 7299072 | tf_op jit(solution)/shard_map/all_gather | solution.py:120
  11.7 156.6 %reduce-scatter.3.cloned.1.call-start = ((), (), s32[]{:S(2)}) async-start(), calls=%async_computation.4 | async-start | bytes 3391488 | tf_op jit(solution)/shard_map/reduce_scatter | solution.py:166
  108.7 7.9 %collective-permute-start = (bf16[128,128]{0,1:T(8,128)(2,1)S(1)}, bf16[128,128]{0,1:T(8,128)(2,1)S(1)}, u32[]{:S(2)}, u32[]{:S(2)}) collective-permute-start(bf16[128,128]{0,1:T(8,128)(2,1)S(1)} %slice.155), channel_id=1, source_target_pairs={{0,8},{8,16},{16,24},{24,32},{32,40},{40,48},{48,56},{56,64},{64,7... | collective-permute-start | bytes 98312 | tf_op jit(solution)/shard_map/ppermute | solution.py:22
  111.6 5.5 %copy-start.13 = (f32[8]{0:T(128)S(1)}, f32[8]{0:T(128)}, u32[]{:S(2)}) copy-start(f32[8]{0:T(128)} %param.12) | copy-start | bytes 100
  111.7 7.1 %copy-start.4 = (bf16[2,128,8,64]{1,0,3,2:T(2,128)(2,1)}, bf16[2,128,8,64]{1,0,3,2:T(2,128)(2,1)S(1)}, u32[]{:S(2)}) copy-start(bf16[2,128,8,64]{1,0,3,2:T(2,128)(2,1)S(1)} %reshape.307) | copy-start | bytes 786436
  116.6 2.2 copy-start.11
  117.1 1.4 copy-start.1
  124.2 99.0 %reduce-scatter.5.cloned.1.call-start = ((), (), s32[]{:S(2)}) async-start(), calls=%async_computation.5 | async-start | bytes 4423680 | tf_op jit(solution)/shard_map/reduce_scatter | solution.py:211
  144.8 2.3 copy-start.7
  144.8 2.5 %copy-start.2 = (f32[2,1,8,128,256]{3,4,2,0,1:T(8,128)S(1)}, f32[2,1,8,128,256]{3,4,2,0,1:T(8,128)}, u32[]{:S(2)}) copy-start(f32[2,1,8,128,256]{3,4,2,0,1:T(8,128)} %copy-done.1) | copy-start | bytes 6291460
  144.8 2.5 %copy-start.6 = (bf16[2,128,8,64]{1,0,3,2:T(2,128)(2,1)S(1)}, bf16[2,128,8,64]{1,0,3,2:T(2,128)(2,1)}, u32[]{:S(2)}) copy-start(bf16[2,128,8,64]{1,0,3,2:T(2,128)(2,1)} %reshape.311) | copy-start | bytes 786436
  147.1 1.0 copy-start.5
  147.3 5.1 %copy-start.12 = (bf16[2,128,1,64]{1,3,0,2:T(8,128)(2,1)S(1)}, bf16[2,128,1,64]{1,3,0,2:T(8,128)(2,1)}, u32[]{:S(2)}) copy-start(bf16[2,128,1,64]{1,3,0,2:T(8,128)(2,1)} %copy-done.11) | copy-start | bytes 98308
  148.6 1.3 copy-start.10
  149.9 6.7 %collective-permute-start.1 = (bf16[128,128]{0,1:T(8,128)(2,1)}, bf16[128,128]{0,1:T(8,128)(2,1)}, u32[]{:S(2)}, u32[]{:S(2)}) collective-permute-start(bf16[128,128]{0,1:T(8,128)(2,1)} %pad_maximum_fusion.3), channel_id=1, source_target_pairs={{8,0},{16,8},{24,16},{32,24},{40,32},{48,40},{56,48},{64,56},{72,6... | collective-permute-start | bytes 98312 | tf_op jit(solution)/shard_map/ppermute | solution.py:22
  173.6 2.0 copy-start.8
  175.6 12.8 %collective-permute-start.2 = (bf16[256,4,4,90]{0,2,3,1:T(4,128)(2,1)}, bf16[256,4,4,90]{0,2,3,1:T(4,128)(2,1)}, u32[]{:S(2)}, u32[]{:S(2)}) collective-permute-start(bf16[256,4,4,90]{0,2,3,1:T(4,128)(2,1)} %copy.106), channel_id=1, source_target_pairs={{0,1},{1,0},{2,3},{3,2},{4,5},{5,4},{6,7},{7,6},{8,9},{9,8},{10,11... | collective-permute-start | bytes 2211848 | tf_op jit(solution)/shard_map/ppermute | solution.py:76
  175.6 12.1 %all-to-all-start.1 = ((bf16[4,16,2880]{2,1,0:T(8,128)(2,1)}), bf16[4,16,2880]{2,1,0:T(8,128)(2,1)S(1)}, u32[]{:S(2)}, u32[]{:S(2)}) async-start(bf16[4,16,2880]{2,1,0:T(8,128)(2,1)} %bitcast.48), calls=%async_computation.3 | async-start | bytes 753664 | tf_op jit(solution)/shard_map/all_to_all | solution.py:219
  188.4 39.7 %copy-start.9 = (f32[16,2880]{1,0:T(8,128)S(1)}, f32[16,2880]{1,0:T(8,128)}, u32[]{:S(2)}) copy-start(f32[16,2880]{1,0:T(8,128)} %convert_reduce_fusion.1) | copy-start | bytes 552964
  190.7 1.2 copy-start.3
  192.1 36.7 %collective-permute-start.5 = (bf16[256,4,90]{0,1,2:T(4,128)(2,1)S(1)}, bf16[256,4,90]{0,1,2:T(4,128)(2,1)S(1)}, u32[]{:S(2)}, u32[]{:S(2)}) collective-permute-start(bf16[256,4,90]{0,1,2:T(4,128)(2,1)S(1)} %get-tuple-element.36), channel_id=1, source_target_pairs={{0,6},{1,7},{2,0},{3,1},{4,2},{5,3},{6,4},{7,5},{8,14},{9,15},{10,... | collective-permute-start | bytes 552968 | tf_op jit(solution)/shard_map/ppermute | solution.py:83
  194.9 33.9 %collective-permute-start.4 = (bf16[256,4,90]{0,1,2:T(4,128)(2,1)S(1)}, bf16[256,4,90]{0,1,2:T(4,128)(2,1)S(1)}, u32[]{:S(2)}, u32[]{:S(2)}) collective-permute-start(bf16[256,4,90]{0,1,2:T(4,128)(2,1)S(1)} %get-tuple-element.37), channel_id=1, source_target_pairs={{0,4},{1,5},{2,6},{3,7},{4,0},{5,1},{6,2},{7,3},{8,12},{9,13},{10,... | collective-permute-start | bytes 552968 | tf_op jit(solution)/shard_map/ppermute | solution.py:83
  195.6 33.1 %collective-permute-start.3 = (bf16[256,4,90]{0,1,2:T(4,128)(2,1)S(1)}, bf16[256,4,90]{0,1,2:T(4,128)(2,1)S(1)}, u32[]{:S(2)}, u32[]{:S(2)}) collective-permute-start(bf16[256,4,90]{0,1,2:T(4,128)(2,1)S(1)} %get-tuple-element.35), channel_id=1, source_target_pairs={{0,2},{1,3},{2,4},{3,5},{4,6},{5,7},{6,0},{7,1},{8,10},{9,11},{10,... | collective-permute-start | bytes 552968 | tf_op jit(solution)/shard_map/ppermute | solution.py:83
  223.3 12.4 %all-to-all-start = ((bf16[4,90,640]{2,1,0:T(8,128)(2,1)}), bf16[4,90,640]{2,1,0:T(8,128)(2,1)S(1)}, u32[]{:S(2)}, u32[]{:S(2)}) async-start(bf16[4,90,640]{2,1,0:T(8,128)(2,1)} %bitcast.178), calls=%async_computation.2 | async-start | bytes 983040 | tf_op jit(solution)/shard_map/all_to_all | solution.py:222
Sparse Core Ops, SparseCore 0:
  11.9 93.3 all-gather.3
  124.3 43.9 reduce-scatter.2
  171.0 52.2 reduce-scatter.4
